TPU v7x, 256 devices: a whole 4x4x8 slice. The times are simulated.
256 devices in a mesh: expert: 64 (over z, x, core), cuts: 4 (over y).
Axes of the slice: x: 4, y: 4, z: 8, core: 2. Of those that a mesh axis runs over, the one named last changes fastest.
Arguments:
- queries: bfloat16 [16384, 2048], P(('expert', 'cuts')), as said below
- new_keys: bfloat16 [16384, 2048], P(('expert', 'cuts')), as said below
- new_values: bfloat16 [16384, 2048], P(('expert', 'cuts')), may hold values from -6 to 6
- cache_keys: bfloat16 [131072, 2048], P(('expert', 'cuts')), as said below
- cache_values: bfloat16 [131072, 2048], P(('expert', 'cuts')), may hold values from -6 to 6
- parents: int32 [256, 64], P(('expert', 'cuts')), may hold values from 0 to 62, as said below
- tree_len: int32 [256], P(('expert', 'cuts')), may hold values from 32 to 64
- cache_len: int32 [256], P(('expert', 'cuts')), may hold values from 2 to 512
- accepted_path: int32 [256, 8], P(('expert', 'cuts')), may hold values from 0 to 31, as said below
- residual: bfloat16 [16384, 2048], P(('expert', 'cuts')), as said below
- norm_gain: float32 [2048], replicated, may hold values from 0.25 to 1.75
- out_weight: bfloat16 [2048, 2048], P('cuts'), may hold values from -0.125 to 0.125
- routes: int32 [16384, 4], P('expert'), may hold values from 0 to 63, as said below
- route_weights: float32 [16384, 4], P('expert'), may hold values from 0.05 to 0.6
- w_gate: bfloat16 [64, 2048, 1408], P('expert', None, 'cuts'), may hold values from -0.125 to 0.125
- w_up: bfloat16 [64, 2048, 1408], P('expert', None, 'cuts'), may hold values from -0.125 to 0.125
- w_down: bfloat16 [64, 1408, 2048], P('expert', 'cuts'), may hold values from -0.15625 to 0.15625
Outputs:
- layer_out: bfloat16 [16384, 2048], P(('expert', 'cuts'))
- accepted_kv: bfloat16 [2048, 4096], P(('expert', 'cuts'))
Inputs may be any that keep to these rules, and one draw needn't show every extreme that they name: `parents`: the parent of slot 0 is 0; every other slot's parent is an earlier slot of the same request. `accepted_path`: each row starts at slot 0, each entry is the parent of the next one, and every entry is below the request's tree_len. `routes`: the 4 experts of a slot are distinct. Within each block of 64 consecutive rows (the tree slots of one device), no expert is named more than 8 times, and in every such block some expert is named exactly 8 times. `queries`: entries lie within -110 and 110. `new_keys`: entries lie within -6 and 6. `cache_keys`: entries lie within -4 and 4. `residual`: entries lie within -40 and 40.
All inputs are finite; a program needn't handle non-finite values.
Results may differ from a plain program's by a relative error of at most 0.014.
Values may be sent and summed in bfloat16 or wider, within the bound.
No kernel may reach another device: no remote copies, remote signals or barrier semaphores. Data moves between devices by JAX's collectives and lax.ppermute only.
A program may use at most 128 MiB of HBM per device.

v0:
```python
import math

import jax
import jax.numpy as jnp
from jax import lax
from jax.sharding import PartitionSpec as P

HEADS = 16
HEAD = 128
TOPK = 4
TREE = 64


epsilon = 1e-06


def ancestors(parents):
    slot_ids = jnp.arange(TREE, dtype=jnp.int32)
    linked = (parents[:, None] == slot_ids[None, :]) | (slot_ids[:, None] == slot_ids[None, :])
    reach = linked.astype(jnp.float32)
    for doubling in range(TREE.bit_length()):
        reach = jnp.minimum(jnp.dot(reach, reach, precision=lax.Precision.HIGHEST), 1.0)
    return reach > 0.5


def tree_attention(request):
    queries, new_keys, new_values, cache_keys, cache_values, parents, tree_len, cache_len = request
    cache_rows = cache_keys.shape[0]
    query_heads = queries.reshape(TREE, HEADS, HEAD)
    cache_heads = cache_keys.reshape(cache_rows, HEADS, HEAD)
    fresh_heads = new_keys.reshape(TREE, HEADS, HEAD)
    score_scale = 1.0 / math.sqrt(HEAD)
    cache_scores = (
        jnp.einsum("qhd,khd->hqk", query_heads, cache_heads, preferred_element_type=jnp.float32)
        * score_scale
    )
    fresh_scores = (
        jnp.einsum("qhd,khd->hqk", query_heads, fresh_heads, preferred_element_type=jnp.float32)
        * score_scale
    )
    slot_ids = jnp.arange(TREE, dtype=jnp.int32)
    cache_seen = jnp.arange(cache_rows, dtype=jnp.int32) < cache_len
    fresh_seen = ancestors(parents) & (slot_ids[None, :] < tree_len)
    cache_scores = jnp.where(cache_seen[None, None, :], cache_scores, -jnp.inf)
    fresh_scores = jnp.where(fresh_seen[None, :, :], fresh_scores, -jnp.inf)
    highest = jnp.maximum(jnp.max(cache_scores, axis=2), jnp.max(fresh_scores, axis=2))[:, :, None]
    cache_exp = jnp.exp(cache_scores - highest)
    fresh_exp = jnp.exp(fresh_scores - highest)
    total = jnp.sum(cache_exp, axis=2, keepdims=True) + jnp.sum(fresh_exp, axis=2, keepdims=True)
    cache_weights = (cache_exp / total).astype(jnp.bfloat16)
    fresh_weights = (fresh_exp / total).astype(jnp.bfloat16)
    mixed = jnp.einsum(
        "hqk,khd->qhd",
        cache_weights,
        cache_values.reshape(cache_rows, HEADS, HEAD),
        preferred_element_type=jnp.float32,
    )
    mixed = mixed + jnp.einsum(
        "hqk,khd->qhd",
        fresh_weights,
        new_values.reshape(TREE, HEADS, HEAD),
        preferred_element_type=jnp.float32,
    )
    return mixed.reshape(TREE, HEADS * HEAD).astype(jnp.bfloat16)


def expert_rows(flat_in, gate_w, up_w, down_w):
    gate = jnp.dot(flat_in, gate_w, preferred_element_type=jnp.float32)
    upper = jnp.dot(flat_in, up_w, preferred_element_type=jnp.float32)
    hidden = (jax.nn.silu(gate) * upper).astype(jnp.bfloat16)
    return jnp.dot(hidden, down_w, preferred_element_type=jnp.float32)


def norm_rows(stream, norm_gain):
    power = jnp.mean(stream * stream, axis=1, keepdims=True)
    return (stream * lax.rsqrt(power + epsilon) * norm_gain).astype(jnp.bfloat16)


def on_device(
    queries,
    new_keys,
    new_values,
    cache_keys,
    cache_values,
    parents,
    tree_len,
    cache_len,
    accepted_path,
    residual,
    norm_gain,
    out_weight,
    routes,
    route_weights,
    w_gate,
    w_up,
    w_down,
):
    cut_count = lax.axis_size("cuts")
    place = lax.axis_index("cuts")
    tok_rows = queries.shape[0]
    requests = tok_rows // TREE
    cache_rows = cache_keys.shape[0] // requests
    width = queries.shape[1]
    attended = lax.map(
        tree_attention,
        (
            queries.reshape(requests, TREE, width),
            new_keys.reshape(requests, TREE, width),
            new_values.reshape(requests, TREE, width),
            cache_keys.reshape(requests, cache_rows, width),
            cache_values.reshape(requests, cache_rows, width),
            parents,
            tree_len,
            cache_len,
        ),
    )
    attended = attended.reshape(tok_rows, width)
    head_group = lax.all_to_all(attended, "cuts", split_axis=1, concat_axis=0, tiled=True)
    projected = jnp.dot(head_group, out_weight, preferred_element_type=jnp.float32)
    start = place * tok_rows
    own_part = lax.dynamic_slice_in_dim(projected, start, tok_rows, 0) + residual.astype(
        jnp.float32
    )
    projected = lax.dynamic_update_slice_in_dim(projected, own_part, start, 0)
    experts_all = w_gate.shape[0] * lax.axis_size("expert")
    capacity = 2 * tok_rows * TOPK // experts_all
    group_rows = cut_count * tok_rows
    flat = routes.reshape(cut_count, tok_rows * TOPK)
    onehot = (flat[:, :, None] == jnp.arange(experts_all, dtype=jnp.int32)[None, None, :]).astype(
        jnp.int32
    )
    ahead = jnp.cumsum(onehot, axis=1) - onehot
    slot_of = jnp.sum(ahead * onehot, axis=2)
    gate_w = w_gate[0]
    up_w = w_up[0]
    down_w = w_down[0]
    stream = lax.psum(projected.astype(jnp.bfloat16), "cuts").astype(jnp.float32)
    normed = norm_rows(stream, norm_gain)
    owner = jnp.arange(cut_count, dtype=jnp.int32)[:, None]
    dest = flat * (cut_count * capacity) + owner * capacity + slot_of
    token_of = jnp.arange(group_rows * TOPK, dtype=jnp.int32) // TOPK
    table = (
        jnp.full((experts_all * cut_count * capacity,), -1, jnp.int32)
        .at[dest.reshape(-1)]
        .set(token_of)
    )
    filled = table >= 0
    outgoing = jnp.where(
        filled[:, None], normed[jnp.maximum(table, 0)], jnp.zeros((), jnp.bfloat16)
    )
    outgoing = outgoing.reshape(experts_all, cut_count, capacity, width)
    arrived = lax.all_to_all(outgoing, "expert", split_axis=0, concat_axis=0, tiled=True)
    arrived_shape = arrived.shape
    product = expert_rows(arrived.reshape(-1, width), gate_w, up_w, down_w)
    pieces = product.astype(jnp.bfloat16).reshape(arrived_shape)
    returned = lax.all_to_all(pieces, "expert", split_axis=0, concat_axis=0, tiled=True)
    picked = returned.reshape(-1, width)[dest.reshape(-1)].reshape(group_rows, TOPK, width)
    group_moe = jnp.sum(route_weights.reshape(group_rows, TOPK, 1) * picked, axis=1)
    moe_own = lax.psum_scatter(
        group_moe.astype(jnp.bfloat16), "cuts", scatter_dimension=0, tiled=True
    ).astype(jnp.float32)
    stream_own = lax.dynamic_slice_in_dim(stream, start, tok_rows, 0)
    layer_out = (stream_own + moe_own).astype(jnp.bfloat16)
    picks = (jnp.arange(requests, dtype=jnp.int32)[:, None] * TREE + accepted_path).reshape(-1)
    accepted_kv = jnp.concatenate([new_keys[picks], new_values[picks]], axis=1)
    return (layer_out, accepted_kv)


def solution(mesh):
    placed = (
        P(("expert", "cuts"), None),
        P(("expert", "cuts"), None),
        P(("expert", "cuts"), None),
        P(("expert", "cuts"), None),
        P(("expert", "cuts"), None),
        P(("expert", "cuts"), None),
        P(("expert", "cuts")),
        P(("expert", "cuts")),
        P(("expert", "cuts"), None),
        P(("expert", "cuts"), None),
        P(),
        P("cuts", None),
        P("expert", None),
        P("expert", None),
        P("expert", None, "cuts"),
        P("expert", None, "cuts"),
        P("expert", "cuts", None),
    )
    return jax.shard_map(
        on_device,
        mesh=mesh,
        in_specs=placed,
        out_specs=(P(("expert", "cuts"), None), P(("expert", "cuts"), None)),
        check_vma=False,
    )
```

profile of v0, /device:TPU:1, one launch (start us, length us, event | category | flops | bytes accessed | tf_op | source)
XLA Modules:
  0.0 571.3 jit_solution(3458800312377972334)
XLA Ops:
  8.0 0.9 convolution_minimum_fusion.6
  8.9 0.2 convolution_minimum_fusion.5
  9.1 0.2 convolution_minimum_fusion.4
  9.3 0.2 convolution_minimum_fusion.3
  9.4 0.2 convolution_minimum_fusion.2
  9.6 0.2 convolution_minimum_fusion.1
  10.4 0.2 fusion.24
  10.7 1.9 fusion.7
  12.7 0.3 fusion.58
  13.0 0.6 fusion.8
  13.8 0.3 fusion.34
  14.1 0.5 copy-done.11
  14.6 0.9 fusion.20
  15.5 0.2 copy.53
  15.8 0.7 copy.54
  16.6 5.0 all-to-all-start
  21.6 0.1 copy.57
  22.0 2.4 reduce-window.6
  24.4 0.1 slice.16
  24.5 0.1 copy.59
  24.7 0.2 fusion.33
  24.9 2.2 all-to-all-done
  27.1 2.3 fusion.59
  29.6 1.1 convert_element_type.68
  30.7 0.1 copy.56
  31.1 4.3 scatter_custom_fusion
  35.6 47.0 %all-reduce.2.cloned.1.call-done = bf16[256,2048]{1,0:T(8,128)(2,1)} async-done(((bf16[256,2048]{1,0:T(8,128)(2,1)}), bf16[256,2048]{1,0:T(8,128)(2,1)}) %all-reduce.2.cloned.1.call-update) | async-done | bytes 1048592 | tf_op jit(solution)/shard_map/psum | solution.py:137
  82.6 1.5 multiply_reduce_fusion.1
  84.1 1.5 multiply_convert_fusion
  85.7 11.0 %gather_fusion = bf16[2048,2048]{1,0:T(8,128)(2,1)} fusion(bf16[256,2048]{1,0:T(8,128)(2,1)S(1)} %multiply_convert_fusion, s32[2048]{0:T(1024)S(1)} %maximum_clamp_fusion), kind=kCustom, calls=%fused_computation | custom fusion | bytes 16785408 | tf_op jit(solution)/shard_map/gather | solution.py:149
  96.7 7.3 %broadcast_select_fusion = bf16[64,4,8,2048]{3,2,1,0:T(8,128)(2,1)} fusion(bf16[64,4,8,2048]{3,2,1,0:T(8,128)(2,1)} %bitcast.130, pred[64,4,8]{2,1,0:T(4,128)(4,1)S(1)} %broadcast_in_dim.88), kind=kLoop, calls=%fused_computation.6 | loop fusion | flops 4194304 | bytes 16779264 | tf_op jit(solution)/shard_map/jit(_where)/select_n | solution.py:148
  103.9 197.1 %all_to_all.26 = bf16[64,4,8,2048]{3,2,1,0:T(8,128)(2,1)S(1)} all-to-all(bf16[64,4,8,2048]{3,2,1,0:T(8,128)(2,1)} %broadcast_select_fusion), channel_id=1, replica_groups=mesh['expert'=64,'cuts'=4] {'expert'}, dimensions={0} | all-to-all | bytes 16777216 | tf_op jit(solution)/shard_map/all_to_all | solution.py:152
  301.1 3.2 fusion.11
  304.3 3.5 fusion
  307.8 6.8 %convolution_convert_fusion = bf16[2048,2048]{1,0:T(8,128)(2,1)} fusion(bf16[2048,352]{0,1:T(8,128)(2,1)S(1)} %fusion, bf16[1,352,2048]{2,1,0:T(8,128)(2,1)S(1)} %copy-done.14), kind=kOutput, calls=%fused_computation.7 | convolution fusion | flops 2956984320 | bytes 11272192 | tf_op jit(solution)/shard_map/dot_general | solution.py:71
  314.6 7.3 %all-to-all-start.2 = ((bf16[64,4,8,2048]{3,2,1,0:T(8,128)(2,1)}), bf16[64,4,8,2048]{3,2,1,0:T(8,128)(2,1)}, u32[]{:S(2)}, u32[]{:S(2)}) async-start(bf16[64,4,8,2048]{3,2,1,0:T(8,128)(2,1)} %bitcast.131), calls=%async_computation.2 | async-start | bytes 16777216 | tf_op jit(solution)/shard_map/all_to_all | solution.py:156
  322.0 0.3 reduce-scatter.2.cloned.1.call-start
  322.3 0.1 copy.55
  322.4 182.1 %all-to-all-done.2 = bf16[64,4,8,2048]{3,2,1,0:T(8,128)(2,1)} async-done(((bf16[64,4,8,2048]{3,2,1,0:T(8,128)(2,1)}), bf16[64,4,8,2048]{3,2,1,0:T(8,128)(2,1)}, u32[]{:S(2)}, u32[]{:S(2)}) %all-to-all-start.2) | async-done | bytes 8388640 | tf_op jit(solution)/shard_map/all_to_all | solution.py:156
  504.5 13.3 %gather_fusion.1 = bf16[1024,2048]{1,0:T(8,128)(2,1)} fusion(bf16[2048,2048]{1,0:T(8,128)(2,1)} %bitcast.15, s32[1024]{0:T(1024)S(1)} %broadcast_clamp_fusion), kind=kCustom, calls=%fused_computation.1 | custom fusion | bytes 8392704 | tf_op jit(solution)/shard_map/gather | solution.py:157
  517.8 8.3 %reshape.213 = f32[256,4,2048]{2,1,0:T(4,128)} reshape(bf16[1024,2048]{1,0:T(8,128)(2,1)} %gather_fusion.1) | data formatting | bytes 12582912 | tf_op jit(solution)/shard_map/convert_element_type | solution.py:158
  526.1 11.2 %multiply_reduce_fusion = bf16[256,2048]{1,0:T(8,128)(2,1)} fusion(f32[256,4,2048]{2,1,0:T(4,128)} %reshape.213, f32[256,4]{1,0:T(8,128)S(1)} %copy.55), kind=kLoop, calls=%fused_computation.5 | loop fusion | flops 3670016 | bytes 9441280 | tf_op jit(solution)/shard_map/reduce_sum | solution.py:158
  537.4 0.6 gather_fusion.2
  537.9 0.6 gather_fusion.3
  538.5 0.6 pad_maximum_fusion
  539.2 1.6 convert_element_type.69
  540.8 21.8 %reduce-scatter.2.cloned.1.call-done = bf16[64,2048]{1,0:T(8,128)(2,1)} async-done(((bf16[256,2048]{1,0:T(8,128)(2,1)}), bf16[64,2048]{1,0:T(8,128)(2,1)}) %reduce-scatter.2.cloned.1.call-update) | async-done | bytes 262160 | tf_op jit(solution)/shard_map/reduce_scatter | solution.py:159
  562.6 1.9 add_convert_fusion
  (63 shorter events, 1.2 us)
Async XLA Ops:
  7.2 3.5 copy-start
  10.7 2.0 copy-start.3
  10.7 2.0 copy-start.5
  12.7 1.1 copy-start.6
  13.0 1.6 copy-start.11
  15.5 6.1 %copy-start.8 = (s32[256,4]{0,1:T(4,128)S(1)}, s32[256,4]{0,1:T(4,128)}, u32[]{:S(2)}) copy-start(s32[256,4]{0,1:T(4,128)} %param.29) | copy-start | bytes 12292
  16.6 10.5 %all-to-all-start = ((bf16[64,4,512]{2,0,1:T(8,128)(2,1)}), bf16[64,4,512]{2,0,1:T(8,128)(2,1)S(1)}, u32[]{:S(2)}, u32[]{:S(2)}) async-start(bf16[64,4,512]{2,0,1:T(8,128)(2,1)} %copy.54), calls=%async_computation | async-start | bytes 524288 | tf_op jit(solution)/shard_map/all_to_all | solution.py:118
  21.6 61.0 %all-reduce.2.cloned.1.call-start = ((), (), s32[]{:S(2)}) async-start(), calls=%async_computation.4 | async-start | bytes 2097152 | tf_op jit(solution)/shard_map/psum | solution.py:137
  27.1 2.4 copy-start.4
  29.5 54.6 %copy-start.9 = (f32[2048]{0:T(1024)S(1)}, f32[2048]{0:T(1024)}, u32[]{:S(2)}) copy-start(f32[2048]{0:T(1024)} %param.27) | copy-start | bytes 24580
  103.9 197.1 %copy-start.12 = (bf16[1,2048,352]{1,2,0:T(8,128)(2,1)S(1)}, bf16[1,2048,352]{1,2,0:T(8,128)(2,1)}, u32[]{:S(2)}) copy-start(bf16[1,2048,352]{1,2,0:T(8,128)(2,1)} %param.31) | copy-start | bytes 4325380
  301.1 3.2 copy-start.13
  304.3 3.5 copy-start.14
  314.6 7.6 %copy-start.10 = (f32[256,4]{0,1:T(4,128)S(1)}, f32[256,4]{0,1:T(4,128)}, u32[]{:S(2)}) copy-start(f32[256,4]{0,1:T(4,128)} %param.30) | copy-start | bytes 12292
  314.6 189.9 %all-to-all-start.2 = ((bf16[64,4,8,2048]{3,2,1,0:T(8,128)(2,1)}), bf16[64,4,8,2048]{3,2,1,0:T(8,128)(2,1)}, u32[]{:S(2)}, u32[]{:S(2)}) async-start(bf16[64,4,8,2048]{3,2,1,0:T(8,128)(2,1)} %bitcast.131), calls=%async_computation.2 | async-start | bytes 16777216 | tf_op jit(solution)/shard_map/all_to_all | solution.py:156
  322.0 240.6 %reduce-scatter.2.cloned.1.call-start = ((), (), s32[]{:S(2)}) async-start(), calls=%async_computation.5 | async-start | bytes 1310720 | tf_op jit(solution)/shard_map/reduce_scatter | solution.py:159
  526.1 11.2 %copy-start.15 = (s32[1,8]{1,0:T(1,128)S(1)}, s32[1,8]{1,0:T(1,128)}, u32[]{:S(2)}) copy-start(s32[1,8]{1,0:T(1,128)} %param.25) | copy-start | bytes 100
  526.1 11.8 %copy-start.7 = (bf16[64,2048]{1,0:T(8,128)(2,1)S(1)}, bf16[64,2048]{1,0:T(8,128)(2,1)}, u32[]{:S(2)}) copy-start(bf16[64,2048]{1,0:T(8,128)(2,1)} %param.19) | copy-start | bytes 786436
  537.3 1.9 copy-start.2
  538.5 26.0 %copy-start.1 = (bf16[512,2048]{1,0:T(8,128)(2,1)S(1)}, bf16[512,2048]{1,0:T(8,128)(2,1)}, u32[]{:S(2)}) copy-start(bf16[512,2048]{1,0:T(8,128)(2,1)} %param.20) | copy-start | bytes 6291460
Sparse Core Ops, SparseCore 0:
  30.8 51.7 all-reduce.1
  537.4 25.1 reduce-scatter.1
where the time goes:
time: 573 us; the launch traced here: 571 us
  waiting for transfers between devices  253 us (44%)
  blocking collectives  197 us (34%)
  local copies, waits for them, and re-layouts  41.1 us (7%)
  other arithmetic  30.2 us (5%)
  matrix products  21.1 us (4%)
  between operations  15.9 us (3%)
  starting transfers between devices  12.6 us (2%)
    all_to_all x1, blocking collectives, on_device(): lax.all_to_all(outgoing, 'expert', split_axis=0, concat_axis=0, tiled=True)  197 us
    all_to_all x1, waiting for transfers between devices, on_device(): lax.all_to_all(pieces, 'expert', split_axis=0, concat_axis=0, tiled=True)  182 us
    psum x1, waiting for transfers between devices, on_device(): lax.psum(projected.astype(jnp.bfloat16), 'cuts').astype(jnp.float32)  47 us
    reduce_scatter x1, waiting for transfers between devices, on_device(): lax.psum_scatter(group_moe.astype(jnp.bfloat16), 'cuts', scatter_dimensio...  21.8 us
    gather x1, local copies, waits for them, and re-layouts, on_device(): returned.reshape(-1, width)[dest.reshape(-1)]  13.3 us
  transfers between devices with their start and end apart: 4, of which 4 were waited for; matrix products, arithmetic and copies ran while one was open for 2% of the time, Pallas kernels for 0%

commit v1 on v0

--- a/solution.py
+++ b/solution.py
@@ -9,6 +9,7 @@
 HEAD = 128
 TOPK = 4
 TREE = 64
+CAP = 8
 
 
 epsilon = 1e-06
@@ -95,7 +96,6 @@
     w_up,
     w_down,
 ):
-    cut_count = lax.axis_size("cuts")
     place = lax.axis_index("cuts")
     tok_rows = queries.shape[0]
     requests = tok_rows // TREE
@@ -117,50 +117,40 @@
     attended = attended.reshape(tok_rows, width)
     head_group = lax.all_to_all(attended, "cuts", split_axis=1, concat_axis=0, tiled=True)
     projected = jnp.dot(head_group, out_weight, preferred_element_type=jnp.float32)
+    projected_own = lax.psum_scatter(
+        projected.astype(jnp.bfloat16), "cuts", scatter_dimension=0, tiled=True
+    )
+    stream = residual.astype(jnp.float32) + projected_own.astype(jnp.float32)
+    normed = norm_rows(stream, norm_gain)
+
+    experts_all = w_gate.shape[0] * lax.axis_size("expert")
+    capacity = CAP
     start = place * tok_rows
-    own_part = lax.dynamic_slice_in_dim(projected, start, tok_rows, 0) + residual.astype(
-        jnp.float32
-    )
-    projected = lax.dynamic_update_slice_in_dim(projected, own_part, start, 0)
-    experts_all = w_gate.shape[0] * lax.axis_size("expert")
-    capacity = 2 * tok_rows * TOPK // experts_all
-    group_rows = cut_count * tok_rows
-    flat = routes.reshape(cut_count, tok_rows * TOPK)
-    onehot = (flat[:, :, None] == jnp.arange(experts_all, dtype=jnp.int32)[None, None, :]).astype(
-        jnp.int32
-    )
-    ahead = jnp.cumsum(onehot, axis=1) - onehot
-    slot_of = jnp.sum(ahead * onehot, axis=2)
-    gate_w = w_gate[0]
-    up_w = w_up[0]
-    down_w = w_down[0]
-    stream = lax.psum(projected.astype(jnp.bfloat16), "cuts").astype(jnp.float32)
-    normed = norm_rows(stream, norm_gain)
-    owner = jnp.arange(cut_count, dtype=jnp.int32)[:, None]
-    dest = flat * (cut_count * capacity) + owner * capacity + slot_of
-    token_of = jnp.arange(group_rows * TOPK, dtype=jnp.int32) // TOPK
-    table = (
-        jnp.full((experts_all * cut_count * capacity,), -1, jnp.int32)
-        .at[dest.reshape(-1)]
-        .set(token_of)
-    )
+    own_routes = lax.dynamic_slice_in_dim(routes, start, tok_rows, 0)
+    own_gains = lax.dynamic_slice_in_dim(route_weights, start, tok_rows, 0)
+    flat = own_routes.reshape(tok_rows * TOPK)
+    onehot = (flat[:, None] == jnp.arange(experts_all, dtype=jnp.int32)[None, :]).astype(jnp.int32)
+    ahead = jnp.cumsum(onehot, axis=0) - onehot
+    slot_of = jnp.sum(ahead * onehot, axis=1)
+    dest = flat * capacity + slot_of
+    token_of = jnp.arange(tok_rows * TOPK, dtype=jnp.int32) // TOPK
+    table = jnp.full((experts_all * capacity,), -1, jnp.int32).at[dest].set(token_of)
     filled = table >= 0
     outgoing = jnp.where(
         filled[:, None], normed[jnp.maximum(table, 0)], jnp.zeros((), jnp.bfloat16)
     )
-    outgoing = outgoing.reshape(experts_all, cut_count, capacity, width)
+    outgoing = outgoing.reshape(experts_all, capacity, width)
     arrived = lax.all_to_all(outgoing, "expert", split_axis=0, concat_axis=0, tiled=True)
-    arrived_shape = arrived.shape
-    product = expert_rows(arrived.reshape(-1, width), gate_w, up_w, down_w)
-    pieces = product.astype(jnp.bfloat16).reshape(arrived_shape)
-    returned = lax.all_to_all(pieces, "expert", split_axis=0, concat_axis=0, tiled=True)
-    picked = returned.reshape(-1, width)[dest.reshape(-1)].reshape(group_rows, TOPK, width)
-    group_moe = jnp.sum(route_weights.reshape(group_rows, TOPK, 1) * picked, axis=1)
-    moe_own = lax.psum_scatter(
-        group_moe.astype(jnp.bfloat16), "cuts", scatter_dimension=0, tiled=True
-    ).astype(jnp.float32)
-    stream_own = lax.dynamic_slice_in_dim(stream, start, tok_rows, 0)
-    layer_out = (stream_own + moe_own).astype(jnp.bfloat16)
+    gathered = lax.all_gather(arrived, "cuts", axis=0, tiled=True)
+    product = expert_rows(gathered.reshape(-1, width), w_gate[0], w_up[0], w_down[0])
+    pieces = product.astype(jnp.bfloat16)
+    summed = lax.psum_scatter(pieces, "cuts", scatter_dimension=0, tiled=True)
+    returned = lax.all_to_all(
+        summed.reshape(experts_all, capacity, width), "expert", split_axis=0, concat_axis=0, tiled=True
+    )
+    picked = returned.reshape(-1, width)[dest].reshape(tok_rows, TOPK, width)
+    moe = jnp.sum(own_gains[:, :, None] * picked.astype(jnp.float32), axis=1)
+    layer_out = (stream + moe).astype(jnp.bfloat16)
     picks = (jnp.arange(requests, dtype=jnp.int32)[:, None] * TREE + accepted_path).reshape(-1)
     accepted_kv = jnp.concatenate([new_keys[picks], new_values[picks]], axis=1)
     return (layer_out, accepted_kv)

time: 573 us -> 387 us (0.68)
  blocking collectives: 197 us -> 72.1 us
  local copies, waits for them, and re-layouts: 41.1 us -> 14.1 us
  other arithmetic: 30.2 us -> 10.3 us
  waiting for transfers between devices: 253 us -> 238 us
    all_to_all x2 -> x1, waiting for transfers between devices: 184 us -> 47.6 us  [on_device(): lax.all_to_all(summed.reshape(experts_all, capacity, width), 'expert', sp...]
    all_to_all x1, blocking collectives: 197 us -> 61.7 us  [on_device(): lax.all_to_all(outgoing, 'expert', split_axis=0, concat_axis=0, tiled=True)]
    reduce_scatter x1 -> x2, waiting for transfers between devices: 21.8 us -> 108 us  [the longest x1 84.3 us: on_device(): summed = lax.psum_scatter(pieces, 'cuts', scatter_dimension=0, tiled=True)]
    all_gather x0 -> x1, waiting for transfers between devices: none -> 81.5 us  [on_device(): gathered = lax.all_gather(arrived, 'cuts', axis=0, tiled=True)]
    psum x1 -> x0, waiting for transfers between devices: 47 us -> none  [on_device(): lax.psum(projected.astype(jnp.bfloat16), 'cuts').astype(jnp.float32)]
    all_to_all x0 -> x1, blocking collectives: none -> 10.4 us  [on_device(): lax.all_to_all(attended, 'cuts', split_axis=1, concat_axis=0, tiled=True)]
    gather x1, local copies, waits for them, and re-layouts: 13.3 us -> 4.22 us  [on_device(): picked = returned.reshape(-1, width)[dest].reshape(tok_rows, TOPK, width)]
    reduce_sum x2, other arithmetic: 11.3 us -> 3.32 us  [the longest x1 3.22 us: on_device(): moe = jnp.sum(own_gains[:, :, None] * picked.astype(jnp.float32), axis=1)]
  transfers between devices with their start and end apart: 4 -> 4, of which waited for: 4 -> 4; matrix products, arithmetic and copies ran while one was open for 2% -> 1% of each run, Pallas kernels for 0% -> 0%
where the time goes in v1:
time: 387 us; the launch traced here: 386 us
  waiting for transfers between devices  238 us (61%)
  blocking collectives  72.1 us (19%)
  matrix products  25.4 us (7%)
  between operations  15.6 us (4%)
  local copies, waits for them, and re-layouts  14.1 us (4%)
  starting transfers between devices  11.3 us (3%)
  other arithmetic  10.3 us (3%)
    reduce_scatter x1, waiting for transfers between devices, on_device(): summed = lax.psum_scatter(pieces, 'cuts', scatter_dimension=0, tiled=True)  84.3 us
    all_gather x1, waiting for transfers between devices, on_device(): gathered = lax.all_gather(arrived, 'cuts', axis=0, tiled=True)  81.5 us
    all_to_all x1, blocking collectives, on_device(): lax.all_to_all(outgoing, 'expert', split_axis=0, concat_axis=0, tiled=True)  61.7 us
    all_to_all x1, waiting for transfers between devices, on_device(): lax.all_to_all(summed.reshape(experts_all, capacity, width), 'expert', sp...  47.6 us
    reduce_scatter x1, waiting for transfers between devices, on_device(): lax.psum_scatter(projected.astype(jnp.bfloat16), 'cuts', scatter_dimensio...  24.1 us
    all_to_all x1, starting transfers between devices, on_device(): lax.all_to_all(summed.reshape(experts_all, capacity, width), 'expert', sp...  11 us
    all_to_all x1, blocking collectives, on_device(): lax.all_to_all(attended, 'cuts', split_axis=1, concat_axis=0, tiled=True)  10.4 us
  transfers between devices with their start and end apart: 4, of which 4 were waited for; matrix products, arithmetic and copies ran while one was open for 1% of the time, Pallas kernels for 0%

profile of v1, /device:TPU:1, one launch (start us, length us, event | category | flops | bytes accessed | tf_op | source)
XLA Modules:
  0.0 386.3 jit_solution(15995292803104930187)
XLA Ops:
  8.0 0.9 convolution_minimum_fusion.6
  9.0 0.2 convolution_minimum_fusion.5
  9.1 0.2 convolution_minimum_fusion.4
  9.3 0.2 convolution_minimum_fusion.3
  9.5 0.2 convolution_minimum_fusion.2
  9.6 0.2 convolution_minimum_fusion.1
  10.5 0.2 fusion.32
  10.8 1.9 fusion.16
  12.7 0.3 fusion.61
  13.0 0.6 fusion.17
  13.7 0.1 fusion.38
  13.8 0.3 fusion.39
  14.1 0.5 copy-done.10
  14.6 0.9 fusion.28
  15.5 0.2 copy.51
  15.7 0.1 convert_element_type.61
  15.9 10.4 %all_to_all.26 = bf16[64,4,512]{2,0,1:T(8,128)(2,1)S(1)} all-to-all(bf16[64,4,512]{2,0,1:T(8,128)(2,1)S(1)} %copy.52), channel_id=1, replica_groups=mesh['expert'=64,'cuts'=4] {'cuts'}, dimensions={1} | all-to-all | bytes 524288 | tf_op jit(solution)/shard_map/all_to_all | solution.py:118
  26.2 3.3 convolution_convert_fusion.1
  29.8 0.1 eq.75
  30.0 0.1 eq.71
  30.1 0.6 reduce-window.6
  30.7 0.2 slice_reduce_fusion
  31.0 0.1 mul.70
  31.1 0.1 fusion.51
  31.2 1.4 scatter_custom_fusion
  32.8 24.1 %reduce-scatter.3.cloned.1.call-done = bf16[64,2048]{1,0:T(8,128)(2,1)} async-done(((bf16[256,2048]{1,0:T(8,128)(2,1)}), bf16[64,2048]{1,0:T(8,128)(2,1)}) %reduce-scatter.3.cloned.1.call-update) | async-done | bytes 262160 | tf_op jit(solution)/shard_map/reduce_scatter | solution.py:120
  56.9 1.1 multiply_reduce_fusion.1
  58.1 1.1 multiply_convert_fusion
  59.2 3.3 gather_fusion
  62.5 1.8 bitcast_select_fusion
  64.3 61.7 %all_to_all.27 = bf16[64,8,2048]{2,1,0:T(8,128)(2,1)} all-to-all(bf16[64,8,2048]{2,1,0:T(8,128)(2,1)S(1)} %bitcast_select_fusion), channel_id=1, replica_groups=mesh['expert'=64,'cuts'=4] {'expert'}, dimensions={0} | all-to-all | bytes 4194304 | tf_op jit(solution)/shard_map/all_to_all | solution.py:143
  126.1 0.2 reduce-scatter.5.cloned.1.call-start
  126.3 81.5 %all-gather.2.cloned.1.call-done = bf16[256,8,2048]{2,1,0:T(8,128)(2,1)} async-done(((bf16[64,8,2048]{2,1,0:T(8,128)(2,1)}), bf16[256,8,2048]{2,1,0:T(8,128)(2,1)}) %all-gather.2.cloned.1.call-update) | async-done | bytes 8388624 | tf_op jit(solution)/shard_map/all_gather | solution.py:144
  207.7 6.4 %fusion.2 = f32[2048,352]{0,1:T(8,128)S(1)} fusion(bf16[256,8,2048]{2,1,0:T(8,128)(2,1)} %all-gather.2.cloned.1.call-done, bf16[1,2048,352]{1,2,0:T(8,128)(2,1)} %param.31), kind=kOutput, calls=%fused_computation.7 | convolution fusion | flops 2952790016 | bytes 12713984 | tf_op jit(solution)/shard_map/dot_general | solution.py:69
  214.1 0.2 copy-done.11
  214.4 3.5 fusion.7
  217.9 6.9 %convolution_convert_fusion = bf16[2048,2048]{1,0:T(8,128)(2,1)} fusion(bf16[2048,352]{0,1:T(8,128)(2,1)S(1)} %fusion.7, bf16[1,352,2048]{2,1,0:T(8,128)(2,1)S(1)} %copy-done.12), kind=kOutput, calls=%fused_computation.9 | convolution fusion | flops 2956984320 | bytes 11272192 | tf_op jit(solution)/shard_map/dot_general | solution.py:72
  224.8 84.3 %reduce-scatter.5.cloned.1.call-done = bf16[512,2048]{1,0:T(8,128)(2,1)} async-done(((bf16[2048,2048]{1,0:T(8,128)(2,1)}), bf16[512,2048]{1,0:T(8,128)(2,1)}) %reduce-scatter.5.cloned.1.call-update) | async-done | bytes 2097168 | tf_op jit(solution)/shard_map/reduce_scatter | solution.py:147
  309.1 11.0 %all-to-all-start.2 = ((bf16[64,8,2048]{2,1,0:T(8,128)(2,1)}), bf16[64,8,2048]{2,1,0:T(8,128)(2,1)}, u32[]{:S(2)}, u32[]{:S(2)}) async-start(bf16[64,8,2048]{2,1,0:T(8,128)(2,1)} %bitcast.126), calls=%async_computation.4 | async-start | bytes 4194304 | tf_op jit(solution)/shard_map/all_to_all | solution.py:148
  320.2 0.6 gather_fusion.2
  320.8 0.6 gather_fusion.3
  321.5 0.1 copy.53
  321.6 0.6 pad_maximum_fusion
  322.2 47.6 %all-to-all-done.2 = bf16[64,8,2048]{2,1,0:T(8,128)(2,1)} async-done(((bf16[64,8,2048]{2,1,0:T(8,128)(2,1)}), bf16[64,8,2048]{2,1,0:T(8,128)(2,1)}, u32[]{:S(2)}, u32[]{:S(2)}) %all-to-all-start.2) | async-done | bytes 2097184 | tf_op jit(solution)/shard_map/all_to_all | solution.py:148
  369.8 4.2 %gather_fusion.1 = bf16[256,2048]{1,0:T(8,128)(2,1)S(1)} fusion(bf16[512,2048]{1,0:T(8,128)(2,1)} %bitcast.15, s32[1024]{0:T(1024)S(1)} %pad_clamp_fusion.1), kind=kCustom, calls=%fused_computation.1 | custom fusion | bytes 2098176 | tf_op jit(solution)/shard_map/gather | solution.py:151
  374.0 1.7 reshape.194
  375.7 3.2 multiply_reduce_fusion
  379.0 0.8 add_convert_fusion
  (54 shorter events, 0.9 us)
Async XLA Ops:
  7.2 3.6 copy-start
  7.2 49.8 %reduce-scatter.3.cloned.1.call-start = ((), (), s32[]{:S(2)}) async-start(), calls=%async_computation.5 | async-start | bytes 1310720 | tf_op jit(solution)/shard_map/reduce_scatter | solution.py:120
  10.8 2.0 copy-start.3
  10.8 2.0 copy-start.4
  12.7 1.1 copy-start.5
  13.0 1.6 copy-start.10
  26.2 3.4 copy-start.7
  26.2 30.7 %copy-start.1 = (bf16[64,2048]{1,0:T(8,128)(2,1)S(1)}, bf16[64,2048]{1,0:T(8,128)(2,1)}, u32[]{:S(2)}) copy-start(bf16[64,2048]{1,0:T(8,128)(2,1)} %param.26) | copy-start | bytes 786436
  26.2 31.9 %copy-start.6 = (f32[2048]{0:T(1024)S(1)}, f32[2048]{0:T(1024)}, u32[]{:S(2)}) copy-start(f32[2048]{0:T(1024)} %param.27) | copy-start | bytes 24580
  29.6 178.1 %all-gather.2.cloned.1.call-start = ((), (), s32[]{:S(2)}) async-start(), calls=%async_computation.6 | async-start | bytes 10485760 | tf_op jit(solution)/shard_map/all_gather | solution.py:144
  126.1 183.1 %reduce-scatter.5.cloned.1.call-start = ((), (), s32[]{:S(2)}) async-start(), calls=%async_computation.7 | async-start | bytes 10485760 | tf_op jit(solution)/shard_map/reduce_scatter | solution.py:147
  207.7 6.4 %copy-start.9 = (bf16[256,8,2048]{2,1,0:T(8,128)(2,1)S(1)}, bf16[256,8,2048]{2,1,0:T(8,128)(2,1)}, u32[]{:S(2)}) copy-start(bf16[256,8,2048]{2,1,0:T(8,128)(2,1)} %all-gather.2.cloned.1.call-done) | copy-start | bytes 25165828
  207.7 6.6 %copy-start.11 = (bf16[1,2048,352]{1,2,0:T(8,128)(2,1)S(1)}, bf16[1,2048,352]{1,2,0:T(8,128)(2,1)}, u32[]{:S(2)}) copy-start(bf16[1,2048,352]{1,2,0:T(8,128)(2,1)} %param.32) | copy-start | bytes 4325380
  214.4 3.5 copy-start.12
  309.1 11.0 %copy-start.13 = (s32[1,8]{1,0:T(1,128)S(1)}, s32[1,8]{1,0:T(1,128)}, u32[]{:S(2)}) copy-start(s32[1,8]{1,0:T(1,128)} %param.25) | copy-start | bytes 100
  309.1 12.2 %copy-start.8 = (f32[256,4]{0,1:T(4,128)S(1)}, f32[256,4]{0,1:T(4,128)}, u32[]{:S(2)}) copy-start(f32[256,4]{0,1:T(4,128)} %param.30) | copy-start | bytes 12292
  309.1 60.7 %all-to-all-start.2 = ((bf16[64,8,2048]{2,1,0:T(8,128)(2,1)}), bf16[64,8,2048]{2,1,0:T(8,128)(2,1)}, u32[]{:S(2)}, u32[]{:S(2)}) async-start(bf16[64,8,2048]{2,1,0:T(8,128)(2,1)} %bitcast.126), calls=%async_computation.4 | async-start | bytes 4194304 | tf_op jit(solution)/shard_map/all_to_all | solution.py:148
  375.7 3.2 copy-start.2
Sparse Core Ops, SparseCore 0:
  29.7 27.1 reduce-scatter.2
  126.2 81.5 all-gather.1
  224.9 84.1 reduce-scatter.4

commit v2 on v1

--- a/solution.py
+++ b/solution.py
@@ -10,6 +10,7 @@
 TOPK = 4
 TREE = 64
 CAP = 8
+N_CHUNKS = 2
 
 
 epsilon = 1e-06
@@ -140,14 +141,21 @@
         filled[:, None], normed[jnp.maximum(table, 0)], jnp.zeros((), jnp.bfloat16)
     )
     outgoing = outgoing.reshape(experts_all, capacity, width)
-    arrived = lax.all_to_all(outgoing, "expert", split_axis=0, concat_axis=0, tiled=True)
-    gathered = lax.all_gather(arrived, "cuts", axis=0, tiled=True)
-    product = expert_rows(gathered.reshape(-1, width), w_gate[0], w_up[0], w_down[0])
-    pieces = product.astype(jnp.bfloat16)
-    summed = lax.psum_scatter(pieces, "cuts", scatter_dimension=0, tiled=True)
-    returned = lax.all_to_all(
-        summed.reshape(experts_all, capacity, width), "expert", split_axis=0, concat_axis=0, tiled=True
-    )
+    chunk = capacity // N_CHUNKS
+    returned_parts = []
+    for part in range(N_CHUNKS):
+        sending = outgoing[:, part * chunk:(part + 1) * chunk]
+        arrived = lax.all_to_all(sending, "expert", split_axis=0, concat_axis=0, tiled=True)
+        gathered = lax.all_gather(arrived, "cuts", axis=0, tiled=True)
+        product = expert_rows(gathered.reshape(-1, width), w_gate[0], w_up[0], w_down[0])
+        pieces = product.astype(jnp.bfloat16)
+        summed = lax.psum_scatter(pieces, "cuts", scatter_dimension=0, tiled=True)
+        returned_parts.append(
+            lax.all_to_all(
+                summed.reshape(experts_all, chunk, width), "expert", split_axis=0, concat_axis=0, tiled=True
+            )
+        )
+    returned = jnp.concatenate(returned_parts, axis=1)
     picked = returned.reshape(-1, width)[dest].reshape(tok_rows, TOPK, width)
     moe = jnp.sum(own_gains[:, :, None] * picked.astype(jnp.float32), axis=1)
     layer_out = (stream + moe).astype(jnp.bfloat16)

time: 387 us -> 363 us (0.938)
  waiting for transfers between devices: 238 us -> 161 us
  local copies, waits for them, and re-layouts: 14.1 us -> 29.6 us
  blocking collectives: 72.1 us -> 85.1 us
  matrix products: 25.4 us -> 37.2 us
  starting transfers between devices: 11.3 us -> 22 us
    all_gather x1 -> x2, waiting for transfers between devices: 81.5 us -> 42.4 us  [on_device(): gathered = lax.all_gather(arrived, 'cuts', axis=0, tiled=True)]
    all_to_all x1 -> x2, waiting for transfers between devices: 47.6 us -> 26 us  [on_device(): lax.all_to_all(summed.reshape(experts_all, chunk, width), 'expert', split...]
    reshape x0 -> x4, local copies, waits for them, and re-layouts: none -> 18.3 us  [the longest x2 13.8 us: on_device(): gathered.reshape(-1, width)]
    reduce_scatter x1 -> x2, waiting for transfers between devices: 84.3 us -> 68.7 us  [on_device(): summed = lax.psum_scatter(pieces, 'cuts', scatter_dimension=0, tiled=True)]
    dot_general x1 -> x2, matrix products: 6.86 us -> 20.1 us  [expert_rows(): return jnp.dot(hidden, down_w, preferred_element_type=jnp.float32)]
    all_to_all x1 -> x2, blocking collectives: 61.7 us -> 74.6 us  [on_device(): lax.all_to_all(sending, 'expert', split_axis=0, concat_axis=0, tiled=True)]
    all_to_all x1 -> x2, starting transfers between devices: 11 us -> 21.6 us  [on_device(): lax.all_to_all(summed.reshape(experts_all, chunk, width), 'expert', split...]
    dot_general x1 -> x2, matrix products: 6.36 us -> 10.1 us  [expert_rows(): gate = jnp.dot(flat_in, gate_w, preferred_element_type=jnp.float32)]
  transfers between devices with their start and end apart: 4 -> 7, of which waited for: 4 -> 6; matrix products, arithmetic and copies ran while one was open for 1% -> 15% of each run, Pallas kernels for 0% -> 0%
where the time goes in v2:
time: 363 us; the launch traced here: 362 us
  waiting for transfers between devices  161 us (44%)
  blocking collectives  85.1 us (23%)
  matrix products  37.2 us (10%)
  local copies, waits for them, and re-layouts  29.6 us (8%)
  starting transfers between devices  22 us (6%)
  between operations  15.7 us (4%)
  other arithmetic  11 us (3%)
    all_to_all x2, blocking collectives, on_device(): lax.all_to_all(sending, 'expert', split_axis=0, concat_axis=0, tiled=True)  74.6 us
    reduce_scatter x2, waiting for transfers between devices, on_device(): summed = lax.psum_scatter(pieces, 'cuts', scatter_dimension=0, tiled=True)  68.7 us
    all_gather x2, waiting for transfers between devices, on_device(): gathered = lax.all_gather(arrived, 'cuts', axis=0, tiled=True)  42.4 us
    all_to_all x2, waiting for transfers between devices, on_device(): lax.all_to_all(summed.reshape(experts_all, chunk, width), 'expert', split...  26 us
    reduce_scatter x1, waiting for transfers between devices, on_device(): lax.psum_scatter(projected.astype(jnp.bfloat16), 'cuts', scatter_dimensio...  24.1 us
    all_to_all x2, starting transfers between devices, on_device(): lax.all_to_all(summed.reshape(experts_all, chunk, width), 'expert', split...  21.6 us
    dot_general x2, matrix products, expert_rows(): return jnp.dot(hidden, down_w, preferred_element_type=jnp.float32)  20.1 us
    reshape x2, local copies, waits for them, and re-layouts, on_device(): gathered.reshape(-1, width)  13.8 us
  transfers between devices with their start and end apart: 7, of which 6 were waited for; matrix products, arithmetic and copies ran while one was open for 15% of the time, Pallas kernels for 0%

profile of v2, /device:TPU:1, one launch (start us, length us, event | category | flops | bytes accessed | tf_op | source)
XLA Modules:
  0.0 362.0 jit_solution(2847067877698913783)
XLA Ops:
  8.0 0.9 convolution_minimum_fusion.6
  9.0 0.2 convolution_minimum_fusion.5
  9.5 0.2 convolution_minimum_fusion.2
  10.5 0.2 fusion.33
  10.8 1.9 fusion.6
  12.7 0.3 fusion.71
  13.0 0.6 fusion.7
  13.8 0.3 fusion.46
  14.1 0.5 copy-done.13
  14.6 0.9 fusion.29
  15.5 0.2 copy.51
  15.9 10.5 %all_to_all.36 = bf16[64,4,512]{2,0,1:T(8,128)(2,1)S(1)} all-to-all(bf16[64,4,512]{2,0,1:T(8,128)(2,1)S(1)} %copy.52), channel_id=1, replica_groups=mesh['expert'=64,'cuts'=4] {'cuts'}, dimensions={1} | all-to-all | bytes 524288 | tf_op jit(solution)/shard_map/all_to_all | solution.py:119
  26.4 1.7 convolution_convert_fusion.2
  28.6 0.6 reduce-window.6
  29.2 0.2 slice_reduce_fusion
  29.8 1.4 scatter_custom_fusion
  31.3 24.1 %reduce-scatter.4.cloned.1.call-done = bf16[64,2048]{1,0:T(8,128)(2,1)} async-done(((bf16[256,2048]{1,0:T(8,128)(2,1)}), bf16[64,2048]{1,0:T(8,128)(2,1)}) %reduce-scatter.4.cloned.1.call-update) | async-done | bytes 262160 | tf_op jit(solution)/shard_map/reduce_scatter | solution.py:121
  55.5 1.1 multiply_reduce_fusion.1
  56.6 1.1 multiply_convert_fusion
  57.7 2.5 gather_fusion
  60.2 0.2 bitcast_select_fusion
  60.4 1.1 fusion.70
  61.5 40.3 %all_to_all.37 = bf16[64,4,2048]{2,1,0:T(4,128)(2,1)} all-to-all(bf16[64,4,2048]{2,1,0:T(4,128)(2,1)S(1)} %get-tuple-element.24), channel_id=1, replica_groups=mesh['expert'=64,'cuts'=4] {'expert'}, dimensions={0} | all-to-all | bytes 2097152 | tf_op jit(solution)/shard_map/all_to_all | solution.py:148
  101.9 34.3 %all_to_all.38 = bf16[64,4,2048]{2,1,0:T(4,128)(2,1)} all-to-all(bf16[64,4,2048]{2,1,0:T(4,128)(2,1)S(1)} %get-tuple-element.25), channel_id=1, replica_groups=mesh['expert'=64,'cuts'=4] {'expert'}, dimensions={0} | all-to-all | bytes 2097152 | tf_op jit(solution)/shard_map/all_to_all | solution.py:148
  136.3 0.2 reduce-scatter.6.cloned.1.call-start
  136.5 11.5 %all-gather.3.cloned.1.call-done = bf16[256,4,2048]{2,1,0:T(4,128)(2,1)} async-done(((bf16[64,4,2048]{2,1,0:T(4,128)(2,1)}), bf16[256,4,2048]{2,1,0:T(4,128)(2,1)}) %all-gather.3.cloned.1.call-update) | async-done | bytes 4194320 | tf_op jit(solution)/shard_map/all_gather | solution.py:149
  147.9 6.9 %reshape.196 = bf16[1024,2048]{1,0:T(8,128)(2,1)} reshape(bf16[256,4,2048]{2,1,0:T(4,128)(2,1)} %all-gather.3.cloned.1.call-done) | data formatting | bytes 8388608 | tf_op jit(solution)/shard_map/reshape | solution.py:150
  154.9 5.1 %fusion.14 = f32[1024,352]{0,1:T(8,128)} fusion(bf16[1024,2048]{1,0:T(8,128)(2,1)} %reshape.196, bf16[1,2048,352]{1,2,0:T(8,128)(2,1)S(1)} %copy-done.14), kind=kOutput, calls=%fused_computation.30 | convolution fusion | flops 1476395008 | bytes 7077888 | tf_op jit(solution)/shard_map/dot_general | solution.py:70
  159.9 9.9 %convolution_convert_fusion.1 = bf16[1024,2048]{1,0:T(8,128)(2,1)} fusion(bf16[1,352,2048]{2,1,0:T(8,128)(2,1)} %param.33, bf16[1024,2048]{1,0:T(8,128)(2,1)} %reshape.196, bf16[1,2048,352]{1,2,0:T(8,128)(2,1)} %param.32, f32[1024,352]{0,1:T(8,128)} %fusion.14), kind=kOutput, calls=%fused_computation.6 | convolution fusion | flops 2957049856 | bytes 12713984 | tf_op jit(solution)/shard_map/dot_general | solution.py:73
  169.9 31.0 %all-gather.5.cloned.1.call-done = bf16[256,4,2048]{2,1,0:T(4,128)(2,1)} async-done(((bf16[64,4,2048]{2,1,0:T(4,128)(2,1)}), bf16[256,4,2048]{2,1,0:T(4,128)(2,1)}) %all-gather.5.cloned.1.call-update) | async-done | bytes 4194320 | tf_op jit(solution)/shard_map/all_gather | solution.py:149
  200.9 6.9 %reshape.198 = bf16[1024,2048]{1,0:T(8,128)(2,1)} reshape(bf16[256,4,2048]{2,1,0:T(4,128)(2,1)} %all-gather.5.cloned.1.call-done) | data formatting | bytes 8388608 | tf_op jit(solution)/shard_map/reshape | solution.py:150
  207.8 5.0 %fusion.12 = f32[1024,352]{0,1:T(8,128)} fusion(bf16[1024,2048]{1,0:T(8,128)(2,1)} %reshape.198, bf16[1,2048,352]{1,2,0:T(8,128)(2,1)S(1)} %copy-done.14), kind=kOutput, calls=%fused_computation.28 | convolution fusion | flops 1476395008 | bytes 7077888 | tf_op jit(solution)/shard_map/dot_general | solution.py:70
  212.9 10.2 %convolution_convert_fusion = bf16[1024,2048]{1,0:T(8,128)(2,1)} fusion(bf16[1,352,2048]{2,1,0:T(8,128)(2,1)} %param.33, bf16[1024,2048]{1,0:T(8,128)(2,1)} %reshape.198, bf16[1,2048,352]{1,2,0:T(8,128)(2,1)} %param.32, f32[1024,352]{0,1:T(8,128)} %fusion.12), kind=kOutput, calls=%fused_computation.5 | convolution fusion | flops 2957049856 | bytes 12713984 | tf_op jit(solution)/shard_map/dot_general | solution.py:73
  223.1 30.1 %reduce-scatter.6.cloned.1.call-done = bf16[256,2048]{1,0:T(8,128)(2,1)} async-done(((bf16[1024,2048]{1,0:T(8,128)(2,1)}), bf16[256,2048]{1,0:T(8,128)(2,1)}) %reduce-scatter.6.cloned.1.call-update) | async-done | bytes 1048592 | tf_op jit(solution)/shard_map/reduce_scatter | solution.py:152
  253.2 2.3 reshape.197
  255.5 10.7 %all-to-all-start.2 = ((bf16[64,4,2048]{2,1,0:T(4,128)(2,1)}), bf16[64,4,2048]{2,1,0:T(4,128)(2,1)S(1)}, u32[]{:S(2)}, u32[]{:S(2)}) async-start(bf16[64,4,2048]{2,1,0:T(4,128)(2,1)} %reshape.197), calls=%async_computation.4 | async-start | bytes 2097152 | tf_op jit(solution)/shard_map/all_to_all | solution.py:154
  266.2 38.6 %reduce-scatter.8.cloned.1.call-done = bf16[256,2048]{1,0:T(8,128)(2,1)} async-done(((bf16[1024,2048]{1,0:T(8,128)(2,1)}), bf16[256,2048]{1,0:T(8,128)(2,1)}) %reduce-scatter.8.cloned.1.call-update) | async-done | bytes 1048592 | tf_op jit(solution)/shard_map/reduce_scatter | solution.py:152
  304.8 2.3 reshape.199
  307.1 10.9 %all-to-all-start.4 = ((bf16[64,4,2048]{2,1,0:T(4,128)(2,1)}), bf16[64,4,2048]{2,1,0:T(4,128)(2,1)}, u32[]{:S(2)}, u32[]{:S(2)}) async-start(bf16[64,4,2048]{2,1,0:T(4,128)(2,1)} %reshape.199), calls=%async_computation.7 | async-start | bytes 2097152 | tf_op jit(solution)/shard_map/all_to_all | solution.py:154
  318.0 0.6 gather_fusion.2
  318.6 0.6 gather_fusion.3
  319.4 0.6 pad_maximum_fusion
  320.0 26.0 %all-to-all-done.4 = bf16[64,4,2048]{2,1,0:T(4,128)(2,1)} async-done(((bf16[64,4,2048]{2,1,0:T(4,128)(2,1)}), bf16[64,4,2048]{2,1,0:T(4,128)(2,1)}, u32[]{:S(2)}, u32[]{:S(2)}) %all-to-all-start.4) | async-done | bytes 1048608 | tf_op jit(solution)/shard_map/all_to_all | solution.py:154
  346.1 2.3 maximum_bitcast_fusion
  348.4 1.4 gather_fusion.1
  349.7 1.7 reshape.202
  351.5 3.2 multiply_reduce_fusion
  354.7 0.8 add_convert_fusion
  (74 shorter events, 2.3 us)
Async XLA Ops:
  7.2 3.6 copy-start
  7.2 48.3 %reduce-scatter.4.cloned.1.call-start = ((), (), s32[]{:S(2)}) async-start(), calls=%async_computation.8 | async-start | bytes 1310720 | tf_op jit(solution)/shard_map/reduce_scatter | solution.py:121
  10.8 2.0 copy-start.5
  10.8 2.0 copy-start.6
  12.7 1.1 copy-start.8
  13.0 1.6 copy-start.13
  15.5 10.8 %copy-start.4 = (bf16[512,2048]{1,0:T(8,128)(2,1)S(1)}, bf16[512,2048]{1,0:T(8,128)(2,1)}, u32[]{:S(2)}) copy-start(bf16[512,2048]{1,0:T(8,128)(2,1)} %param.28) | copy-start | bytes 6291460
  26.4 1.8 copy-start.11
  26.4 29.1 %copy-start.2 = (bf16[64,2048]{1,0:T(8,128)(2,1)S(1)}, bf16[64,2048]{1,0:T(8,128)(2,1)}, u32[]{:S(2)}) copy-start(bf16[64,2048]{1,0:T(8,128)(2,1)} %param.26) | copy-start | bytes 786436
  26.4 30.2 %copy-start.10 = (f32[2048]{0:T(1024)S(1)}, f32[2048]{0:T(1024)}, u32[]{:S(2)}) copy-start(f32[2048]{0:T(1024)} %param.27) | copy-start | bytes 24580
  28.1 119.8 %all-gather.3.cloned.1.call-start = ((), (), s32[]{:S(2)}) async-start(), calls=%async_computation.9 | async-start | bytes 5242880 | tf_op jit(solution)/shard_map/all_gather | solution.py:149
  101.8 99.1 %all-gather.5.cloned.1.call-start = ((), (), s32[]{:S(2)}) async-start(), calls=%async_computation.11 | async-start | bytes 5242880 | tf_op jit(solution)/shard_map/all_gather | solution.py:149
  136.2 18.6 %copy-start.14 = (bf16[1,2048,352]{1,2,0:T(8,128)(2,1)S(1)}, bf16[1,2048,352]{1,2,0:T(8,128)(2,1)}, u32[]{:S(2)}) copy-start(bf16[1,2048,352]{1,2,0:T(8,128)(2,1)} %param.31) | copy-start | bytes 4325380
  136.3 117.0 %reduce-scatter.6.cloned.1.call-start = ((), (), s32[]{:S(2)}) async-start(), calls=%async_computation.10 | async-start | bytes 5242880 | tf_op jit(solution)/shard_map/reduce_scatter | solution.py:152
  169.9 134.9 %reduce-scatter.8.cloned.1.call-start = ((), (), s32[]{:S(2)}) async-start(), calls=%async_computation.12 | async-start | bytes 5242880 | tf_op jit(solution)/shard_map/reduce_scatter | solution.py:152
  255.5 51.6 %all-to-all-start.2 = ((bf16[64,4,2048]{2,1,0:T(4,128)(2,1)}), bf16[64,4,2048]{2,1,0:T(4,128)(2,1)S(1)}, u32[]{:S(2)}, u32[]{:S(2)}) async-start(bf16[64,4,2048]{2,1,0:T(4,128)(2,1)} %reshape.197), calls=%async_computation.4 | async-start | bytes 2097152 | tf_op jit(solution)/shard_map/all_to_all | solution.py:154
  266.2 51.8 %copy-start.15 = (s32[1,8]{1,0:T(1,128)S(1)}, s32[1,8]{1,0:T(1,128)}, u32[]{:S(2)}) copy-start(s32[1,8]{1,0:T(1,128)} %param.25) | copy-start | bytes 100
  266.2 51.8 %copy-start.7 = (bf16[64,2048]{1,0:T(8,128)(2,1)S(1)}, bf16[64,2048]{1,0:T(8,128)(2,1)}, u32[]{:S(2)}) copy-start(bf16[64,2048]{1,0:T(8,128)(2,1)} %param.18) | copy-start | bytes 786436
  266.2 52.4 %copy-start.9 = (bf16[64,2048]{1,0:T(8,128)(2,1)S(1)}, bf16[64,2048]{1,0:T(8,128)(2,1)}, u32[]{:S(2)}) copy-start(bf16[64,2048]{1,0:T(8,128)(2,1)} %param.19) | copy-start | bytes 786436
  266.2 53.0 %copy-start.12 = (f32[256,4]{0,1:T(4,128)S(1)}, f32[256,4]{0,1:T(4,128)}, u32[]{:S(2)}) copy-start(f32[256,4]{0,1:T(4,128)} %param.30) | copy-start | bytes 12292
  307.1 39.0 %all-to-all-start.4 = ((bf16[64,4,2048]{2,1,0:T(4,128)(2,1)}), bf16[64,4,2048]{2,1,0:T(4,128)(2,1)}, u32[]{:S(2)}, u32[]{:S(2)}) async-start(bf16[64,4,2048]{2,1,0:T(4,128)(2,1)} %reshape.199), calls=%async_computation.7 | async-start | bytes 2097152 | tf_op jit(solution)/shard_map/all_to_all | solution.py:154
  349.7 5.8 %copy-start.1 = (bf16[512,2048]{1,0:T(8,128)(2,1)S(1)}, bf16[512,2048]{1,0:T(8,128)(2,1)}, u32[]{:S(2)}) copy-start(bf16[512,2048]{1,0:T(8,128)(2,1)} %param.20) | copy-start | bytes 6291460
  351.5 3.2 copy-start.3
Sparse Core Ops, SparseCore 0:
  28.2 27.1 reduce-scatter.3
  101.9 45.9 all-gather.2
  149.8 51.1 all-gather.4
  203.3 49.8 reduce-scatter.5
  255.6 49.1 reduce-scatter.7

commit v3 on v1

--- a/solution.py
+++ b/solution.py
@@ -10,6 +10,7 @@
 TOPK = 4
 TREE = 64
 CAP = 8
+N_CHUNKS = 2
 
 
 epsilon = 1e-06
@@ -116,11 +117,18 @@
     )
     attended = attended.reshape(tok_rows, width)
     head_group = lax.all_to_all(attended, "cuts", split_axis=1, concat_axis=0, tiled=True)
+    gate_full = lax.all_gather(w_gate[0], "cuts", axis=0)
+    up_full = lax.all_gather(w_up[0], "cuts", axis=0)
+    down_full = lax.all_gather(w_down[0], "cuts", axis=0)
     projected = jnp.dot(head_group, out_weight, preferred_element_type=jnp.float32)
-    projected_own = lax.psum_scatter(
-        projected.astype(jnp.bfloat16), "cuts", scatter_dimension=0, tiled=True
+    partials = lax.all_to_all(
+        projected.astype(jnp.bfloat16).reshape(lax.axis_size("cuts"), tok_rows, width),
+        "cuts",
+        split_axis=0,
+        concat_axis=0,
+        tiled=True,
     )
-    stream = residual.astype(jnp.float32) + projected_own.astype(jnp.float32)
+    stream = residual.astype(jnp.float32) + jnp.sum(partials.astype(jnp.float32), axis=0)
     normed = norm_rows(stream, norm_gain)
 
     experts_all = w_gate.shape[0] * lax.axis_size("expert")
@@ -141,12 +149,17 @@
     )
     outgoing = outgoing.reshape(experts_all, capacity, width)
     arrived = lax.all_to_all(outgoing, "expert", split_axis=0, concat_axis=0, tiled=True)
-    gathered = lax.all_gather(arrived, "cuts", axis=0, tiled=True)
-    product = expert_rows(gathered.reshape(-1, width), w_gate[0], w_up[0], w_down[0])
-    pieces = product.astype(jnp.bfloat16)
-    summed = lax.psum_scatter(pieces, "cuts", scatter_dimension=0, tiled=True)
+    rows = arrived.reshape(-1, width)
+    gate = jnp.einsum("rd,cdf->rcf", rows, gate_full, preferred_element_type=jnp.float32)
+    upper = jnp.einsum("rd,cdf->rcf", rows, up_full, preferred_element_type=jnp.float32)
+    hidden = (jax.nn.silu(gate) * upper).astype(jnp.bfloat16)
+    product = jnp.einsum("rcf,cfd->rd", hidden, down_full, preferred_element_type=jnp.float32)
     returned = lax.all_to_all(
-        summed.reshape(experts_all, capacity, width), "expert", split_axis=0, concat_axis=0, tiled=True
+        product.astype(jnp.bfloat16).reshape(experts_all, capacity, width),
+        "expert",
+        split_axis=0,
+        concat_axis=0,
+        tiled=True,
     )
     picked = returned.reshape(-1, width)[dest].reshape(tok_rows, TOPK, width)
     moe = jnp.sum(own_gains[:, :, None] * picked.astype(jnp.float32), axis=1)

time: 387 us -> 316 us (0.82)
  waiting for transfers between devices: 238 us -> 159 us
  starting transfers between devices: 11.3 us -> 20.7 us
  blocking collectives: 72.1 us -> 64.1 us
    reduce_scatter x2 -> x0, waiting for transfers between devices: 108 us -> none  [the longest x1 84.3 us: on_device(): summed = lax.psum_scatter(pieces, 'cuts', scatter_dimension=0, tiled=True)]
    all_to_all x1 -> x3, waiting for transfers between devices: 47.6 us -> 76 us  [the longest x1 47.6 us: on_device(): lax.all_to_all(product.astype(jnp.bfloat16).reshape(experts_all, capacity...]
    all_to_all x1 -> x0, blocking collectives: 10.4 us -> none  [on_device(): lax.all_to_all(attended, 'cuts', split_axis=1, concat_axis=0, tiled=True)]
    all_to_all x1 -> x3, starting transfers between devices: 11 us -> 20.5 us  [the longest x1 11.2 us: on_device(): lax.all_to_all(product.astype(jnp.bfloat16).reshape(experts_all, capacity...]
    dot_general x3 -> x2, matrix products: 16.7 us -> 22.2 us  [the longest x1 14.1 us: on_device(): jnp.einsum('rcf,cfd->rd', hidden, down_full, preferred_element_type=jnp.f...]
    all_gather x1 -> x3, waiting for transfers between devices: 81.5 us -> 80.8 us  [the longest x1 66.3 us: on_device(): down_full = lax.all_gather(w_down[0], 'cuts', axis=0)]
  transfers between devices with their start and end apart: 4 -> 6, of which waited for: 4 -> 5; matrix products, arithmetic and copies ran while one was open for 1% -> 9% of each run, Pallas kernels for 0% -> 0%
where the time goes in v3:
time: 316 us; the launch traced here: 315 us
  waiting for transfers between devices  159 us (50%)
  blocking collectives  64.1 us (20%)
  matrix products  29.1 us (9%)
  starting transfers between devices  20.7 us (7%)
  local copies, waits for them, and re-layouts  16.5 us (5%)
  between operations  15.4 us (5%)
  other arithmetic  9.85 us (3%)
    all_gather x1, waiting for transfers between devices, on_device(): down_full = lax.all_gather(w_down[0], 'cuts', axis=0)  66.3 us
    all_to_all x1, blocking collectives, on_device(): lax.all_to_all(outgoing, 'expert', split_axis=0, concat_axis=0, tiled=True)  64.1 us
    all_to_all x1, waiting for transfers between devices, on_device(): lax.all_to_all(product.astype(jnp.bfloat16).reshape(experts_all, capacity...  47.6 us
    all_to_all x1, waiting for transfers between devices, on_device(): lax.all_to_all(projected.astype(jnp.bfloat16).reshape(lax.axis_size('cuts...  24.3 us
    all_gather x1, waiting for transfers between devices, on_device(): gate_full = lax.all_gather(w_gate[0], 'cuts', axis=0)  14.6 us
    dot_general x1, matrix products, on_device(): jnp.einsum('rcf,cfd->rd', hidden, down_full, preferred_element_type=jnp.f...  14.1 us
    all_to_all x1, starting transfers between devices, on_device(): lax.all_to_all(product.astype(jnp.bfloat16).reshape(experts_all, capacity...  11.2 us
    dot_general x1, matrix products, on_device(): jnp.einsum('rd,cdf->rcf', rows, up_full, preferred_element_type=jnp.float32)  8.11 us
  transfers between devices with their start and end apart: 6, of which 5 were waited for; matrix products, arithmetic and copies ran while one was open for 9% of the time, Pallas kernels for 0%

profile of v3, /device:TPU:1, one launch (start us, length us, event | category | flops | bytes accessed | tf_op | source)
XLA Modules:
  0.0 314.5 jit_solution(4136722881336585013)
XLA Ops:
  7.2 0.7 all-gather.6.cloned.1.call-update
  8.0 0.7 all-gather.4.cloned.1.call-update
  8.7 0.7 all-gather.8.cloned.1.call-update
  10.1 0.2 convolution_minimum_fusion.6
  10.3 0.2 convolution_minimum_fusion.5
  10.5 0.2 convolution_minimum_fusion.4
  10.6 0.2 convolution_minimum_fusion.3
  10.8 0.2 convolution_minimum_fusion.2
  11.0 0.2 convolution_minimum_fusion.1
  11.8 0.2 fusion.26
  12.1 0.9 fusion.13
  13.1 0.3 fusion.58
  13.4 0.6 fusion.14
  14.0 0.1 fusion.34
  14.1 0.3 fusion.35
  14.4 0.5 copy-done.9
  15.0 0.9 fusion.22
  15.9 0.2 copy.51
  16.2 0.7 copy.52
  16.9 5.0 %all-to-all-start = ((bf16[64,4,512]{2,0,1:T(8,128)(2,1)}), bf16[64,4,512]{2,0,1:T(8,128)(2,1)S(1)}, u32[]{:S(2)}, u32[]{:S(2)}) async-start(bf16[64,4,512]{2,0,1:T(8,128)(2,1)} %copy.52), calls=%async_computation | async-start | bytes 524288 | tf_op jit(solution)/shard_map/all_to_all | solution.py:119
  22.2 0.1 eq.71
  22.3 0.6 reduce-window.6
  22.9 0.2 slice_reduce_fusion
  23.1 0.1 fusion.47
  23.3 4.2 %all-to-all-done = bf16[64,4,512]{2,0,1:T(8,128)(2,1)S(1)} async-done(((bf16[64,4,512]{2,0,1:T(8,128)(2,1)}), bf16[64,4,512]{2,0,1:T(8,128)(2,1)S(1)}, u32[]{:S(2)}, u32[]{:S(2)}) %all-to-all-start) | async-done | bytes 262176 | tf_op jit(solution)/shard_map/all_to_all | solution.py:119
  27.4 3.4 %convolution_convert_fusion = bf16[256,2048]{1,0:T(8,128)(2,1)} fusion(bf16[256,512]{1,0:T(8,128)(2,1)S(1)} %bitcast.127, bf16[512,2048]{1,0:T(8,128)(2,1)} %param.28), kind=kOutput, calls=%fused_computation.8 | convolution fusion | flops 537395200 | bytes 3407872 | tf_op jit(solution)/shard_map/dot_general | solution.py:123
  30.8 4.4 %all-to-all-start.1 = ((bf16[4,64,2048]{2,1,0:T(8,128)(2,1)}), bf16[4,64,2048]{2,1,0:T(8,128)(2,1)}, u32[]{:S(2)}, u32[]{:S(2)}) async-start(bf16[4,64,2048]{2,1,0:T(8,128)(2,1)} %bitcast.6), calls=%async_computation.1 | async-start | bytes 2097152 | tf_op jit(solution)/shard_map/all_to_all | solution.py:124
  35.4 1.4 scatter_custom_fusion
  37.0 24.3 %all-to-all-done.1 = bf16[4,64,2048]{2,1,0:T(8,128)(2,1)} async-done(((bf16[4,64,2048]{2,1,0:T(8,128)(2,1)}), bf16[4,64,2048]{2,1,0:T(8,128)(2,1)}, u32[]{:S(2)}, u32[]{:S(2)}) %all-to-all-start.1) | async-done | bytes 1048608 | tf_op jit(solution)/shard_map/all_to_all | solution.py:124
  61.2 1.5 convert_reduce_fusion
  62.7 0.2 multiply_reduce_fusion.1
  62.9 0.1 multiply_convert_fusion.1
  63.0 3.3 %gather_fusion = bf16[512,2048]{1,0:T(8,128)(2,1)} fusion(bf16[64,2048]{1,0:T(8,128)(2,1)S(1)} %multiply_convert_fusion.1, s32[1024]{0:T(1024)S(1)} %pad_clamp_fusion.2), kind=kCustom, calls=%fused_computation | custom fusion | bytes 4196352 | tf_op jit(solution)/shard_map/gather | solution.py:148
  66.3 1.8 bitcast_select_fusion
  68.1 64.1 %all_to_all.31 = bf16[64,8,2048]{2,1,0:T(8,128)(2,1)} all-to-all(bf16[64,8,2048]{2,1,0:T(8,128)(2,1)S(1)} %bitcast_select_fusion), channel_id=1, replica_groups=mesh['expert'=64,'cuts'=4] {'expert'}, dimensions={0} | all-to-all | bytes 4194304 | tf_op jit(solution)/shard_map/all_to_all | solution.py:151
  132.2 8.1 %fusion.7 = f32[512,4,352]{0,2,1:T(8,128)} fusion(bf16[4,2048,352]{1,2,0:T(8,128)(2,1)} %all-gather.6.cloned.1.call-done, bf16[64,8,2048]{2,1,0:T(8,128)(2,1)} %all_to_all.31), kind=kOutput, calls=%fused_computation.15 | convolution fusion | flops 2952790016 | bytes 10747904 | tf_op jit(solution)/shard_map/rd,cdf->rcf/dot_general | solution.py:154
  140.3 14.6 %all-gather.4.cloned.1.call-done = bf16[4,2048,352]{1,2,0:T(8,128)(2,1)} async-done(((bf16[1,2048,352]{1,2,0:T(8,128)(2,1)}), bf16[4,2048,352]{1,2,0:T(8,128)(2,1)}) %all-gather.4.cloned.1.call-update) | async-done | bytes 5767184 | tf_op jit(solution)/shard_map/all_gather | solution.py:120
  154.9 66.3 %all-gather.8.cloned.1.call-done = bf16[4,352,2048]{2,1,0:T(8,128)(2,1)} async-done(((bf16[1,352,2048]{2,1,0:T(8,128)(2,1)}), bf16[4,352,2048]{2,1,0:T(8,128)(2,1)}) %all-gather.8.cloned.1.call-update) | async-done | bytes 5767184 | tf_op jit(solution)/shard_map/all_gather | solution.py:122
  221.2 14.1 %fusion = bf16[64,8,2048]{2,1,0:T(8,128)(2,1)} fusion(bf16[4,352,2048]{2,1,0:T(8,128)(2,1)} %all-gather.8.cloned.1.call-done, f32[512,4,352]{0,2,1:T(8,128)} %fusion.7, bf16[4,2048,352]{1,2,0:T(8,128)(2,1)} %all-gather.4.cloned.1.call-done, bf16[64,8,2048]{2,1,0:T(8,128)(2,1)} %all_to_all.31), kind=kOutput, calls=%fused_computation.7 | convolution fusion | flops 5910953984 | bytes 18612224 | tf_op jit(solution)/shard_map/rcf,cfd->rd/dot_general | solution.py:156
  235.3 11.2 %all-to-all-start.3 = ((bf16[64,8,2048]{2,1,0:T(8,128)(2,1)}), bf16[64,8,2048]{2,1,0:T(8,128)(2,1)}, u32[]{:S(2)}, u32[]{:S(2)}) async-start(bf16[64,8,2048]{2,1,0:T(8,128)(2,1)} %fusion), calls=%async_computation.3 | async-start | bytes 4194304 | tf_op jit(solution)/shard_map/all_to_all | solution.py:157
  246.5 0.6 gather_fusion.2
  247.1 0.6 gather_fusion.3
  247.9 0.6 pad_maximum_fusion
  248.5 47.6 %all-to-all-done.3 = bf16[64,8,2048]{2,1,0:T(8,128)(2,1)} async-done(((bf16[64,8,2048]{2,1,0:T(8,128)(2,1)}), bf16[64,8,2048]{2,1,0:T(8,128)(2,1)}, u32[]{:S(2)}, u32[]{:S(2)}) %all-to-all-start.3) | async-done | bytes 2097184 | tf_op jit(solution)/shard_map/all_to_all | solution.py:157
  296.1 5.2 %gather_fusion.1 = bf16[256,2048]{1,0:T(8,128)(2,1)} fusion(bf16[512,2048]{1,0:T(8,128)(2,1)} %bitcast.16, s32[1024]{0:T(1024)S(1)} %pad_clamp_fusion.1), kind=kCustom, calls=%fused_computation.1 | custom fusion | bytes 2098176 | tf_op jit(solution)/shard_map/gather | solution.py:164
  301.3 2.7 reshape.198
  304.0 3.2 %multiply_reduce_fusion = f32[64,2048]{1,0:T(8,128)S(1)} fusion(f32[64,4,2048]{2,1,0:T(4,128)} %reshape.198, f32[64,4]{1,0:T(8,128)S(1)} %copy.53), kind=kLoop, calls=%fused_computation.20 | loop fusion | flops 917504 | bytes 2622464 | tf_op jit(solution)/shard_map/reduce_sum | solution.py:165
  307.2 0.8 add_convert_fusion
  (53 shorter events, 1.2 us)
Async XLA Ops:
  7.2 4.9 %copy-start = (bf16[512,2048]{1,0:T(8,128)(2,1)S(1)}, bf16[512,2048]{1,0:T(8,128)(2,1)}, u32[]{:S(2)}) copy-start(bf16[512,2048]{1,0:T(8,128)(2,1)} %param.20) | copy-start | bytes 6291460
  7.2 2.9 copy-start.10
  7.2 125.0 %all-gather.6.cloned.1.call-start = ((), (), s32[]{:S(2)}) async-start(), calls=%async_computation.5 | async-start | bytes 7208960 | tf_op jit(solution)/shard_map/all_gather | solution.py:121
  7.9 4.2 %copy-start.2 = (bf16[64,2048]{1,0:T(8,128)(2,1)S(1)}, bf16[64,2048]{1,0:T(8,128)(2,1)}, u32[]{:S(2)}) copy-start(bf16[64,2048]{1,0:T(8,128)(2,1)} %param.17) | copy-start | bytes 786436
  7.9 147.0 %all-gather.4.cloned.1.call-start = ((), (), s32[]{:S(2)}) async-start(), calls=%async_computation.4 | async-start | bytes 7208960 | tf_op jit(solution)/shard_map/all_gather | solution.py:120
  8.7 212.5 %all-gather.8.cloned.1.call-start = ((), (), s32[]{:S(2)}) async-start(), calls=%async_computation.6 | async-start | bytes 7208960 | tf_op jit(solution)/shard_map/all_gather | solution.py:122
  12.1 1.0 copy-start.3
  13.0 1.1 copy-start.4
  13.3 1.6 copy-start.9
  15.8 6.1 %copy-start.7 = (s32[256,4]{0,1:T(4,128)S(1)}, s32[256,4]{0,1:T(4,128)}, u32[]{:S(2)}) copy-start(s32[256,4]{0,1:T(4,128)} %param.29) | copy-start | bytes 12292
  16.9 10.5 %all-to-all-start = ((bf16[64,4,512]{2,0,1:T(8,128)(2,1)}), bf16[64,4,512]{2,0,1:T(8,128)(2,1)S(1)}, u32[]{:S(2)}, u32[]{:S(2)}) async-start(bf16[64,4,512]{2,0,1:T(8,128)(2,1)} %copy.52), calls=%async_computation | async-start | bytes 524288 | tf_op jit(solution)/shard_map/all_to_all | solution.py:119
  30.8 31.9 %copy-start.1 = (bf16[64,2048]{1,0:T(8,128)(2,1)S(1)}, bf16[64,2048]{1,0:T(8,128)(2,1)}, u32[]{:S(2)}) copy-start(bf16[64,2048]{1,0:T(8,128)(2,1)} %param.26) | copy-start | bytes 786436
  30.8 32.1 %copy-start.6 = (f32[2048]{0:T(1024)S(1)}, f32[2048]{0:T(1024)}, u32[]{:S(2)}) copy-start(f32[2048]{0:T(1024)} %param.27) | copy-start | bytes 24580
  30.8 30.4 %all-to-all-start.1 = ((bf16[4,64,2048]{2,1,0:T(8,128)(2,1)}), bf16[4,64,2048]{2,1,0:T(8,128)(2,1)}, u32[]{:S(2)}, u32[]{:S(2)}) async-start(bf16[4,64,2048]{2,1,0:T(8,128)(2,1)} %bitcast.6), calls=%async_computation.1 | async-start | bytes 2097152 | tf_op jit(solution)/shard_map/all_to_all | solution.py:124
  235.3 11.2 %copy-start.11 = (s32[1,8]{1,0:T(1,128)S(1)}, s32[1,8]{1,0:T(1,128)}, u32[]{:S(2)}) copy-start(s32[1,8]{1,0:T(1,128)} %param.25) | copy-start | bytes 100
  235.3 11.8 %copy-start.5 = (bf16[64,2048]{1,0:T(8,128)(2,1)S(1)}, bf16[64,2048]{1,0:T(8,128)(2,1)}, u32[]{:S(2)}) copy-start(bf16[64,2048]{1,0:T(8,128)(2,1)} %param.19) | copy-start | bytes 786436
  235.3 12.4 %copy-start.8 = (f32[256,4]{0,1:T(4,128)S(1)}, f32[256,4]{0,1:T(4,128)}, u32[]{:S(2)}) copy-start(f32[256,4]{0,1:T(4,128)} %param.30) | copy-start | bytes 12292
  235.3 60.8 %all-to-all-start.3 = ((bf16[64,8,2048]{2,1,0:T(8,128)(2,1)}), bf16[64,8,2048]{2,1,0:T(8,128)(2,1)}, u32[]{:S(2)}, u32[]{:S(2)}) async-start(bf16[64,8,2048]{2,1,0:T(8,128)(2,1)} %fusion), calls=%async_computation.3 | async-start | bytes 4194304 | tf_op jit(solution)/shard_map/all_to_all | solution.py:157
Sparse Core Ops, SparseCore 0:
  9.8 78.7 all-gather.5
  90.4 64.4 all-gather.3
  156.7 64.4 all-gather.7

commit v4 on v3

--- a/solution.py
+++ b/solution.py
@@ -119,7 +119,11 @@
     head_group = lax.all_to_all(attended, "cuts", split_axis=1, concat_axis=0, tiled=True)
     gate_full = lax.all_gather(w_gate[0], "cuts", axis=0)
     up_full = lax.all_gather(w_up[0], "cuts", axis=0)
-    down_full = lax.all_gather(w_down[0], "cuts", axis=0)
+    cut_count = lax.axis_size("cuts")
+    down_parts = [w_down[0]] + [
+        lax.ppermute(w_down[0], "cuts", [(i, (i + shift) % cut_count) for i in range(cut_count)])
+        for shift in range(1, cut_count)
+    ]
     projected = jnp.dot(head_group, out_weight, preferred_element_type=jnp.float32)
     partials = lax.all_to_all(
         projected.astype(jnp.bfloat16).reshape(lax.axis_size("cuts"), tok_rows, width),
@@ -153,7 +157,12 @@
     gate = jnp.einsum("rd,cdf->rcf", rows, gate_full, preferred_element_type=jnp.float32)
     upper = jnp.einsum("rd,cdf->rcf", rows, up_full, preferred_element_type=jnp.float32)
     hidden = (jax.nn.silu(gate) * upper).astype(jnp.bfloat16)
-    product = jnp.einsum("rcf,cfd->rd", hidden, down_full, preferred_element_type=jnp.float32)
+    product = None
+    for shift, down_part in enumerate(down_parts):
+        owner = (place - shift) % cut_count
+        slice_hidden = lax.dynamic_index_in_dim(hidden, owner, axis=1, keepdims=False)
+        term = jnp.dot(slice_hidden, down_part, preferred_element_type=jnp.float32)
+        product = term if product is None else product + term
     returned = lax.all_to_all(
         product.astype(jnp.bfloat16).reshape(experts_all, capacity, width),
         "expert",

time: 316 us -> 297 us (0.940)
  blocking collectives: 64.1 us -> 0 us
  waiting for transfers between devices: 159 us -> 180 us
  starting transfers between devices: 20.7 us -> 37.8 us
  matrix products: 29.1 us -> 34.2 us
    all_gather x1 -> x0, waiting for transfers between devices: 66.3 us -> none  [on_device(): down_full = lax.all_gather(w_down[0], 'cuts', axis=0)]
    all_to_all x1 -> x0, blocking collectives: 64.1 us -> none  [on_device(): lax.all_to_all(outgoing, 'expert', split_axis=0, concat_axis=0, tiled=True)]
    all_to_all x0 -> x1, waiting for transfers between devices: none -> 46.8 us  [on_device(): lax.all_to_all(outgoing, 'expert', split_axis=0, concat_axis=0, tiled=True)]
    all_gather x1, waiting for transfers between devices: 14.6 us -> 55.6 us  [on_device(): gate_full = lax.all_gather(w_gate[0], 'cuts', axis=0)]
    all_to_all x0 -> x1, starting transfers between devices: none -> 14.6 us  [on_device(): lax.all_to_all(outgoing, 'expert', split_axis=0, concat_axis=0, tiled=True)]
    dot_general x1 -> x5, matrix products: 14.1 us -> 18.9 us  [the longest x4 11 us: on_device(): term = jnp.dot(slice_hidden, down_part, preferred_element_type=jnp.float32)]
  transfers between devices with their start and end apart: 6 -> 9, of which waited for: 5 -> 5; matrix products, arithmetic and copies ran while one was open for 9% -> 15% of each run, Pallas kernels for 0% -> 0%
where the time goes in v4:
time: 297 us; the launch traced here: 295 us
  waiting for transfers between devices  180 us (61%)
  starting transfers between devices  37.8 us (13%)
  matrix products  34.2 us (12%)
  local copies, waits for them, and re-layouts  16.5 us (6%)
  between operations  15.8 us (5%)
  other arithmetic  11.3 us (4%)
    all_gather x1, waiting for transfers between devices, on_device(): gate_full = lax.all_gather(w_gate[0], 'cuts', axis=0)  55.6 us
    all_to_all x1, waiting for transfers between devices, on_device(): lax.all_to_all(product.astype(jnp.bfloat16).reshape(experts_all, capacity...  47.6 us
    all_to_all x1, waiting for transfers between devices, on_device(): lax.all_to_all(outgoing, 'expert', split_axis=0, concat_axis=0, tiled=True)  46.8 us
    all_to_all x1, waiting for transfers between devices, on_device(): lax.all_to_all(projected.astype(jnp.bfloat16).reshape(lax.axis_size('cuts...  24.3 us
    all_to_all x1, starting transfers between devices, on_device(): lax.all_to_all(outgoing, 'expert', split_axis=0, concat_axis=0, tiled=True)  14.6 us
    dot_general x4, matrix products, on_device(): term = jnp.dot(slice_hidden, down_part, preferred_element_type=jnp.float32)  11 us
    all_to_all x1, starting transfers between devices, on_device(): lax.all_to_all(product.astype(jnp.bfloat16).reshape(experts_all, capacity...  10.9 us
    dot_general x1, matrix products, on_device(): jnp.einsum('rd,cdf->rcf', rows, up_full, preferred_element_type=jnp.float32)  8.23 us
  transfers between devices with their start and end apart: 9, of which 5 were waited for; matrix products, arithmetic and copies ran while one was open for 15% of the time, Pallas kernels for 0%

profile of v4, /device:TPU:1, one launch (start us, length us, event | category | flops | bytes accessed | tf_op | source)
XLA Modules:
  0.0 295.3 jit_solution(9643075560985131217)
XLA Ops:
  7.2 0.7 all-gather.5.cloned.1.call-update
  8.0 0.7 all-gather.3.cloned.1.call-update
  9.4 0.2 convolution_minimum_fusion.6
  9.6 0.2 convolution_minimum_fusion.5
  9.7 0.2 convolution_minimum_fusion.4
  10.2 0.2 convolution_minimum_fusion.1
  11.1 0.2 fusion.26
  11.4 0.9 fusion.13
  12.3 0.3 fusion.74
  12.6 0.6 fusion.14
  13.4 0.3 fusion.47
  13.7 0.5 copy-done.10
  14.2 0.9 fusion.22
  15.1 0.2 copy.51
  15.4 0.7 copy.52
  16.2 5.0 %all-to-all-start = ((bf16[64,4,512]{2,0,1:T(8,128)(2,1)}), bf16[64,4,512]{2,0,1:T(8,128)(2,1)S(1)}, u32[]{:S(2)}, u32[]{:S(2)}) async-start(bf16[64,4,512]{2,0,1:T(8,128)(2,1)} %copy.52), calls=%async_computation | async-start | bytes 524288 | tf_op jit(solution)/shard_map/all_to_all | solution.py:119
  21.6 0.6 reduce-window.6
  22.2 0.2 slice_reduce_fusion
  22.5 4.2 %all-to-all-done = bf16[64,4,512]{2,0,1:T(8,128)(2,1)S(1)} async-done(((bf16[64,4,512]{2,0,1:T(8,128)(2,1)}), bf16[64,4,512]{2,0,1:T(8,128)(2,1)S(1)}, u32[]{:S(2)}, u32[]{:S(2)}) %all-to-all-start) | async-done | bytes 262176 | tf_op jit(solution)/shard_map/all_to_all | solution.py:119
  26.7 3.6 %convolution_convert_fusion = bf16[256,2048]{1,0:T(8,128)(2,1)} fusion(bf16[256,512]{1,0:T(8,128)(2,1)S(1)} %bitcast.143, bf16[512,2048]{1,0:T(8,128)(2,1)} %param.28), kind=kOutput, calls=%fused_computation.7 | convolution fusion | flops 537395200 | bytes 3407872 | tf_op jit(solution)/shard_map/dot_general | solution.py:127
  30.3 4.4 %all-to-all-start.1 = ((bf16[4,64,2048]{2,1,0:T(8,128)(2,1)}), bf16[4,64,2048]{2,1,0:T(8,128)(2,1)}, u32[]{:S(2)}, u32[]{:S(2)}) async-start(bf16[4,64,2048]{2,1,0:T(8,128)(2,1)} %bitcast.6), calls=%async_computation.1 | async-start | bytes 2097152 | tf_op jit(solution)/shard_map/all_to_all | solution.py:128
  34.9 1.4 scatter_custom_fusion
  36.4 24.3 %all-to-all-done.1 = bf16[4,64,2048]{2,1,0:T(8,128)(2,1)} async-done(((bf16[4,64,2048]{2,1,0:T(8,128)(2,1)}), bf16[4,64,2048]{2,1,0:T(8,128)(2,1)}, u32[]{:S(2)}, u32[]{:S(2)}) %all-to-all-start.1) | async-done | bytes 1048608 | tf_op jit(solution)/shard_map/all_to_all | solution.py:128
  60.7 1.5 convert_reduce_fusion
  62.2 0.2 multiply_reduce_fusion.1
  62.5 3.3 %gather_fusion = bf16[512,2048]{1,0:T(8,128)(2,1)} fusion(bf16[64,2048]{1,0:T(8,128)(2,1)S(1)} %multiply_convert_fusion.1, s32[1024]{0:T(1024)S(1)} %pad_clamp_fusion.2), kind=kCustom, calls=%fused_computation | custom fusion | bytes 4196352 | tf_op jit(solution)/shard_map/gather | solution.py:152
  65.8 3.3 %bitcast_select_fusion = bf16[64,8,2048]{2,1,0:T(8,128)(2,1)} fusion(bf16[512,2048]{1,0:T(8,128)(2,1)} %gather_fusion, pred[64,8]{1,0:T(8,128)(4,1)S(1)} %broadcast_in_dim.88), kind=kLoop, calls=%fused_computation.19 | loop fusion | flops 1048576 | bytes 4194816 | tf_op jit(solution)/shard_map/jit(_where)/select_n | solution.py:151
  69.0 14.6 %all-to-all-start.2 = ((bf16[64,8,2048]{2,1,0:T(8,128)(2,1)}), bf16[64,8,2048]{2,1,0:T(8,128)(2,1)}, u32[]{:S(2)}, u32[]{:S(2)}) async-start(bf16[64,8,2048]{2,1,0:T(8,128)(2,1)} %bitcast_select_fusion), calls=%async_computation.2 | async-start | bytes 4194304 | tf_op jit(solution)/shard_map/all_to_all | solution.py:155
  83.6 0.4 collective-permute-start
  84.0 1.8 collective-permute-start.1
  85.8 0.7 collective-permute-start.2
  86.5 46.8 %all-to-all-done.2 = bf16[64,8,2048]{2,1,0:T(8,128)(2,1)} async-done(((bf16[64,8,2048]{2,1,0:T(8,128)(2,1)}), bf16[64,8,2048]{2,1,0:T(8,128)(2,1)}, u32[]{:S(2)}, u32[]{:S(2)}) %all-to-all-start.2) | async-done | bytes 2097184 | tf_op jit(solution)/shard_map/all_to_all | solution.py:155
  133.2 8.2 %fusion.7 = f32[512,4,352]{0,2,1:T(8,128)} fusion(bf16[4,2048,352]{1,2,0:T(8,128)(2,1)} %all-gather.5.cloned.1.call-done, bf16[64,8,2048]{2,1,0:T(8,128)(2,1)} %all-to-all-done.2), kind=kOutput, calls=%fused_computation.15 | convolution fusion | flops 2952790016 | bytes 10747904 | tf_op jit(solution)/shard_map/rd,cdf->rcf/dot_general | solution.py:158
  141.5 55.6 %all-gather.3.cloned.1.call-done = bf16[4,2048,352]{1,2,0:T(8,128)(2,1)} async-done(((bf16[1,2048,352]{1,2,0:T(8,128)(2,1)}), bf16[4,2048,352]{1,2,0:T(8,128)(2,1)}) %all-gather.3.cloned.1.call-update) | async-done | bytes 5767184 | tf_op jit(solution)/shard_map/all_gather | solution.py:120
  197.0 7.9 %multiply_convert_fusion = bf16[512,4,352]{0,2,1:T(8,128)(2,1)S(1)} fusion(f32[512,4,352]{0,2,1:T(8,128)} %fusion.7, bf16[4,2048,352]{1,2,0:T(8,128)(2,1)} %all-gather.3.cloned.1.call-done, bf16[64,8,2048]{2,1,0:T(8,128)(2,1)} %all-to-all-done.2), kind=kOutput, calls=%fused_computation.6 | convolution fusion | flops 2957115392 | bytes 12189696 | tf_op jit(solution)/shard_map/rd,cdf->rcf/dot_general | solution.py:157
  205.0 1.3 fusion.41
  206.3 2.7 fusion.39
  208.9 2.7 fusion.37
  211.6 4.4 %fusion = bf16[64,8,2048]{2,1,0:T(8,128)(2,1)} fusion(f32[512,2048]{1,0:T(8,128)S(1)} %fusion.37, f32[512,2048]{1,0:T(8,128)S(1)} %fusion.41, f32[512,2048]{1,0:T(8,128)S(1)} %fusion.39, bf16[352,2048]{1,0:T(8,128)(2,1)} %collective-permute-done.2, bf16[512,4,352]{0,2,1:T(8,128)(2,1)S(1)} %multiply_convert_fusion, s32[]{:T(128)S(6)} %select_n.92), kind=kOutput, calls=%fused_computation.8 | convolution fusion | flops 742391808 | bytes 16482308 | tf_op jit(solution)/shard_map/dot_general | solution.py:164
  216.0 10.9 %all-to-all-start.3 = ((bf16[64,8,2048]{2,1,0:T(8,128)(2,1)}), bf16[64,8,2048]{2,1,0:T(8,128)(2,1)}, u32[]{:S(2)}, u32[]{:S(2)}) async-start(bf16[64,8,2048]{2,1,0:T(8,128)(2,1)} %fusion), calls=%async_computation.3 | async-start | bytes 4194304 | tf_op jit(solution)/shard_map/all_to_all | solution.py:166
  226.9 0.6 gather_fusion.2
  227.5 0.6 gather_fusion.3
  228.3 0.6 pad_maximum_fusion
  228.9 47.6 %all-to-all-done.3 = bf16[64,8,2048]{2,1,0:T(8,128)(2,1)} async-done(((bf16[64,8,2048]{2,1,0:T(8,128)(2,1)}), bf16[64,8,2048]{2,1,0:T(8,128)(2,1)}, u32[]{:S(2)}, u32[]{:S(2)}) %all-to-all-start.3) | async-done | bytes 2097184 | tf_op jit(solution)/shard_map/all_to_all | solution.py:166
  276.5 5.2 %gather_fusion.1 = bf16[256,2048]{1,0:T(8,128)(2,1)} fusion(bf16[512,2048]{1,0:T(8,128)(2,1)} %bitcast.20, s32[1024]{0:T(1024)S(1)} %pad_clamp_fusion.1), kind=kCustom, calls=%fused_computation.1 | custom fusion | bytes 2098176 | tf_op jit(solution)/shard_map/gather | solution.py:173
  281.7 2.7 reshape.198
  284.4 3.2 %multiply_reduce_fusion = f32[64,2048]{1,0:T(8,128)S(1)} fusion(f32[64,4,2048]{2,1,0:T(4,128)} %reshape.198, f32[64,4]{1,0:T(8,128)S(1)} %copy.53), kind=kLoop, calls=%fused_computation.20 | loop fusion | flops 917504 | bytes 2622464 | tf_op jit(solution)/shard_map/reduce_sum | solution.py:174
  287.6 0.8 add_convert_fusion.1
  (63 shorter events, 2.0 us)
Async XLA Ops:
  7.2 4.2 %copy-start = (bf16[512,2048]{1,0:T(8,128)(2,1)S(1)}, bf16[512,2048]{1,0:T(8,128)(2,1)}, u32[]{:S(2)}) copy-start(bf16[512,2048]{1,0:T(8,128)(2,1)} %param.20) | copy-start | bytes 6291460
  7.2 2.2 copy-start.11
  7.2 4.2 %copy-start.3 = (bf16[64,2048]{1,0:T(8,128)(2,1)S(1)}, bf16[64,2048]{1,0:T(8,128)(2,1)}, u32[]{:S(2)}) copy-start(bf16[64,2048]{1,0:T(8,128)(2,1)} %param.17) | copy-start | bytes 786436
  7.2 126.0 %all-gather.5.cloned.1.call-start = ((), (), s32[]{:S(2)}) async-start(), calls=%async_computation.5 | async-start | bytes 7208960 | tf_op jit(solution)/shard_map/all_gather | solution.py:121
  7.9 189.1 %all-gather.3.cloned.1.call-start = ((), (), s32[]{:S(2)}) async-start(), calls=%async_computation.4 | async-start | bytes 7208960 | tf_op jit(solution)/shard_map/all_gather | solution.py:120
  11.4 1.0 copy-start.4
  12.3 1.1 copy-start.5
  12.6 1.6 copy-start.10
  15.1 6.1 %copy-start.8 = (s32[256,4]{0,1:T(4,128)S(1)}, s32[256,4]{0,1:T(4,128)}, u32[]{:S(2)}) copy-start(s32[256,4]{0,1:T(4,128)} %param.29) | copy-start | bytes 12292
  16.2 10.5 %all-to-all-start = ((bf16[64,4,512]{2,0,1:T(8,128)(2,1)}), bf16[64,4,512]{2,0,1:T(8,128)(2,1)S(1)}, u32[]{:S(2)}, u32[]{:S(2)}) async-start(bf16[64,4,512]{2,0,1:T(8,128)(2,1)} %copy.52), calls=%async_computation | async-start | bytes 524288 | tf_op jit(solution)/shard_map/all_to_all | solution.py:119
  30.3 31.9 %copy-start.1 = (bf16[64,2048]{1,0:T(8,128)(2,1)S(1)}, bf16[64,2048]{1,0:T(8,128)(2,1)}, u32[]{:S(2)}) copy-start(bf16[64,2048]{1,0:T(8,128)(2,1)} %param.26) | copy-start | bytes 786436
  30.3 32.1 %copy-start.7 = (f32[2048]{0:T(1024)S(1)}, f32[2048]{0:T(1024)}, u32[]{:S(2)}) copy-start(f32[2048]{0:T(1024)} %param.27) | copy-start | bytes 24580
  30.3 30.4 %all-to-all-start.1 = ((bf16[4,64,2048]{2,1,0:T(8,128)(2,1)}), bf16[4,64,2048]{2,1,0:T(8,128)(2,1)}, u32[]{:S(2)}, u32[]{:S(2)}) async-start(bf16[4,64,2048]{2,1,0:T(8,128)(2,1)} %bitcast.6), calls=%async_computation.1 | async-start | bytes 2097152 | tf_op jit(solution)/shard_map/all_to_all | solution.py:128
  69.0 64.2 %all-to-all-start.2 = ((bf16[64,8,2048]{2,1,0:T(8,128)(2,1)}), bf16[64,8,2048]{2,1,0:T(8,128)(2,1)}, u32[]{:S(2)}, u32[]{:S(2)}) async-start(bf16[64,8,2048]{2,1,0:T(8,128)(2,1)} %bitcast_select_fusion), calls=%async_computation.2 | async-start | bytes 4194304 | tf_op jit(solution)/shard_map/all_to_all | solution.py:155
  83.6 122.6 %collective-permute-start = (bf16[352,2048]{1,0:T(8,128)(2,1)}, bf16[352,2048]{1,0:T(8,128)(2,1)}, u32[]{:S(2)}, u32[]{:S(2)}) collective-permute-start(bf16[352,2048]{1,0:T(8,128)(2,1)} %bitcast.140), channel_id=1, source_target_pairs={{0,1},{1,2},{2,3},{3,0},{4,5},{5,6},{6,7},{7,4},{8,9},{9,10},{10,1... | collective-permute-start | bytes 4325384 | tf_op jit(solution)/shard_map/ppermute | solution.py:124
  84.0 124.9 %collective-permute-start.1 = (bf16[352,2048]{1,0:T(8,128)(2,1)}, bf16[352,2048]{1,0:T(8,128)(2,1)}, u32[]{:S(2)}, u32[]{:S(2)}) collective-permute-start(bf16[352,2048]{1,0:T(8,128)(2,1)} %bitcast.141), channel_id=1, source_target_pairs={{0,2},{1,3},{2,0},{3,1},{4,6},{5,7},{6,4},{7,5},{8,10},{9,11},{10,... | collective-permute-start | bytes 4325384 | tf_op jit(solution)/shard_map/ppermute | solution.py:124
  85.8 125.8 %collective-permute-start.2 = (bf16[352,2048]{1,0:T(8,128)(2,1)}, bf16[352,2048]{1,0:T(8,128)(2,1)}, u32[]{:S(2)}, u32[]{:S(2)}) collective-permute-start(bf16[352,2048]{1,0:T(8,128)(2,1)} %bitcast.142), channel_id=1, source_target_pairs={{0,3},{1,0},{2,1},{3,2},{4,7},{5,4},{6,5},{7,6},{8,11},{9,8},{10,9... | collective-permute-start | bytes 4325384 | tf_op jit(solution)/shard_map/ppermute | solution.py:124
  197.0 7.9 %copy-start.2 = (bf16[1,352,2048]{2,1,0:T(8,128)(2,1)S(1)}, bf16[1,352,2048]{2,1,0:T(8,128)(2,1)}, u32[]{:S(2)}) copy-start(bf16[1,352,2048]{2,1,0:T(8,128)(2,1)} %param.33) | copy-start | bytes 4325380
  216.0 10.9 %copy-start.12 = (s32[1,8]{1,0:T(1,128)S(1)}, s32[1,8]{1,0:T(1,128)}, u32[]{:S(2)}) copy-start(s32[1,8]{1,0:T(1,128)} %param.25) | copy-start | bytes 100
  216.0 11.5 %copy-start.6 = (bf16[64,2048]{1,0:T(8,128)(2,1)S(1)}, bf16[64,2048]{1,0:T(8,128)(2,1)}, u32[]{:S(2)}) copy-start(bf16[64,2048]{1,0:T(8,128)(2,1)} %param.19) | copy-start | bytes 786436
  216.0 12.1 %copy-start.9 = (f32[256,4]{0,1:T(4,128)S(1)}, f32[256,4]{0,1:T(4,128)}, u32[]{:S(2)}) copy-start(f32[256,4]{0,1:T(4,128)} %param.30) | copy-start | bytes 12292
  216.0 60.5 %all-to-all-start.3 = ((bf16[64,8,2048]{2,1,0:T(8,128)(2,1)}), bf16[64,8,2048]{2,1,0:T(8,128)(2,1)}, u32[]{:S(2)}, u32[]{:S(2)}) async-start(bf16[64,8,2048]{2,1,0:T(8,128)(2,1)} %fusion), calls=%async_computation.3 | async-start | bytes 4194304 | tf_op jit(solution)/shard_map/all_to_all | solution.py:166
Sparse Core Ops, SparseCore 0:
  9.8 78.9 all-gather.4
  90.6 106.3 all-gather.2

commit v5 on v4

--- a/solution.py
+++ b/solution.py
@@ -120,10 +120,13 @@
     gate_full = lax.all_gather(w_gate[0], "cuts", axis=0)
     up_full = lax.all_gather(w_up[0], "cuts", axis=0)
     cut_count = lax.axis_size("cuts")
-    down_parts = [w_down[0]] + [
-        lax.ppermute(w_down[0], "cuts", [(i, (i + shift) % cut_count) for i in range(cut_count)])
+    half = width // 2
+    down_early = w_down[0][:, :half]
+    down_parts = [down_early] + [
+        lax.ppermute(down_early, "cuts", [(i, (i + shift) % cut_count) for i in range(cut_count)])
         for shift in range(1, cut_count)
     ]
+    down_late = lax.all_gather(w_down[0][:, half:], "cuts", axis=0)
     projected = jnp.dot(head_group, out_weight, preferred_element_type=jnp.float32)
     partials = lax.all_to_all(
         projected.astype(jnp.bfloat16).reshape(lax.axis_size("cuts"), tok_rows, width),
@@ -163,15 +166,26 @@
         slice_hidden = lax.dynamic_index_in_dim(hidden, owner, axis=1, keepdims=False)
         term = jnp.dot(slice_hidden, down_part, preferred_element_type=jnp.float32)
         product = term if product is None else product + term
-    returned = lax.all_to_all(
-        product.astype(jnp.bfloat16).reshape(experts_all, capacity, width),
+    returned_early = lax.all_to_all(
+        product.astype(jnp.bfloat16).reshape(experts_all, capacity, half),
         "expert",
         split_axis=0,
         concat_axis=0,
         tiled=True,
     )
-    picked = returned.reshape(-1, width)[dest].reshape(tok_rows, TOPK, width)
-    moe = jnp.sum(own_gains[:, :, None] * picked.astype(jnp.float32), axis=1)
+    product_late = jnp.einsum("rcf,cfd->rd", hidden, down_late, preferred_element_type=jnp.float32)
+    returned_late = lax.all_to_all(
+        product_late.astype(jnp.bfloat16).reshape(experts_all, capacity, half),
+        "expert",
+        split_axis=0,
+        concat_axis=0,
+        tiled=True,
+    )
+    moe_parts = []
+    for returned in (returned_early, returned_late):
+        picked = returned.reshape(-1, half)[dest].reshape(tok_rows, TOPK, half)
+        moe_parts.append(jnp.sum(own_gains[:, :, None] * picked.astype(jnp.float32), axis=1))
+    moe = jnp.concatenate(moe_parts, axis=1)
     layer_out = (stream + moe).astype(jnp.bfloat16)
     picks = (jnp.arange(requests, dtype=jnp.int32)[:, None] * TREE + accepted_path).reshape(-1)
     accepted_kv = jnp.concatenate([new_keys[picks], new_values[picks]], axis=1)

time: 297 us -> 271 us (0.912)
  waiting for transfers between devices: 180 us -> 146 us
  starting transfers between devices: 37.8 us -> 43.2 us
  local copies, waits for them, and re-layouts: 16.5 us -> 20.1 us
    all_to_all x1, waiting for transfers between devices: 47.6 us -> 7.01 us  [on_device(): lax.all_to_all(product.astype(jnp.bfloat16).reshape(experts_all, capacity...]
    all_gather x1, waiting for transfers between devices: 55.6 us -> 26.5 us  [on_device(): gate_full = lax.all_gather(w_gate[0], 'cuts', axis=0)]
    all_to_all x0 -> x1, waiting for transfers between devices: none -> 20.7 us  [on_device(): lax.all_to_all(product_late.astype(jnp.bfloat16).reshape(experts_all, cap...]
    all_gather x0 -> x1, waiting for transfers between devices: none -> 16.1 us  [on_device(): down_late = lax.all_gather(w_down[0][:, half:], 'cuts', axis=0)]
    all_to_all x0 -> x1, starting transfers between devices: none -> 6.47 us  [on_device(): lax.all_to_all(product_late.astype(jnp.bfloat16).reshape(experts_all, cap...]
    dot_general x0 -> x1, matrix products: none -> 5.03 us  [on_device(): jnp.einsum('rcf,cfd->rd', hidden, down_late, preferred_element_type=jnp.f...]
    dot_general x4, matrix products: 11 us -> 7.29 us  [on_device(): term = jnp.dot(slice_hidden, down_part, preferred_element_type=jnp.float32)]
  transfers between devices with their start and end apart: 9 -> 11, of which waited for: 5 -> 7; matrix products, arithmetic and copies ran while one was open for 15% -> 21% of each run, Pallas kernels for 0% -> 0%
where the time goes in v5:
time: 271 us; the launch traced here: 270 us
  waiting for transfers between devices  146 us (54%)
  starting transfers between devices  43.2 us (16%)
  matrix products  35.3 us (13%)
  local copies, waits for them, and re-layouts  20.1 us (7%)
  between operations  15.6 us (6%)
  other arithmetic  9.76 us (4%)
    all_to_all x1, waiting for transfers between devices, on_device(): lax.all_to_all(outgoing, 'expert', split_axis=0, concat_axis=0, tiled=True)  45.5 us
    all_gather x1, waiting for transfers between devices, on_device(): gate_full = lax.all_gather(w_gate[0], 'cuts', axis=0)  26.5 us
    all_to_all x1, waiting for transfers between devices, on_device(): lax.all_to_all(projected.astype(jnp.bfloat16).reshape(lax.axis_size('cuts...  24.2 us
    all_to_all x1, waiting for transfers between devices, on_device(): lax.all_to_all(product_late.astype(jnp.bfloat16).reshape(experts_all, cap...  20.7 us
    all_gather x1, waiting for transfers between devices, on_device(): down_late = lax.all_gather(w_down[0][:, half:], 'cuts', axis=0)  16.1 us
    all_to_all x1, starting transfers between devices, on_device(): lax.all_to_all(outgoing, 'expert', split_axis=0, concat_axis=0, tiled=True)  14.8 us
    all_to_all x1, starting transfers between devices, on_device(): lax.all_to_all(product.astype(jnp.bfloat16).reshape(experts_all, capacity...  10.5 us
    dot_general x1, matrix products, on_device(): jnp.einsum('rd,cdf->rcf', rows, up_full, preferred_element_type=jnp.float32)  8.1 us
  transfers between devices with their start and end apart: 11, of which 7 were waited for; matrix products, arithmetic and copies ran while one was open for 21% of the time, Pallas kernels for 0%

profile of v5, /device:TPU:1, one launch (start us, length us, event | category | flops | bytes accessed | tf_op | source)
XLA Modules:
  0.0 269.6 jit_solution(894990186288492605)
XLA Ops:
  7.2 0.7 all-gather.7.cloned.1.call-update
  8.0 0.7 all-gather.5.cloned.1.call-update
  9.4 0.2 convolution_minimum_fusion.6
  11.4 0.9 fusion.12
  12.3 0.3 fusion.77
  12.7 0.6 fusion.13
  13.4 0.3 fusion.49
  13.7 0.7 copy-done.14
  14.3 0.9 fusion.22
  15.5 0.7 copy.52
  16.3 5.0 %all-to-all-start = ((bf16[64,4,512]{2,0,1:T(8,128)(2,1)}), bf16[64,4,512]{2,0,1:T(8,128)(2,1)S(1)}, u32[]{:S(2)}, u32[]{:S(2)}) async-start(bf16[64,4,512]{2,0,1:T(8,128)(2,1)} %copy.52), calls=%async_computation | async-start | bytes 524288 | tf_op jit(solution)/shard_map/all_to_all | solution.py:119
  21.7 0.6 reduce-window.6
  22.6 4.2 %all-to-all-done = bf16[64,4,512]{2,0,1:T(8,128)(2,1)S(1)} async-done(((bf16[64,4,512]{2,0,1:T(8,128)(2,1)}), bf16[64,4,512]{2,0,1:T(8,128)(2,1)S(1)}, u32[]{:S(2)}, u32[]{:S(2)}) %all-to-all-start) | async-done | bytes 262176 | tf_op jit(solution)/shard_map/all_to_all | solution.py:119
  26.8 3.5 %convolution_convert_fusion = bf16[256,2048]{1,0:T(8,128)(2,1)} fusion(bf16[256,512]{1,0:T(8,128)(2,1)S(1)} %bitcast.152, bf16[512,2048]{1,0:T(8,128)(2,1)} %param.28), kind=kOutput, calls=%fused_computation.7 | convolution fusion | flops 537395200 | bytes 3407872 | tf_op jit(solution)/shard_map/dot_general | solution.py:130
  30.3 3.6 %all-to-all-start.1 = ((bf16[4,64,2048]{2,1,0:T(8,128)(2,1)}), bf16[4,64,2048]{2,1,0:T(8,128)(2,1)S(1)}, u32[]{:S(2)}, u32[]{:S(2)}) async-start(bf16[4,64,2048]{2,1,0:T(8,128)(2,1)} %bitcast.149), calls=%async_computation.1 | async-start | bytes 2097152 | tf_op jit(solution)/shard_map/all_to_all | solution.py:131
  34.2 1.4 scatter_custom_fusion
  35.7 24.2 %all-to-all-done.1 = bf16[4,64,2048]{2,1,0:T(8,128)(2,1)S(1)} async-done(((bf16[4,64,2048]{2,1,0:T(8,128)(2,1)}), bf16[4,64,2048]{2,1,0:T(8,128)(2,1)S(1)}, u32[]{:S(2)}, u32[]{:S(2)}) %all-to-all-start.1) | async-done | bytes 1048608 | tf_op jit(solution)/shard_map/all_to_all | solution.py:131
  60.3 0.6 copy-done.1
  61.0 3.4 %gather_fusion = bf16[512,2048]{1,0:T(8,128)(2,1)} fusion(bf16[64,2048]{1,0:T(8,128)(2,1)S(1)} %multiply_convert_fusion.1, s32[1024]{0:T(1024)S(1)} %pad_clamp_fusion.2), kind=kCustom, calls=%fused_computation | custom fusion | bytes 4196352 | tf_op jit(solution)/shard_map/gather | solution.py:155
  64.4 3.1 %bitcast_select_fusion = bf16[64,8,2048]{2,1,0:T(8,128)(2,1)} fusion(bf16[512,2048]{1,0:T(8,128)(2,1)} %gather_fusion, pred[64,8]{1,0:T(8,128)(4,1)S(1)} %broadcast_in_dim.90), kind=kLoop, calls=%fused_computation.19 | loop fusion | flops 1048576 | bytes 4194816 | tf_op jit(solution)/shard_map/jit(_where)/select_n | solution.py:154
  67.5 14.8 %all-to-all-start.2 = ((bf16[64,8,2048]{2,1,0:T(8,128)(2,1)}), bf16[64,8,2048]{2,1,0:T(8,128)(2,1)}, u32[]{:S(2)}, u32[]{:S(2)}) async-start(bf16[64,8,2048]{2,1,0:T(8,128)(2,1)} %bitcast_select_fusion), calls=%async_computation.2 | async-start | bytes 4194304 | tf_op jit(solution)/shard_map/all_to_all | solution.py:158
  82.3 1.2 fusion.76
  83.5 0.3 collective-permute-start
  83.8 1.8 collective-permute-start.1
  85.6 0.6 collective-permute-start.2
  86.3 45.5 %all-to-all-done.2 = bf16[64,8,2048]{2,1,0:T(8,128)(2,1)} async-done(((bf16[64,8,2048]{2,1,0:T(8,128)(2,1)}), bf16[64,8,2048]{2,1,0:T(8,128)(2,1)}, u32[]{:S(2)}, u32[]{:S(2)}) %all-to-all-start.2) | async-done | bytes 2097184 | tf_op jit(solution)/shard_map/all_to_all | solution.py:158
  131.9 8.1 %fusion.6 = f32[512,4,352]{0,2,1:T(8,128)} fusion(bf16[4,2048,352]{1,2,0:T(8,128)(2,1)} %all-gather.7.cloned.1.call-done, bf16[64,8,2048]{2,1,0:T(8,128)(2,1)} %all-to-all-done.2), kind=kOutput, calls=%fused_computation.15 | convolution fusion | flops 2952790016 | bytes 10747904 | tf_op jit(solution)/shard_map/rd,cdf->rcf/dot_general | solution.py:161
  140.0 26.5 %all-gather.5.cloned.1.call-done = bf16[4,2048,352]{1,2,0:T(8,128)(2,1)} async-done(((bf16[1,2048,352]{1,2,0:T(8,128)(2,1)}), bf16[4,2048,352]{1,2,0:T(8,128)(2,1)}) %all-gather.5.cloned.1.call-update) | async-done | bytes 5767184 | tf_op jit(solution)/shard_map/all_gather | solution.py:120
  166.4 7.8 %multiply_convert_fusion = bf16[512,4,352]{0,2,1:T(8,128)(2,1)S(1)} fusion(f32[512,4,352]{0,2,1:T(8,128)} %fusion.6, bf16[4,2048,352]{1,2,0:T(8,128)(2,1)} %all-gather.5.cloned.1.call-done, bf16[64,8,2048]{2,1,0:T(8,128)(2,1)} %all-to-all-done.2), kind=kOutput, calls=%fused_computation.6 | convolution fusion | flops 2957115392 | bytes 12189696 | tf_op jit(solution)/shard_map/rd,cdf->rcf/dot_general | solution.py:160
  174.3 0.7 fusion.43
  175.0 1.8 fusion.41
  176.9 1.8 fusion.39
  178.7 2.9 %fusion.27 = bf16[64,8,1024]{2,1,0:T(8,128)(2,1)} fusion(f32[512,1024]{1,0:T(8,128)S(1)} %fusion.39, f32[512,1024]{1,0:T(8,128)S(1)} %fusion.43, f32[512,1024]{1,0:T(8,128)S(1)} %fusion.41, bf16[352,1024]{1,0:T(8,128)(2,1)} %collective-permute-done.2, bf16[512,4,352]{0,2,1:T(8,128)(2,1)S(1)} %multiply_convert_fusion, s32[]{:T(128)S(6)} %select_n.93), kind=kOutput, calls=%fused_computation.42 | convolution fusion | flops 371195904 | bytes 8421380 | tf_op jit(solution)/shard_map/dot_general | solution.py:167
  181.6 10.5 %all-to-all-start.3 = ((bf16[64,8,1024]{2,1,0:T(8,128)(2,1)}), bf16[64,8,1024]{2,1,0:T(8,128)(2,1)S(1)}, u32[]{:S(2)}, u32[]{:S(2)}) async-start(bf16[64,8,1024]{2,1,0:T(8,128)(2,1)} %fusion.27), calls=%async_computation.3 | async-start | bytes 2097152 | tf_op jit(solution)/shard_map/all_to_all | solution.py:169
  192.1 16.1 %all-gather.9.cloned.1.call-done = bf16[1408,1024]{1,0:T(8,128)(2,1)} async-done(((bf16[352,1024]{1,0:T(8,128)(2,1)}), bf16[1408,1024]{1,0:T(8,128)(2,1)}) %all-gather.9.cloned.1.call-update) | async-done | bytes 2883600 | tf_op jit(solution)/shard_map/all_gather | solution.py:129
  208.2 5.0 %fusion.14 = bf16[64,8,1024]{2,1,0:T(8,128)(2,1)} fusion(bf16[512,4,352]{0,2,1:T(8,128)(2,1)} %copy-done.6, bf16[4,352,1024]{2,1,0:T(8,128)(2,1)} %bitcast.156), kind=kOutput, calls=%fused_computation.27 | convolution fusion | flops 1476919296 | bytes 5373952 | tf_op jit(solution)/shard_map/rcf,cfd->rd/dot_general | solution.py:176
  213.2 7.0 %all-to-all-done.3 = bf16[64,8,1024]{2,1,0:T(8,128)(2,1)S(1)} async-done(((bf16[64,8,1024]{2,1,0:T(8,128)(2,1)}), bf16[64,8,1024]{2,1,0:T(8,128)(2,1)S(1)}, u32[]{:S(2)}, u32[]{:S(2)}) %all-to-all-start.3) | async-done | bytes 1048608 | tf_op jit(solution)/shard_map/all_to_all | solution.py:169
  220.3 6.5 %all-to-all-start.4 = ((bf16[64,8,1024]{2,1,0:T(8,128)(2,1)}), bf16[64,8,1024]{2,1,0:T(8,128)(2,1)}, u32[]{:S(2)}, u32[]{:S(2)}) async-start(bf16[64,8,1024]{2,1,0:T(8,128)(2,1)} %fusion.14), calls=%async_computation.4 | async-start | bytes 2097152 | tf_op jit(solution)/shard_map/all_to_all | solution.py:177
  226.8 0.6 gather_fusion.3
  227.4 1.6 gather_fusion.4
  229.2 0.6 pad_maximum_fusion
  229.8 2.0 gather_fusion.1
  231.8 2.4 reshape.209
  234.1 20.7 %all-to-all-done.4 = bf16[64,8,1024]{2,1,0:T(8,128)(2,1)} async-done(((bf16[64,8,1024]{2,1,0:T(8,128)(2,1)}), bf16[64,8,1024]{2,1,0:T(8,128)(2,1)}, u32[]{:S(2)}, u32[]{:S(2)}) %all-to-all-start.4) | async-done | bytes 1048608 | tf_op jit(solution)/shard_map/all_to_all | solution.py:177
  254.8 2.9 %gather_fusion.2 = bf16[256,1024]{1,0:T(8,128)(2,1)S(1)} fusion(bf16[512,1024]{1,0:T(8,128)(2,1)} %bitcast.24, s32[1024]{0:T(1024)S(1)} %pad_clamp_fusion.1), kind=kCustom, calls=%fused_computation.2 | custom fusion | bytes 1049600 | tf_op jit(solution)/shard_map/gather | solution.py:186
  257.8 1.3 reshape.210
  259.1 3.1 %multiply_reduce_fusion.1 = (f32[64,1024]{1,0:T(8,128)S(1)}, f32[64,1024]{1,0:T(8,128)S(1)}) fusion(f32[64,4,1024]{2,1,0:T(4,128)} %reshape.209, f32[64,4]{1,0:T(8,128)S(1)} %copy.53, f32[64,4,1024]{2,1,0:T(4,128)} %reshape.210), kind=kLoop, calls=%fused_computation.44 | loop fusion | flops 917504 | bytes 2622464 | tf_op jit(solution)/shard_map/reduce_sum | solution.py:187
  262.2 0.8 fusion.33
  (80 shorter events, 3.4 us)
Async XLA Ops:
  7.2 4.2 %copy-start = (bf16[512,2048]{1,0:T(8,128)(2,1)S(1)}, bf16[512,2048]{1,0:T(8,128)(2,1)}, u32[]{:S(2)}) copy-start(bf16[512,2048]{1,0:T(8,128)(2,1)} %param.20) | copy-start | bytes 6291460
  7.2 2.2 copy-start.15
  7.2 4.2 %copy-start.7 = (bf16[64,2048]{1,0:T(8,128)(2,1)S(1)}, bf16[64,2048]{1,0:T(8,128)(2,1)}, u32[]{:S(2)}) copy-start(bf16[64,2048]{1,0:T(8,128)(2,1)} %param.17) | copy-start | bytes 786436
  7.2 124.7 %all-gather.7.cloned.1.call-start = ((), (), s32[]{:S(2)}) async-start(), calls=%async_computation.6 | async-start | bytes 7208960 | tf_op jit(solution)/shard_map/all_gather | solution.py:121
  7.9 158.5 %all-gather.5.cloned.1.call-start = ((), (), s32[]{:S(2)}) async-start(), calls=%async_computation.5 | async-start | bytes 7208960 | tf_op jit(solution)/shard_map/all_gather | solution.py:120
  11.4 1.0 copy-start.8
  12.3 1.1 copy-start.10
  12.7 1.6 copy-start.14
  15.2 6.1 %copy-start.12 = (s32[256,4]{0,1:T(4,128)S(1)}, s32[256,4]{0,1:T(4,128)}, u32[]{:S(2)}) copy-start(s32[256,4]{0,1:T(4,128)} %param.29) | copy-start | bytes 12292
  16.3 10.5 %all-to-all-start = ((bf16[64,4,512]{2,0,1:T(8,128)(2,1)}), bf16[64,4,512]{2,0,1:T(8,128)(2,1)S(1)}, u32[]{:S(2)}, u32[]{:S(2)}) async-start(bf16[64,4,512]{2,0,1:T(8,128)(2,1)} %copy.52), calls=%async_computation | async-start | bytes 524288 | tf_op jit(solution)/shard_map/all_to_all | solution.py:119
  30.3 29.8 %copy-start.4 = (bf16[64,2048]{1,0:T(8,128)(2,1)S(1)}, bf16[64,2048]{1,0:T(8,128)(2,1)}, u32[]{:S(2)}) copy-start(bf16[64,2048]{1,0:T(8,128)(2,1)} %param.26) | copy-start | bytes 786436
  30.3 30.6 %copy-start.11 = (f32[2048]{0:T(1024)S(1)}, f32[2048]{0:T(1024)}, u32[]{:S(2)}) copy-start(f32[2048]{0:T(1024)} %param.27) | copy-start | bytes 24580
  30.3 29.6 %all-to-all-start.1 = ((bf16[4,64,2048]{2,1,0:T(8,128)(2,1)}), bf16[4,64,2048]{2,1,0:T(8,128)(2,1)S(1)}, u32[]{:S(2)}, u32[]{:S(2)}) async-start(bf16[4,64,2048]{2,1,0:T(8,128)(2,1)} %bitcast.149), calls=%async_computation.1 | async-start | bytes 2097152 | tf_op jit(solution)/shard_map/all_to_all | solution.py:131
  60.1 0.8 copy-start.1
  67.5 14.8 %copy-start.3 = (bf16[1,352,2048]{2,1,0:T(8,128)(2,1)S(1)}, bf16[1,352,2048]{2,1,0:T(8,128)(2,1)}, u32[]{:S(2)}) copy-start(bf16[1,352,2048]{2,1,0:T(8,128)(2,1)} %param.33) | copy-start | bytes 4325380
  67.5 64.4 %all-to-all-start.2 = ((bf16[64,8,2048]{2,1,0:T(8,128)(2,1)}), bf16[64,8,2048]{2,1,0:T(8,128)(2,1)}, u32[]{:S(2)}, u32[]{:S(2)}) async-start(bf16[64,8,2048]{2,1,0:T(8,128)(2,1)} %bitcast_select_fusion), calls=%async_computation.2 | async-start | bytes 4194304 | tf_op jit(solution)/shard_map/all_to_all | solution.py:158
  82.2 126.0 %all-gather.9.cloned.1.call-start = ((), (), s32[]{:S(2)}) async-start(), calls=%async_computation.7 | async-start | bytes 3604480 | tf_op jit(solution)/shard_map/all_gather | solution.py:129
  83.5 91.5 %collective-permute-start = (bf16[352,1024]{1,0:T(8,128)(2,1)}, bf16[352,1024]{1,0:T(8,128)(2,1)}, u32[]{:S(2)}, u32[]{:S(2)}) collective-permute-start(bf16[352,1024]{1,0:T(8,128)(2,1)} %get-tuple-element.27), channel_id=1, source_target_pairs={{0,1},{1,2},{2,3},{3,0},{4,5},{5,6},{6,7},{7,4},{8,9},{9,10},{10,1... | collective-permute-start | bytes 2162696 | tf_op jit(solution)/shard_map/ppermute | solution.py:126
  83.8 93.0 %collective-permute-start.1 = (bf16[352,1024]{1,0:T(8,128)(2,1)}, bf16[352,1024]{1,0:T(8,128)(2,1)}, u32[]{:S(2)}, u32[]{:S(2)}) collective-permute-start(bf16[352,1024]{1,0:T(8,128)(2,1)} %get-tuple-element.27), channel_id=1, source_target_pairs={{0,2},{1,3},{2,0},{3,1},{4,6},{5,7},{6,4},{7,5},{8,10},{9,11},{10,... | collective-permute-start | bytes 2162696 | tf_op jit(solution)/shard_map/ppermute | solution.py:126
  85.6 93.1 %collective-permute-start.2 = (bf16[352,1024]{1,0:T(8,128)(2,1)}, bf16[352,1024]{1,0:T(8,128)(2,1)}, u32[]{:S(2)}, u32[]{:S(2)}) collective-permute-start(bf16[352,1024]{1,0:T(8,128)(2,1)} %get-tuple-element.27), channel_id=1, source_target_pairs={{0,3},{1,0},{2,1},{3,2},{4,7},{5,4},{6,5},{7,6},{8,11},{9,8},{10,9... | collective-permute-start | bytes 2162696 | tf_op jit(solution)/shard_map/ppermute | solution.py:126
  174.3 4.5 %copy-start.6 = (bf16[512,4,352]{0,2,1:T(8,128)(2,1)}, bf16[512,4,352]{0,2,1:T(8,128)(2,1)S(1)}, u32[]{:S(2)}) copy-start(bf16[512,4,352]{0,2,1:T(8,128)(2,1)S(1)} %multiply_convert_fusion) | copy-start | bytes 4325380
  181.6 38.7 %all-to-all-start.3 = ((bf16[64,8,1024]{2,1,0:T(8,128)(2,1)}), bf16[64,8,1024]{2,1,0:T(8,128)(2,1)S(1)}, u32[]{:S(2)}, u32[]{:S(2)}) async-start(bf16[64,8,1024]{2,1,0:T(8,128)(2,1)} %fusion.27), calls=%async_computation.3 | async-start | bytes 2097152 | tf_op jit(solution)/shard_map/all_to_all | solution.py:169
  213.2 13.5 %copy-start.16 = (s32[1,8]{1,0:T(1,128)S(1)}, s32[1,8]{1,0:T(1,128)}, u32[]{:S(2)}) copy-start(s32[1,8]{1,0:T(1,128)} %param.25) | copy-start | bytes 100
  213.2 13.5 %copy-start.9 = (bf16[64,2048]{1,0:T(8,128)(2,1)S(1)}, bf16[64,2048]{1,0:T(8,128)(2,1)}, u32[]{:S(2)}) copy-start(bf16[64,2048]{1,0:T(8,128)(2,1)} %param.18) | copy-start | bytes 786436
  213.2 15.7 %copy-start.13 = (f32[256,4]{0,1:T(4,128)S(1)}, f32[256,4]{0,1:T(4,128)}, u32[]{:S(2)}) copy-start(f32[256,4]{0,1:T(4,128)} %param.30) | copy-start | bytes 12292
  220.3 34.6 %all-to-all-start.4 = ((bf16[64,8,1024]{2,1,0:T(8,128)(2,1)}), bf16[64,8,1024]{2,1,0:T(8,128)(2,1)}, u32[]{:S(2)}, u32[]{:S(2)}) async-start(bf16[64,8,1024]{2,1,0:T(8,128)(2,1)} %fusion.14), calls=%async_computation.4 | async-start | bytes 2097152 | tf_op jit(solution)/shard_map/all_to_all | solution.py:177
  257.7 4.5 %copy-start.2 = (f32[64,2048]{1,0:T(8,128)S(1)}, f32[64,2048]{1,0:T(8,128)}, u32[]{:S(2)}) copy-start(f32[64,2048]{1,0:T(8,128)} %copy-done.1) | copy-start | bytes 1572868
  257.7 4.5 %copy-start.5 = (bf16[64,2048]{1,0:T(8,128)(2,1)S(1)}, bf16[64,2048]{1,0:T(8,128)(2,1)}, u32[]{:S(2)}) copy-start(bf16[64,2048]{1,0:T(8,128)(2,1)} %param.26) | copy-start | bytes 786436
Sparse Core Ops, SparseCore 0:
  9.8 79.0 all-gather.6
  90.7 75.7 all-gather.4
  168.3 39.9 all-gather.8

commit v6 on v5

--- a/solution.py
+++ b/solution.py
@@ -117,8 +117,7 @@
     )
     attended = attended.reshape(tok_rows, width)
     head_group = lax.all_to_all(attended, "cuts", split_axis=1, concat_axis=0, tiled=True)
-    gate_full = lax.all_gather(w_gate[0], "cuts", axis=0)
-    up_full = lax.all_gather(w_up[0], "cuts", axis=0)
+    gate_up_full = lax.all_gather(jnp.stack([w_gate[0], w_up[0]]), "cuts", axis=0)
     cut_count = lax.axis_size("cuts")
     half = width // 2
     down_early = w_down[0][:, :half]
@@ -157,8 +156,8 @@
     outgoing = outgoing.reshape(experts_all, capacity, width)
     arrived = lax.all_to_all(outgoing, "expert", split_axis=0, concat_axis=0, tiled=True)
     rows = arrived.reshape(-1, width)
-    gate = jnp.einsum("rd,cdf->rcf", rows, gate_full, preferred_element_type=jnp.float32)
-    upper = jnp.einsum("rd,cdf->rcf", rows, up_full, preferred_element_type=jnp.float32)
+    gate = jnp.einsum("rd,cdf->rcf", rows, gate_up_full[:, 0], preferred_element_type=jnp.float32)
+    upper = jnp.einsum("rd,cdf->rcf", rows, gate_up_full[:, 1], preferred_element_type=jnp.float32)
     hidden = (jax.nn.silu(gate) * upper).astype(jnp.bfloat16)
     product = None
     for shift, down_part in enumerate(down_parts):

time: 271 us -> 278 us (1.026)
  waiting for transfers between devices: 146 us -> 153 us
  matrix products: 35.3 us -> 31.2 us
  other arithmetic: 9.76 us -> 13.6 us
    all_gather x2 -> x1, waiting for transfers between devices: 26.5 us -> 34.8 us  [on_device(): lax.all_gather(jnp.stack([w_gate[0], w_up[0]]), 'cuts', axis=0)]
    dot_general x2, matrix products: 15.9 us -> 11.5 us  [the longest x1 6.02 us: on_device(): jnp.einsum('rd,cdf->rcf', rows, gate_up_full[:, 1], preferred_element_typ...]
    another operation x2 -> x3, other arithmetic: 0.65 us -> 4.51 us  [the longest x1 3.87 us: on_device(): jnp.stack([w_gate[0], w_up[0]])]
    all_to_all x1, waiting for transfers between devices: 7.01 us -> 10.9 us  [on_device(): lax.all_to_all(product.astype(jnp.bfloat16).reshape(experts_all, capacity...]
    all_gather x1, waiting for transfers between devices: 16.1 us -> 12.3 us  [on_device(): down_late = lax.all_gather(w_down[0][:, half:], 'cuts', axis=0)]
  transfers between devices with their start and end apart: 11 -> 10, of which waited for: 7 -> 7; matrix products, arithmetic and copies ran while one was open for 21% -> 19% of each run, Pallas kernels for 0% -> 0%
where the time goes in v6:
time: 278 us
  waiting for transfers between devices  153 us (55%)
  starting transfers between devices  43.4 us (16%)
  matrix products  31.2 us (11%)
  local copies, waits for them, and re-layouts  20.7 us (7%)
  between operations  16 us (6%)
  other arithmetic  13.6 us (5%)
    all_to_all x1, waiting for transfers between devices, on_device(): lax.all_to_all(outgoing, 'expert', split_axis=0, concat_axis=0, tiled=True)  45.5 us
    all_gather x1, waiting for transfers between devices, on_device(): lax.all_gather(jnp.stack([w_gate[0], w_up[0]]), 'cuts', axis=0)  34.8 us
    all_to_all x1, waiting for transfers between devices, on_device(): lax.all_to_all(projected.astype(jnp.bfloat16).reshape(lax.axis_size('cuts...  24.3 us
    all_to_all x1, waiting for transfers between devices, on_device(): lax.all_to_all(product_late.astype(jnp.bfloat16).reshape(experts_all, cap...  20.7 us
    all_to_all x1, starting transfers between devices, on_device(): lax.all_to_all(outgoing, 'expert', split_axis=0, concat_axis=0, tiled=True)  14.7 us
    all_gather x1, waiting for transfers between devices, on_device(): down_late = lax.all_gather(w_down[0][:, half:], 'cuts', axis=0)  12.3 us
    all_to_all x1, waiting for transfers between devices, on_device(): lax.all_to_all(product.astype(jnp.bfloat16).reshape(experts_all, capacity...  10.9 us
    all_to_all x1, starting transfers between devices, on_device(): lax.all_to_all(product.astype(jnp.bfloat16).reshape(experts_all, capacity...  10.8 us
  transfers between devices with their start and end apart: 10, of which 7 were waited for; matrix products, arithmetic and copies ran while one was open for 19% of the time, Pallas kernels for 0%

profile of v6, /device:TPU:1, one launch (start us, length us, event | category | flops | bytes accessed | tf_op | source)
XLA Modules:
  0.0 277.5 jit_solution(8801939455100728704)
XLA Ops:
  7.2 3.9 %pad_maximum_fusion = bf16[2,2048,352]{1,2,0:T(8,128)(2,1)} fusion(bf16[1,2048,352]{1,2,0:T(8,128)(2,1)} %param.32, bf16[1,2048,352]{1,2,0:T(8,128)(2,1)} %param.31), kind=kLoop, calls=%fused_computation.10 | loop fusion | flops 1441792 | bytes 5767168 | tf_op jit(solution)/shard_map/stack | solution.py:120
  12.5 0.2 convolution_minimum_fusion.6
  13.9 0.3 fusion.77
  14.2 0.9 fusion.10
  15.2 0.6 fusion.11
  16.0 0.3 fusion.49
  16.3 0.5 copy-done.15
  16.8 0.9 fusion.22
  18.0 0.7 copy.54
  18.8 5.0 %all-to-all-start = ((bf16[64,4,512]{2,0,1:T(8,128)(2,1)}), bf16[64,4,512]{2,0,1:T(8,128)(2,1)S(1)}, u32[]{:S(2)}, u32[]{:S(2)}) async-start(bf16[64,4,512]{2,0,1:T(8,128)(2,1)} %copy.54), calls=%async_computation | async-start | bytes 524288 | tf_op jit(solution)/shard_map/all_to_all | solution.py:119
  24.2 0.6 reduce-window.6
  25.1 4.2 %all-to-all-done = bf16[64,4,512]{2,0,1:T(8,128)(2,1)S(1)} async-done(((bf16[64,4,512]{2,0,1:T(8,128)(2,1)}), bf16[64,4,512]{2,0,1:T(8,128)(2,1)S(1)}, u32[]{:S(2)}, u32[]{:S(2)}) %all-to-all-start) | async-done | bytes 262176 | tf_op jit(solution)/shard_map/all_to_all | solution.py:119
  29.3 3.6 %convolution_convert_fusion = bf16[256,2048]{1,0:T(8,128)(2,1)} fusion(bf16[256,512]{1,0:T(8,128)(2,1)S(1)} %bitcast.163, bf16[512,2048]{1,0:T(8,128)(2,1)} %param.28), kind=kOutput, calls=%fused_computation.12 | convolution fusion | flops 537395200 | bytes 3407872 | tf_op jit(solution)/shard_map/dot_general | solution.py:129
  32.9 3.7 %all-to-all-start.1 = ((bf16[4,64,2048]{2,1,0:T(8,128)(2,1)}), bf16[4,64,2048]{2,1,0:T(8,128)(2,1)S(1)}, u32[]{:S(2)}, u32[]{:S(2)}) async-start(bf16[4,64,2048]{2,1,0:T(8,128)(2,1)} %bitcast.160), calls=%async_computation.1 | async-start | bytes 2097152 | tf_op jit(solution)/shard_map/all_to_all | solution.py:130
  36.8 1.4 scatter_custom_fusion
  38.4 24.3 %all-to-all-done.1 = bf16[4,64,2048]{2,1,0:T(8,128)(2,1)S(1)} async-done(((bf16[4,64,2048]{2,1,0:T(8,128)(2,1)}), bf16[4,64,2048]{2,1,0:T(8,128)(2,1)S(1)}, u32[]{:S(2)}, u32[]{:S(2)}) %all-to-all-start.1) | async-done | bytes 1048608 | tf_op jit(solution)/shard_map/all_to_all | solution.py:130
  63.0 0.6 copy-done.1
  63.8 3.3 %gather_fusion = bf16[512,2048]{1,0:T(8,128)(2,1)} fusion(bf16[64,2048]{1,0:T(8,128)(2,1)S(1)} %multiply_convert_fusion.1, s32[1024]{0:T(1024)S(1)} %pad_clamp_fusion.2), kind=kCustom, calls=%fused_computation | custom fusion | bytes 4196352 | tf_op jit(solution)/shard_map/gather | solution.py:154
  67.1 3.1 %bitcast_select_fusion = bf16[64,8,2048]{2,1,0:T(8,128)(2,1)} fusion(bf16[512,2048]{1,0:T(8,128)(2,1)} %gather_fusion, pred[64,8]{1,0:T(8,128)(4,1)S(1)} %broadcast_in_dim.90), kind=kLoop, calls=%fused_computation.22 | loop fusion | flops 1048576 | bytes 4194816 | tf_op jit(solution)/shard_map/jit(_where)/select_n | solution.py:153
  70.2 14.7 %all-to-all-start.2 = ((bf16[64,8,2048]{2,1,0:T(8,128)(2,1)}), bf16[64,8,2048]{2,1,0:T(8,128)(2,1)}, u32[]{:S(2)}, u32[]{:S(2)}) async-start(bf16[64,8,2048]{2,1,0:T(8,128)(2,1)} %bitcast_select_fusion), calls=%async_computation.2 | async-start | bytes 4194304 | tf_op jit(solution)/shard_map/all_to_all | solution.py:157
  84.9 1.3 fusion.76
  86.2 0.3 collective-permute-start
  86.5 1.8 collective-permute-start.1
  88.3 0.6 collective-permute-start.2
  89.0 45.5 %all-to-all-done.2 = bf16[64,8,2048]{2,1,0:T(8,128)(2,1)} async-done(((bf16[64,8,2048]{2,1,0:T(8,128)(2,1)}), bf16[64,8,2048]{2,1,0:T(8,128)(2,1)}, u32[]{:S(2)}, u32[]{:S(2)}) %all-to-all-start.2) | async-done | bytes 2097184 | tf_op jit(solution)/shard_map/all_to_all | solution.py:157
  134.5 34.8 %all-gather.5.cloned.1.call-done = bf16[8,2048,352]{1,2,0:T(8,128)(2,1)} async-done(((bf16[2,2048,352]{1,2,0:T(8,128)(2,1)}), bf16[8,2048,352]{1,2,0:T(8,128)(2,1)}) %all-gather.5.cloned.1.call-update) | async-done | bytes 11534352 | tf_op jit(solution)/shard_map/all_gather | solution.py:120
  169.3 6.0 %fusion = f32[512,4,352]{0,2,1:T(8,128)S(1)} fusion(bf16[4,2,2048,352]{2,3,1,0:T(8,128)(2,1)} %bitcast.167, bf16[64,8,2048]{2,1,0:T(8,128)(2,1)} %all-to-all-done.2), kind=kOutput, calls=%fused_computation.7 | convolution fusion | flops 2952790016 | bytes 10747904 | tf_op jit(solution)/shard_map/rd,cdf->rcf/dot_general | solution.py:160
  175.3 0.6 copy-done.14
  175.9 5.5 %multiply_convert_fusion = bf16[512,4,352]{0,2,1:T(8,128)(2,1)S(1)} fusion(f32[512,4,352]{0,2,1:T(8,128)S(1)} %fusion, bf16[4,2,2048,352]{2,3,1,0:T(8,128)(2,1)S(1)} %bitcast.168, bf16[64,8,2048]{2,1,0:T(8,128)(2,1)} %all-to-all-done.2), kind=kOutput, calls=%fused_computation.11 | convolution fusion | flops 2957115392 | bytes 12189696 | tf_op jit(solution)/shard_map/rd,cdf->rcf/dot_general | solution.py:159
  181.4 0.8 fusion.43
  182.2 1.9 fusion.41
  184.0 1.9 fusion.39
  186.0 2.9 %fusion.27 = bf16[64,8,1024]{2,1,0:T(8,128)(2,1)} fusion(f32[512,1024]{1,0:T(8,128)S(1)} %fusion.39, f32[512,1024]{1,0:T(8,128)S(1)} %fusion.43, f32[512,1024]{1,0:T(8,128)S(1)} %fusion.41, bf16[352,1024]{1,0:T(8,128)(2,1)} %collective-permute-done.2, bf16[512,4,352]{0,2,1:T(8,128)(2,1)S(1)} %multiply_convert_fusion, s32[]{:T(128)S(6)} %select_n.93), kind=kOutput, calls=%fused_computation.45 | convolution fusion | flops 371195904 | bytes 8421380 | tf_op jit(solution)/shard_map/dot_general | solution.py:166
  188.9 10.8 %all-to-all-start.3 = ((bf16[64,8,1024]{2,1,0:T(8,128)(2,1)}), bf16[64,8,1024]{2,1,0:T(8,128)(2,1)S(1)}, u32[]{:S(2)}, u32[]{:S(2)}) async-start(bf16[64,8,1024]{2,1,0:T(8,128)(2,1)} %fusion.27), calls=%async_computation.3 | async-start | bytes 2097152 | tf_op jit(solution)/shard_map/all_to_all | solution.py:168
  199.7 12.3 %all-gather.7.cloned.1.call-done = bf16[1408,1024]{1,0:T(8,128)(2,1)} async-done(((bf16[352,1024]{1,0:T(8,128)(2,1)}), bf16[1408,1024]{1,0:T(8,128)(2,1)}) %all-gather.7.cloned.1.call-update) | async-done | bytes 2883600 | tf_op jit(solution)/shard_map/all_gather | solution.py:128
  212.0 5.0 %fusion.12 = bf16[64,8,1024]{2,1,0:T(8,128)(2,1)} fusion(bf16[512,4,352]{0,2,1:T(8,128)(2,1)} %copy-done.6, bf16[4,352,1024]{2,1,0:T(8,128)(2,1)} %bitcast.169), kind=kOutput, calls=%fused_computation.30 | convolution fusion | flops 1476919296 | bytes 5373952 | tf_op jit(solution)/shard_map/rcf,cfd->rd/dot_general | solution.py:175
  217.0 10.9 %all-to-all-done.3 = bf16[64,8,1024]{2,1,0:T(8,128)(2,1)S(1)} async-done(((bf16[64,8,1024]{2,1,0:T(8,128)(2,1)}), bf16[64,8,1024]{2,1,0:T(8,128)(2,1)S(1)}, u32[]{:S(2)}, u32[]{:S(2)}) %all-to-all-start.3) | async-done | bytes 1048608 | tf_op jit(solution)/shard_map/all_to_all | solution.py:168
  227.9 6.5 %all-to-all-start.4 = ((bf16[64,8,1024]{2,1,0:T(8,128)(2,1)}), bf16[64,8,1024]{2,1,0:T(8,128)(2,1)}, u32[]{:S(2)}, u32[]{:S(2)}) async-start(bf16[64,8,1024]{2,1,0:T(8,128)(2,1)} %fusion.12), calls=%async_computation.4 | async-start | bytes 2097152 | tf_op jit(solution)/shard_map/all_to_all | solution.py:176
  234.4 0.6 gather_fusion.3
  235.0 1.6 gather_fusion.4
  236.8 0.6 pad_maximum_fusion.1
  237.4 2.0 gather_fusion.1
  239.4 2.4 reshape.209
  241.8 20.7 %all-to-all-done.4 = bf16[64,8,1024]{2,1,0:T(8,128)(2,1)} async-done(((bf16[64,8,1024]{2,1,0:T(8,128)(2,1)}), bf16[64,8,1024]{2,1,0:T(8,128)(2,1)}, u32[]{:S(2)}, u32[]{:S(2)}) %all-to-all-start.4) | async-done | bytes 1048608 | tf_op jit(solution)/shard_map/all_to_all | solution.py:176
  262.5 2.9 %gather_fusion.2 = bf16[256,1024]{1,0:T(8,128)(2,1)S(1)} fusion(bf16[512,1024]{1,0:T(8,128)(2,1)} %bitcast.27, s32[1024]{0:T(1024)S(1)} %pad_clamp_fusion.1), kind=kCustom, calls=%fused_computation.2 | custom fusion | bytes 1049600 | tf_op jit(solution)/shard_map/gather | solution.py:185
  265.4 1.3 reshape.210
  266.7 3.1 %multiply_reduce_fusion.1 = (f32[64,1024]{1,0:T(8,128)S(1)}, f32[64,1024]{1,0:T(8,128)S(1)}) fusion(f32[64,4,1024]{2,1,0:T(4,128)} %reshape.209, f32[64,4]{1,0:T(8,128)S(1)} %copy.55, f32[64,4,1024]{2,1,0:T(4,128)} %reshape.210), kind=kLoop, calls=%fused_computation.47 | loop fusion | flops 917504 | bytes 2622464 | tf_op jit(solution)/shard_map/reduce_sum | solution.py:186
  269.9 0.8 fusion.33
  (80 shorter events, 3.5 us)
Async XLA Ops:
  7.2 7.0 %copy-start = (bf16[512,2048]{1,0:T(8,128)(2,1)S(1)}, bf16[512,2048]{1,0:T(8,128)(2,1)}, u32[]{:S(2)}) copy-start(bf16[512,2048]{1,0:T(8,128)(2,1)} %param.20) | copy-start | bytes 6291460
  7.2 162.1 %all-gather.5.cloned.1.call-start = ((), (), s32[]{:S(2)}) async-start(), calls=%async_computation.5 | async-start | bytes 14417920 | tf_op jit(solution)/shard_map/all_gather | solution.py:120
  11.1 1.4 copy-start.16
  11.1 2.7 copy-start.7
  11.1 2.8 copy-start.8
  15.1 1.0 copy-start.10
  15.2 1.6 copy-start.15
  17.7 6.1 %copy-start.12 = (s32[256,4]{0,1:T(4,128)S(1)}, s32[256,4]{0,1:T(4,128)}, u32[]{:S(2)}) copy-start(s32[256,4]{0,1:T(4,128)} %param.29) | copy-start | bytes 12292
  18.8 10.5 %all-to-all-start = ((bf16[64,4,512]{2,0,1:T(8,128)(2,1)}), bf16[64,4,512]{2,0,1:T(8,128)(2,1)S(1)}, u32[]{:S(2)}, u32[]{:S(2)}) async-start(bf16[64,4,512]{2,0,1:T(8,128)(2,1)} %copy.54), calls=%async_computation | async-start | bytes 524288 | tf_op jit(solution)/shard_map/all_to_all | solution.py:119
  32.9 29.9 %copy-start.4 = (bf16[64,2048]{1,0:T(8,128)(2,1)S(1)}, bf16[64,2048]{1,0:T(8,128)(2,1)}, u32[]{:S(2)}) copy-start(bf16[64,2048]{1,0:T(8,128)(2,1)} %param.26) | copy-start | bytes 786436
  32.9 30.7 %copy-start.11 = (f32[2048]{0:T(1024)S(1)}, f32[2048]{0:T(1024)}, u32[]{:S(2)}) copy-start(f32[2048]{0:T(1024)} %param.27) | copy-start | bytes 24580
  32.9 29.7 %all-to-all-start.1 = ((bf16[4,64,2048]{2,1,0:T(8,128)(2,1)}), bf16[4,64,2048]{2,1,0:T(8,128)(2,1)S(1)}, u32[]{:S(2)}, u32[]{:S(2)}) async-start(bf16[4,64,2048]{2,1,0:T(8,128)(2,1)} %bitcast.160), calls=%async_computation.1 | async-start | bytes 2097152 | tf_op jit(solution)/shard_map/all_to_all | solution.py:130
  62.8 0.8 copy-start.1
  70.2 14.7 %copy-start.3 = (bf16[1,352,2048]{2,1,0:T(8,128)(2,1)S(1)}, bf16[1,352,2048]{2,1,0:T(8,128)(2,1)}, u32[]{:S(2)}) copy-start(bf16[1,352,2048]{2,1,0:T(8,128)(2,1)} %param.33) | copy-start | bytes 4325380
  70.2 64.3 %all-to-all-start.2 = ((bf16[64,8,2048]{2,1,0:T(8,128)(2,1)}), bf16[64,8,2048]{2,1,0:T(8,128)(2,1)}, u32[]{:S(2)}, u32[]{:S(2)}) async-start(bf16[64,8,2048]{2,1,0:T(8,128)(2,1)} %bitcast_select_fusion), calls=%async_computation.2 | async-start | bytes 4194304 | tf_op jit(solution)/shard_map/all_to_all | solution.py:157
  84.9 127.1 %all-gather.7.cloned.1.call-start = ((), (), s32[]{:S(2)}) async-start(), calls=%async_computation.6 | async-start | bytes 3604480 | tf_op jit(solution)/shard_map/all_gather | solution.py:128
  86.2 95.9 %collective-permute-start = (bf16[352,1024]{1,0:T(8,128)(2,1)}, bf16[352,1024]{1,0:T(8,128)(2,1)}, u32[]{:S(2)}, u32[]{:S(2)}) collective-permute-start(bf16[352,1024]{1,0:T(8,128)(2,1)} %get-tuple-element.27), channel_id=1, source_target_pairs={{0,1},{1,2},{2,3},{3,0},{4,5},{5,6},{6,7},{7,4},{8,9},{9,10},{10,1... | collective-permute-start | bytes 2162696 | tf_op jit(solution)/shard_map/ppermute | solution.py:125
  86.5 97.5 %collective-permute-start.1 = (bf16[352,1024]{1,0:T(8,128)(2,1)}, bf16[352,1024]{1,0:T(8,128)(2,1)}, u32[]{:S(2)}, u32[]{:S(2)}) collective-permute-start(bf16[352,1024]{1,0:T(8,128)(2,1)} %get-tuple-element.27), channel_id=1, source_target_pairs={{0,2},{1,3},{2,0},{3,1},{4,6},{5,7},{6,4},{7,5},{8,10},{9,11},{10,... | collective-permute-start | bytes 2162696 | tf_op jit(solution)/shard_map/ppermute | solution.py:125
  88.3 97.7 %collective-permute-start.2 = (bf16[352,1024]{1,0:T(8,128)(2,1)}, bf16[352,1024]{1,0:T(8,128)(2,1)}, u32[]{:S(2)}, u32[]{:S(2)}) collective-permute-start(bf16[352,1024]{1,0:T(8,128)(2,1)} %get-tuple-element.27), channel_id=1, source_target_pairs={{0,3},{1,0},{2,1},{3,2},{4,7},{5,4},{6,5},{7,6},{8,11},{9,8},{10,9... | collective-permute-start | bytes 2162696 | tf_op jit(solution)/shard_map/ppermute | solution.py:125
  169.3 6.6 %copy-start.14 = (bf16[8,2048,352]{1,2,0:T(8,128)(2,1)S(1)}, bf16[8,2048,352]{1,2,0:T(8,128)(2,1)}, u32[]{:S(2)}) copy-start(bf16[8,2048,352]{1,2,0:T(8,128)(2,1)} %all-gather.5.cloned.1.call-done) | copy-start | bytes 34603012
  181.4 4.6 %copy-start.6 = (bf16[512,4,352]{0,2,1:T(8,128)(2,1)}, bf16[512,4,352]{0,2,1:T(8,128)(2,1)S(1)}, u32[]{:S(2)}) copy-start(bf16[512,4,352]{0,2,1:T(8,128)(2,1)S(1)} %multiply_convert_fusion) | copy-start | bytes 4325380
  188.9 39.0 %all-to-all-start.3 = ((bf16[64,8,1024]{2,1,0:T(8,128)(2,1)}), bf16[64,8,1024]{2,1,0:T(8,128)(2,1)S(1)}, u32[]{:S(2)}, u32[]{:S(2)}) async-start(bf16[64,8,1024]{2,1,0:T(8,128)(2,1)} %fusion.27), calls=%async_computation.3 | async-start | bytes 2097152 | tf_op jit(solution)/shard_map/all_to_all | solution.py:168
  217.0 17.4 %copy-start.17 = (s32[1,8]{1,0:T(1,128)S(1)}, s32[1,8]{1,0:T(1,128)}, u32[]{:S(2)}) copy-start(s32[1,8]{1,0:T(1,128)} %param.25) | copy-start | bytes 100
  217.0 17.4 %copy-start.9 = (bf16[64,2048]{1,0:T(8,128)(2,1)S(1)}, bf16[64,2048]{1,0:T(8,128)(2,1)}, u32[]{:S(2)}) copy-start(bf16[64,2048]{1,0:T(8,128)(2,1)} %param.18) | copy-start | bytes 786436
  217.0 19.6 %copy-start.13 = (f32[256,4]{0,1:T(4,128)S(1)}, f32[256,4]{0,1:T(4,128)}, u32[]{:S(2)}) copy-start(f32[256,4]{0,1:T(4,128)} %param.30) | copy-start | bytes 12292
  227.9 34.6 %all-to-all-start.4 = ((bf16[64,8,1024]{2,1,0:T(8,128)(2,1)}), bf16[64,8,1024]{2,1,0:T(8,128)(2,1)}, u32[]{:S(2)}, u32[]{:S(2)}) async-start(bf16[64,8,1024]{2,1,0:T(8,128)(2,1)} %fusion.12), calls=%async_computation.4 | async-start | bytes 2097152 | tf_op jit(solution)/shard_map/all_to_all | solution.py:176
  265.4 4.5 %copy-start.2 = (f32[64,2048]{1,0:T(8,128)S(1)}, f32[64,2048]{1,0:T(8,128)}, u32[]{:S(2)}) copy-start(f32[64,2048]{1,0:T(8,128)} %copy-done.1) | copy-start | bytes 1572868
  265.4 4.5 %copy-start.5 = (bf16[64,2048]{1,0:T(8,128)(2,1)S(1)}, bf16[64,2048]{1,0:T(8,128)(2,1)}, u32[]{:S(2)}) copy-start(bf16[64,2048]{1,0:T(8,128)(2,1)} %param.26) | copy-start | bytes 786436
Sparse Core Ops, SparseCore 0:
  11.2 157.9 all-gather.4
  171.1 40.8 all-gather.6

commit v7 on v5

--- a/solution.py
+++ b/solution.py
@@ -118,7 +118,6 @@
     attended = attended.reshape(tok_rows, width)
     head_group = lax.all_to_all(attended, "cuts", split_axis=1, concat_axis=0, tiled=True)
     gate_full = lax.all_gather(w_gate[0], "cuts", axis=0)
-    up_full = lax.all_gather(w_up[0], "cuts", axis=0)
     cut_count = lax.axis_size("cuts")
     half = width // 2
     down_early = w_down[0][:, :half]
@@ -127,6 +126,10 @@
         for shift in range(1, cut_count)
     ]
     down_late = lax.all_gather(w_down[0][:, half:], "cuts", axis=0)
+    up_parts = [w_up[0]] + [
+        lax.ppermute(w_up[0], "cuts", [(i, (i + shift) % cut_count) for i in range(cut_count)])
+        for shift in range(1, cut_count)
+    ]
     projected = jnp.dot(head_group, out_weight, preferred_element_type=jnp.float32)
     partials = lax.all_to_all(
         projected.astype(jnp.bfloat16).reshape(lax.axis_size("cuts"), tok_rows, width),
@@ -158,12 +161,14 @@
     arrived = lax.all_to_all(outgoing, "expert", split_axis=0, concat_axis=0, tiled=True)
     rows = arrived.reshape(-1, width)
     gate = jnp.einsum("rd,cdf->rcf", rows, gate_full, preferred_element_type=jnp.float32)
-    upper = jnp.einsum("rd,cdf->rcf", rows, up_full, preferred_element_type=jnp.float32)
-    hidden = (jax.nn.silu(gate) * upper).astype(jnp.bfloat16)
+    slices = []
+    for shift, up_part in enumerate(up_parts):
+        owner = (place - shift) % cut_count
+        slice_gate = lax.dynamic_index_in_dim(gate, owner, axis=1, keepdims=False)
+        upper = jnp.dot(rows, up_part, preferred_element_type=jnp.float32)
+        slices.append((owner, (jax.nn.silu(slice_gate) * upper).astype(jnp.bfloat16)))
     product = None
-    for shift, down_part in enumerate(down_parts):
-        owner = (place - shift) % cut_count
-        slice_hidden = lax.dynamic_index_in_dim(hidden, owner, axis=1, keepdims=False)
+    for (owner, slice_hidden), down_part in zip(slices, down_parts):
         term = jnp.dot(slice_hidden, down_part, preferred_element_type=jnp.float32)
         product = term if product is None else product + term
     returned_early = lax.all_to_all(
@@ -173,7 +178,11 @@
         concat_axis=0,
         tiled=True,
     )
-    product_late = jnp.einsum("rcf,cfd->rd", hidden, down_late, preferred_element_type=jnp.float32)
+    product_late = None
+    for owner, slice_hidden in slices:
+        down_w = lax.dynamic_index_in_dim(down_late, owner, axis=0, keepdims=False)
+        term = jnp.dot(slice_hidden, down_w, preferred_element_type=jnp.float32)
+        product_late = term if product_late is None else product_late + term
     returned_late = lax.all_to_all(
         product_late.astype(jnp.bfloat16).reshape(experts_all, capacity, half),
         "expert",

time: 271 us -> 298 us (1.100)
  waiting for transfers between devices: 146 us -> 169 us
  starting transfers between devices: 43.2 us -> 49 us
    ppermute x3, waiting for transfers between devices: 0.01 us -> 44.8 us  [on_device(): lax.ppermute(down_early, 'cuts', [(i, (i + shift) % cut_count) for i in r...]
    all_gather x1, waiting for transfers between devices: 26.5 us -> 0.01 us  [on_device(): gate_full = lax.all_gather(w_gate[0], 'cuts', axis=0)]
    all_gather x1, waiting for transfers between devices: 16.1 us -> 0.02 us  [on_device(): down_late = lax.all_gather(w_down[0][:, half:], 'cuts', axis=0)]
    all_to_all x1, waiting for transfers between devices: 7.01 us -> 22.6 us  [on_device(): lax.all_to_all(product.astype(jnp.bfloat16).reshape(experts_all, capacity...]
    ppermute x0 -> x3, waiting for transfers between devices: none -> 9.6 us  [on_device(): lax.ppermute(w_up[0], 'cuts', [(i, (i + shift) % cut_count) for i in rang...]
    ppermute x0 -> x3, starting transfers between devices: none -> 4.22 us  [on_device(): lax.ppermute(w_up[0], 'cuts', [(i, (i + shift) % cut_count) for i in rang...]
    dot_general x2 -> x8, matrix products: 13.1 us -> 17.1 us  [the longest x4 11.9 us: on_device(): upper = jnp.dot(rows, up_part, preferred_element_type=jnp.float32)]
    all_to_all x1, waiting for transfers between devices: 45.5 us -> 41.6 us  [on_device(): lax.all_to_all(outgoing, 'expert', split_axis=0, concat_axis=0, tiled=True)]
  transfers between devices with their start and end apart: 11 -> 13, of which waited for: 7 -> 8; matrix products, arithmetic and copies ran while one was open for 21% -> 18% of each run, Pallas kernels for 0% -> 0%
where the time goes in v7:
time: 298 us; the launch traced here: 296 us
  waiting for transfers between devices  169 us (57%)
  starting transfers between devices  49 us (16%)
  matrix products  35.2 us (12%)
  local copies, waits for them, and re-layouts  18.2 us (6%)
  between operations  16 us (5%)
  other arithmetic  8.22 us (3%)
    ppermute x3, waiting for transfers between devices, on_device(): lax.ppermute(down_early, 'cuts', [(i, (i + shift) % cut_count) for i in r...  44.8 us
    all_to_all x1, waiting for transfers between devices, on_device(): lax.all_to_all(outgoing, 'expert', split_axis=0, concat_axis=0, tiled=True)  41.6 us
    all_to_all x1, waiting for transfers between devices, on_device(): lax.all_to_all(projected.astype(jnp.bfloat16).reshape(lax.axis_size('cuts...  24.2 us
    all_to_all x1, waiting for transfers between devices, on_device(): lax.all_to_all(product.astype(jnp.bfloat16).reshape(experts_all, capacity...  22.6 us
    all_to_all x1, waiting for transfers between devices, on_device(): lax.all_to_all(product_late.astype(jnp.bfloat16).reshape(experts_all, cap...  21.8 us
    all_to_all x1, starting transfers between devices, on_device(): lax.all_to_all(outgoing, 'expert', split_axis=0, concat_axis=0, tiled=True)  14.9 us
    dot_general x4, matrix products, on_device(): upper = jnp.dot(rows, up_part, preferred_element_type=jnp.float32)  11.9 us
    all_to_all x1, starting transfers between devices, on_device(): lax.all_to_all(product.astype(jnp.bfloat16).reshape(experts_all, capacity...  11.5 us
  transfers between devices with their start and end apart: 13, of which 8 were waited for; matrix products, arithmetic and copies ran while one was open for 18% of the time, Pallas kernels for 0%

profile of v7, /device:TPU:1, one launch (start us, length us, event | category | flops | bytes accessed | tf_op | source)
XLA Modules:
  0.0 296.1 jit_solution(4235876914136207171)
XLA Ops:
  7.2 0.7 all-gather.4.cloned.1.call-update
  7.9 0.9 convolution_minimum_fusion.6
  11.6 0.9 fusion.16
  12.7 0.6 fusion.17
  14.3 0.9 fusion.50
  15.6 0.7 copy.52
  16.3 5.0 %all-to-all-start = ((bf16[64,4,512]{2,0,1:T(8,128)(2,1)}), bf16[64,4,512]{2,0,1:T(8,128)(2,1)S(1)}, u32[]{:S(2)}, u32[]{:S(2)}) async-start(bf16[64,4,512]{2,0,1:T(8,128)(2,1)} %copy.52), calls=%async_computation | async-start | bytes 524288 | tf_op jit(solution)/shard_map/all_to_all | solution.py:119
  22.7 4.2 %all-to-all-done = bf16[64,4,512]{2,0,1:T(8,128)(2,1)S(1)} async-done(((bf16[64,4,512]{2,0,1:T(8,128)(2,1)}), bf16[64,4,512]{2,0,1:T(8,128)(2,1)S(1)}, u32[]{:S(2)}, u32[]{:S(2)}) %all-to-all-start) | async-done | bytes 262176 | tf_op jit(solution)/shard_map/all_to_all | solution.py:119
  26.8 1.7 convolution_convert_fusion
  28.6 3.6 %all-to-all-start.1 = ((bf16[4,64,2048]{2,1,0:T(8,128)(2,1)}), bf16[4,64,2048]{2,1,0:T(8,128)(2,1)S(1)}, u32[]{:S(2)}, u32[]{:S(2)}) async-start(bf16[4,64,2048]{2,1,0:T(8,128)(2,1)} %bitcast.6), calls=%async_computation.1 | async-start | bytes 2097152 | tf_op jit(solution)/shard_map/all_to_all | solution.py:134
  32.4 1.4 scatter_custom_fusion
  34.0 24.2 %all-to-all-done.1 = bf16[4,64,2048]{2,1,0:T(8,128)(2,1)S(1)} async-done(((bf16[4,64,2048]{2,1,0:T(8,128)(2,1)}), bf16[4,64,2048]{2,1,0:T(8,128)(2,1)S(1)}, u32[]{:S(2)}, u32[]{:S(2)}) %all-to-all-start.1) | async-done | bytes 1048608 | tf_op jit(solution)/shard_map/all_to_all | solution.py:134
  58.7 2.5 gather_fusion
  61.1 1.6 bitcast_select_fusion
  62.7 14.9 %all-to-all-start.2 = ((bf16[64,8,2048]{2,1,0:T(8,128)(2,1)}), bf16[64,8,2048]{2,1,0:T(8,128)(2,1)}, u32[]{:S(2)}, u32[]{:S(2)}) async-start(bf16[64,8,2048]{2,1,0:T(8,128)(2,1)} %bitcast_select_fusion), calls=%async_computation.2 | async-start | bytes 4194304 | tf_op jit(solution)/shard_map/all_to_all | solution.py:161
  77.7 1.5 collective-permute-start
  79.2 1.3 fusion.115
  80.4 2.4 collective-permute-start.3
  82.8 2.7 collective-permute-start.4
  85.6 41.6 %all-to-all-done.2 = bf16[64,8,2048]{2,1,0:T(8,128)(2,1)} async-done(((bf16[64,8,2048]{2,1,0:T(8,128)(2,1)}), bf16[64,8,2048]{2,1,0:T(8,128)(2,1)}, u32[]{:S(2)}, u32[]{:S(2)}) %all-to-all-start.2) | async-done | bytes 2097184 | tf_op jit(solution)/shard_map/all_to_all | solution.py:161
  127.2 5.9 %fusion.6 = f32[512,4,352]{0,2,1:T(8,128)S(1)} fusion(bf16[4,2048,352]{1,2,0:T(8,128)(2,1)} %all-gather.4.cloned.1.call-done, bf16[64,8,2048]{2,1,0:T(8,128)(2,1)} %all-to-all-done.2), kind=kOutput, calls=%fused_computation.13 | convolution fusion | flops 2952790016 | bytes 10747904 | tf_op jit(solution)/shard_map/rd,cdf->rcf/dot_general | solution.py:163
  133.1 3.0 %fusion.37 = bf16[512,352]{0,1:T(8,128)(2,1)S(1)} fusion(bf16[64,8,2048]{2,1,0:T(8,128)(2,1)} %all-to-all-done.2, f32[512,4,352]{0,2,1:T(8,128)S(1)} %fusion.6, s32[]{:T(128)S(6)} %select_n.92, bf16[1,2048,352]{1,2,0:T(8,128)(2,1)} %param.32), kind=kOutput, calls=%fused_computation.39 | convolution fusion | flops 739278848 | bytes 4620292 | tf_op jit(solution)/shard_map/dot_general | solution.py:168
  136.1 1.0 collective-permute-start.5
  137.0 3.0 %fusion.31 = bf16[512,352]{0,1:T(8,128)(2,1)S(1)} fusion(bf16[2048,352]{0,1:T(8,128)(2,1)} %collective-permute-done.2, bf16[64,8,2048]{2,1,0:T(8,128)(2,1)} %all-to-all-done.2, f32[512,4,352]{0,2,1:T(8,128)S(1)} %fusion.6, s32[]{:T(128)S(6)} %select_n.96), kind=kOutput, calls=%fused_computation.37 | convolution fusion | flops 739278848 | bytes 4620292 | tf_op jit(solution)/shard_map/dot_general | solution.py:168
  140.1 0.7 fusion.113
  140.8 9.6 %collective-permute-done = bf16[2048,352]{0,1:T(8,128)(2,1)} collective-permute-done((bf16[2048,352]{0,1:T(8,128)(2,1)}, bf16[2048,352]{0,1:T(8,128)(2,1)}, u32[]{:S(2)}, u32[]{:S(2)}) %collective-permute-start) | collective-permute-done | bytes 1441824 | tf_op jit(solution)/shard_map/ppermute | solution.py:130
  150.4 3.0 %fusion.34 = bf16[512,352]{0,1:T(8,128)(2,1)S(1)} fusion(bf16[2048,352]{0,1:T(8,128)(2,1)} %collective-permute-done, bf16[64,8,2048]{2,1,0:T(8,128)(2,1)} %all-to-all-done.2, f32[512,4,352]{0,2,1:T(8,128)S(1)} %fusion.6, s32[]{:T(128)S(6)} %select_n.94), kind=kOutput, calls=%fused_computation.38 | convolution fusion | flops 739278848 | bytes 4620292 | tf_op jit(solution)/shard_map/dot_general | solution.py:168
  153.4 20.4 %collective-permute-done.3 = bf16[352,1024]{1,0:T(8,128)(2,1)} collective-permute-done((bf16[352,1024]{1,0:T(8,128)(2,1)}, bf16[352,1024]{1,0:T(8,128)(2,1)}, u32[]{:S(2)}, u32[]{:S(2)}) %collective-permute-start.3) | collective-permute-done | bytes 720928 | tf_op jit(solution)/shard_map/ppermute | solution.py:125
  173.8 1.9 fusion.118
  175.6 24.4 %collective-permute-done.1 = bf16[352,1024]{1,0:T(8,128)(2,1)} collective-permute-done((bf16[352,1024]{1,0:T(8,128)(2,1)}, bf16[352,1024]{1,0:T(8,128)(2,1)}, u32[]{:S(2)}, u32[]{:S(2)}) %collective-permute-start.1) | collective-permute-done | bytes 720928 | tf_op jit(solution)/shard_map/ppermute | solution.py:125
  200.0 1.9 fusion.117
  201.9 3.0 %fusion.40 = bf16[512,352]{0,1:T(8,128)(2,1)S(1)} fusion(bf16[2048,352]{0,1:T(8,128)(2,1)} %collective-permute-done.4, bf16[64,8,2048]{2,1,0:T(8,128)(2,1)} %all-to-all-done.2, f32[512,4,352]{0,2,1:T(8,128)S(1)} %fusion.6, s32[]{:T(128)S(6)} %select_n.98), kind=kOutput, calls=%fused_computation.40 | convolution fusion | flops 739278848 | bytes 4620292 | tf_op jit(solution)/shard_map/dot_general | solution.py:168
  204.9 1.8 fusion.55
  206.7 11.5 %all-to-all-start.3 = ((bf16[64,8,1024]{2,1,0:T(8,128)(2,1)}), bf16[64,8,1024]{2,1,0:T(8,128)(2,1)S(1)}, u32[]{:S(2)}, u32[]{:S(2)}) async-start(bf16[64,8,1024]{2,1,0:T(8,128)(2,1)} %fusion.55), calls=%async_computation.3 | async-start | bytes 2097152 | tf_op jit(solution)/shard_map/all_to_all | solution.py:174
  218.3 2.0 fusion.62
  220.3 0.7 fusion.66
  221.3 0.7 fusion.64
  222.0 1.8 fusion.18
  223.8 22.6 %all-to-all-done.3 = bf16[64,8,1024]{2,1,0:T(8,128)(2,1)S(1)} async-done(((bf16[64,8,1024]{2,1,0:T(8,128)(2,1)}), bf16[64,8,1024]{2,1,0:T(8,128)(2,1)S(1)}, u32[]{:S(2)}, u32[]{:S(2)}) %all-to-all-start.3) | async-done | bytes 1048608 | tf_op jit(solution)/shard_map/all_to_all | solution.py:174
  246.4 6.3 %all-to-all-start.4 = ((bf16[64,8,1024]{2,1,0:T(8,128)(2,1)}), bf16[64,8,1024]{2,1,0:T(8,128)(2,1)S(1)}, u32[]{:S(2)}, u32[]{:S(2)}) async-start(bf16[64,8,1024]{2,1,0:T(8,128)(2,1)} %fusion.18), calls=%async_computation.4 | async-start | bytes 2097152 | tf_op jit(solution)/shard_map/all_to_all | solution.py:186
  254.1 0.6 pad_maximum_fusion
  254.7 2.0 gather_fusion.1
  256.7 2.3 reshape.209
  259.1 21.8 %all-to-all-done.4 = bf16[64,8,1024]{2,1,0:T(8,128)(2,1)S(1)} async-done(((bf16[64,8,1024]{2,1,0:T(8,128)(2,1)}), bf16[64,8,1024]{2,1,0:T(8,128)(2,1)S(1)}, u32[]{:S(2)}, u32[]{:S(2)}) %all-to-all-start.4) | async-done | bytes 1048608 | tf_op jit(solution)/shard_map/all_to_all | solution.py:186
  280.9 2.0 gather_fusion.2
  282.8 2.5 reshape.210
  285.4 3.1 %multiply_reduce_fusion.1 = (f32[64,1024]{1,0:T(8,128)S(1)}, f32[64,1024]{1,0:T(8,128)S(1)}) fusion(f32[64,4,1024]{2,1,0:T(4,128)} %reshape.209, f32[64,4]{1,0:T(8,128)S(1)} %copy.53, f32[64,4,1024]{2,1,0:T(4,128)} %reshape.210), kind=kLoop, calls=%fused_computation.57 | loop fusion | flops 917504 | bytes 2622464 | tf_op jit(solution)/shard_map/reduce_sum | solution.py:196
  288.5 0.8 fusion.84
  (101 shorter events, 6.7 us)
Async XLA Ops:
  7.2 4.5 %copy-start = (bf16[512,2048]{1,0:T(8,128)(2,1)S(1)}, bf16[512,2048]{1,0:T(8,128)(2,1)}, u32[]{:S(2)}) copy-start(bf16[512,2048]{1,0:T(8,128)(2,1)} %param.20) | copy-start | bytes 6291460
  7.2 4.1 %copy-start.16 = (bf16[64,2048]{1,0:T(8,128)(2,1)S(1)}, bf16[64,2048]{1,0:T(8,128)(2,1)}, u32[]{:S(2)}) copy-start(bf16[64,2048]{1,0:T(8,128)(2,1)} %param.18) | copy-start | bytes 786436
  7.2 4.1 %copy-start.13 = (bf16[64,2048]{1,0:T(8,128)(2,1)S(1)}, bf16[64,2048]{1,0:T(8,128)(2,1)}, u32[]{:S(2)}) copy-start(bf16[64,2048]{1,0:T(8,128)(2,1)} %param.17) | copy-start | bytes 786436
  7.2 120.0 %all-gather.4.cloned.1.call-start = ((), (), s32[]{:S(2)}) async-start(), calls=%async_computation.5 | async-start | bytes 7208960 | tf_op jit(solution)/shard_map/all_gather | solution.py:120
  12.6 1.0 copy-start.14
  12.7 1.6 copy-start.21
  15.2 6.1 %copy-start.19 = (s32[256,4]{0,1:T(4,128)S(1)}, s32[256,4]{0,1:T(4,128)}, u32[]{:S(2)}) copy-start(s32[256,4]{0,1:T(4,128)} %param.29) | copy-start | bytes 12292
  15.3 11.6 %copy-start.6 = (bf16[512,2048]{1,0:T(8,128)(2,1)S(1)}, bf16[512,2048]{1,0:T(8,128)(2,1)}, u32[]{:S(2)}) copy-start(bf16[512,2048]{1,0:T(8,128)(2,1)} %param.28) | copy-start | bytes 6291460
  16.3 10.5 %all-to-all-start = ((bf16[64,4,512]{2,0,1:T(8,128)(2,1)}), bf16[64,4,512]{2,0,1:T(8,128)(2,1)S(1)}, u32[]{:S(2)}, u32[]{:S(2)}) async-start(bf16[64,4,512]{2,0,1:T(8,128)(2,1)} %copy.52), calls=%async_computation | async-start | bytes 524288 | tf_op jit(solution)/shard_map/all_to_all | solution.py:119
  28.6 29.8 %copy-start.5 = (bf16[64,2048]{1,0:T(8,128)(2,1)S(1)}, bf16[64,2048]{1,0:T(8,128)(2,1)}, u32[]{:S(2)}) copy-start(bf16[64,2048]{1,0:T(8,128)(2,1)} %param.26) | copy-start | bytes 786436
  28.6 30.0 %copy-start.18 = (f32[2048]{0:T(1024)S(1)}, f32[2048]{0:T(1024)}, u32[]{:S(2)}) copy-start(f32[2048]{0:T(1024)} %param.27) | copy-start | bytes 24580
  28.6 29.6 %all-to-all-start.1 = ((bf16[4,64,2048]{2,1,0:T(8,128)(2,1)}), bf16[4,64,2048]{2,1,0:T(8,128)(2,1)S(1)}, u32[]{:S(2)}, u32[]{:S(2)}) async-start(bf16[4,64,2048]{2,1,0:T(8,128)(2,1)} %bitcast.6), calls=%async_computation.1 | async-start | bytes 2097152 | tf_op jit(solution)/shard_map/all_to_all | solution.py:134
  62.7 16.5 %copy-start.2 = (bf16[1,352,2048]{2,1,0:T(8,128)(2,1)S(1)}, bf16[1,352,2048]{2,1,0:T(8,128)(2,1)}, u32[]{:S(2)}) copy-start(bf16[1,352,2048]{2,1,0:T(8,128)(2,1)} %param.33) | copy-start | bytes 4325380
  62.7 64.5 %all-to-all-start.2 = ((bf16[64,8,2048]{2,1,0:T(8,128)(2,1)}), bf16[64,8,2048]{2,1,0:T(8,128)(2,1)}, u32[]{:S(2)}, u32[]{:S(2)}) async-start(bf16[64,8,2048]{2,1,0:T(8,128)(2,1)} %bitcast_select_fusion), calls=%async_computation.2 | async-start | bytes 4194304 | tf_op jit(solution)/shard_map/all_to_all | solution.py:161
  77.5 140.7 %all-gather.6.cloned.1.call-start = ((), (), s32[]{:S(2)}) async-start(), calls=%async_computation.6 | async-start | bytes 3604480 | tf_op jit(solution)/shard_map/all_gather | solution.py:128
  77.6 58.5 %collective-permute-start.2 = (bf16[2048,352]{0,1:T(8,128)(2,1)}, bf16[2048,352]{0,1:T(8,128)(2,1)}, u32[]{:S(2)}, u32[]{:S(2)}) collective-permute-start(bf16[2048,352]{0,1:T(8,128)(2,1)} %bitcast.14), channel_id=1, source_target_pairs={{0,2},{1,3},{2,0},{3,1},{4,6},{5,7},{6,4},{7,5},{8,10},{9,11},{10,... | collective-permute-start | bytes 4325384 | tf_op jit(solution)/shard_map/ppermute | solution.py:130
  77.7 72.7 %collective-permute-start = (bf16[2048,352]{0,1:T(8,128)(2,1)}, bf16[2048,352]{0,1:T(8,128)(2,1)}, u32[]{:S(2)}, u32[]{:S(2)}) collective-permute-start(bf16[2048,352]{0,1:T(8,128)(2,1)} %bitcast.14), channel_id=1, source_target_pairs={{0,1},{1,2},{2,3},{3,0},{4,5},{5,6},{6,7},{7,4},{8,9},{9,10},{10,1... | collective-permute-start | bytes 4325384 | tf_op jit(solution)/shard_map/ppermute | solution.py:130
  80.4 93.4 %collective-permute-start.3 = (bf16[352,1024]{1,0:T(8,128)(2,1)}, bf16[352,1024]{1,0:T(8,128)(2,1)}, u32[]{:S(2)}, u32[]{:S(2)}) collective-permute-start(bf16[352,1024]{1,0:T(8,128)(2,1)} %get-tuple-element.27), channel_id=1, source_target_pairs={{0,2},{1,3},{2,0},{3,1},{4,6},{5,7},{6,4},{7,5},{8,10},{9,11},{10,... | collective-permute-start | bytes 2162696 | tf_op jit(solution)/shard_map/ppermute | solution.py:125
  82.8 117.2 %collective-permute-start.1 = (bf16[352,1024]{1,0:T(8,128)(2,1)}, bf16[352,1024]{1,0:T(8,128)(2,1)}, u32[]{:S(2)}, u32[]{:S(2)}) collective-permute-start(bf16[352,1024]{1,0:T(8,128)(2,1)} %get-tuple-element.27), channel_id=1, source_target_pairs={{0,1},{1,2},{2,3},{3,0},{4,5},{5,6},{6,7},{7,4},{8,9},{9,10},{10,1... | collective-permute-start | bytes 2162696 | tf_op jit(solution)/shard_map/ppermute | solution.py:125
  82.8 119.1 %collective-permute-start.4 = (bf16[2048,352]{0,1:T(8,128)(2,1)}, bf16[2048,352]{0,1:T(8,128)(2,1)}, u32[]{:S(2)}, u32[]{:S(2)}) collective-permute-start(bf16[2048,352]{0,1:T(8,128)(2,1)} %bitcast.14), channel_id=1, source_target_pairs={{0,3},{1,0},{2,1},{3,2},{4,7},{5,4},{6,5},{7,6},{8,11},{9,8},{10,9... | collective-permute-start | bytes 4325384 | tf_op jit(solution)/shard_map/ppermute | solution.py:130
  136.0 4.0 %copy-start.7 = (bf16[512,352]{0,1:T(8,128)(2,1)}, bf16[512,352]{0,1:T(8,128)(2,1)S(1)}, u32[]{:S(2)}) copy-start(bf16[512,352]{0,1:T(8,128)(2,1)S(1)} %fusion.37) | copy-start | bytes 1081348
  136.1 4.0 %copy-start.3 = (bf16[1,352,2048]{2,1,0:T(8,128)(2,1)S(1)}, bf16[1,352,2048]{2,1,0:T(8,128)(2,1)}, u32[]{:S(2)}) copy-start(bf16[1,352,2048]{2,1,0:T(8,128)(2,1)} %param.33) | copy-start | bytes 4325380
  136.1 68.8 %collective-permute-start.5 = (bf16[352,1024]{1,0:T(8,128)(2,1)}, bf16[352,1024]{1,0:T(8,128)(2,1)S(1)}, u32[]{:S(2)}, u32[]{:S(2)}) collective-permute-start(bf16[352,1024]{1,0:T(8,128)(2,1)} %get-tuple-element.27), channel_id=1, source_target_pairs={{0,3},{1,0},{2,1},{3,2},{4,7},{5,4},{6,5},{7,6},{8,11},{9,8},{10,9... | collective-permute-start | bytes 2162696 | tf_op jit(solution)/shard_map/ppermute | solution.py:125
  140.0 33.7 %copy-start.9 = (bf16[512,352]{0,1:T(8,128)(2,1)}, bf16[512,352]{0,1:T(8,128)(2,1)S(1)}, u32[]{:S(2)}) copy-start(bf16[512,352]{0,1:T(8,128)(2,1)S(1)} %fusion.31) | copy-start | bytes 1081348
  153.4 48.5 %copy-start.11 = (bf16[512,352]{0,1:T(8,128)(2,1)}, bf16[512,352]{0,1:T(8,128)(2,1)S(1)}, u32[]{:S(2)}) copy-start(bf16[512,352]{0,1:T(8,128)(2,1)S(1)} %fusion.34) | copy-start | bytes 1081348
  206.7 11.6 %copy-start.10 = (bf16[512,352]{0,1:T(8,128)(2,1)S(1)}, bf16[512,352]{0,1:T(8,128)(2,1)}, u32[]{:S(2)}) copy-start(bf16[512,352]{0,1:T(8,128)(2,1)} %copy-done.9) | copy-start | bytes 1081348
  206.7 13.6 %copy-start.8 = (bf16[512,352]{0,1:T(8,128)(2,1)S(1)}, bf16[512,352]{0,1:T(8,128)(2,1)}, u32[]{:S(2)}) copy-start(bf16[512,352]{0,1:T(8,128)(2,1)} %copy-done.7) | copy-start | bytes 1081348
  206.7 39.7 %all-to-all-start.3 = ((bf16[64,8,1024]{2,1,0:T(8,128)(2,1)}), bf16[64,8,1024]{2,1,0:T(8,128)(2,1)S(1)}, u32[]{:S(2)}, u32[]{:S(2)}) async-start(bf16[64,8,1024]{2,1,0:T(8,128)(2,1)} %fusion.55), calls=%async_computation.3 | async-start | bytes 2097152 | tf_op jit(solution)/shard_map/all_to_all | solution.py:174
  218.3 2.0 copy-start.4
  220.3 1.0 copy-start.12
  223.8 28.9 %copy-start.22 = (s32[1,8]{1,0:T(1,128)S(1)}, s32[1,8]{1,0:T(1,128)}, u32[]{:S(2)}) copy-start(s32[1,8]{1,0:T(1,128)} %param.25) | copy-start | bytes 100
  223.8 29.0 %copy-start.15 = (bf16[64,2048]{1,0:T(8,128)(2,1)S(1)}, bf16[64,2048]{1,0:T(8,128)(2,1)}, u32[]{:S(2)}) copy-start(bf16[64,2048]{1,0:T(8,128)(2,1)} %param.19) | copy-start | bytes 786436
  223.8 29.5 %copy-start.17 = (bf16[64,2048]{1,0:T(8,128)(2,1)S(1)}, bf16[64,2048]{1,0:T(8,128)(2,1)}, u32[]{:S(2)}) copy-start(bf16[64,2048]{1,0:T(8,128)(2,1)} %param.18) | copy-start | bytes 786436
  223.8 30.1 %copy-start.20 = (f32[256,4]{0,1:T(4,128)S(1)}, f32[256,4]{0,1:T(4,128)}, u32[]{:S(2)}) copy-start(f32[256,4]{0,1:T(4,128)} %param.30) | copy-start | bytes 12292
  246.4 34.4 %all-to-all-start.4 = ((bf16[64,8,1024]{2,1,0:T(8,128)(2,1)}), bf16[64,8,1024]{2,1,0:T(8,128)(2,1)S(1)}, u32[]{:S(2)}, u32[]{:S(2)}) async-start(bf16[64,8,1024]{2,1,0:T(8,128)(2,1)} %fusion.18), calls=%async_computation.4 | async-start | bytes 2097152 | tf_op jit(solution)/shard_map/all_to_all | solution.py:186
  282.8 6.5 %copy-start.1 = (bf16[512,2048]{1,0:T(8,128)(2,1)S(1)}, bf16[512,2048]{1,0:T(8,128)(2,1)}, u32[]{:S(2)}) copy-start(bf16[512,2048]{1,0:T(8,128)(2,1)} %param.20) | copy-start | bytes 6291460
Sparse Core Ops, SparseCore 0:
  9.8 115.7 all-gather.3
  127.4 77.3 all-gather.5

commit v8 on v5

--- a/solution.py
+++ b/solution.py
@@ -181,10 +181,12 @@
         concat_axis=0,
         tiled=True,
     )
+    route_major = dest.reshape(tok_rows, TOPK).T.reshape(-1)
+    gains_route_major = own_gains.T[:, :, None]
     moe_parts = []
     for returned in (returned_early, returned_late):
-        picked = returned.reshape(-1, half)[dest].reshape(tok_rows, TOPK, half)
-        moe_parts.append(jnp.sum(own_gains[:, :, None] * picked.astype(jnp.float32), axis=1))
+        picked = returned.reshape(-1, half)[route_major].reshape(TOPK, tok_rows, half)
+        moe_parts.append(jnp.sum(gains_route_major * picked.astype(jnp.float32), axis=0))
     moe = jnp.concatenate(moe_parts, axis=1)
     layer_out = (stream + moe).astype(jnp.bfloat16)
     picks = (jnp.arange(requests, dtype=jnp.int32)[:, None] * TREE + accepted_path).reshape(-1)

time: 271 us -> 268 us (0.989)
    convert_element_type x2 -> x0, local copies, waits for them, and re-layouts: 3.65 us -> none  [on_device(): picked.astype(jnp.float32)]
  transfers between devices with their start and end apart: 11 -> 11, of which waited for: 7 -> 7; matrix products, arithmetic and copies ran while one was open for 21% -> 20% of each run, Pallas kernels for 0% -> 0%
where the time goes in v8:
time: 268 us; the launch traced here: 267 us
  waiting for transfers between devices  148 us (55%)
  starting transfers between devices  43.1 us (16%)
  matrix products  35.3 us (13%)
  local copies, waits for them, and re-layouts  17.4 us (6%)
  between operations  15.6 us (6%)
  other arithmetic  7.91 us (3%)
    all_to_all x1, waiting for transfers between devices, on_device(): lax.all_to_all(outgoing, 'expert', split_axis=0, concat_axis=0, tiled=True)  45.5 us
    all_gather x1, waiting for transfers between devices, on_device(): gate_full = lax.all_gather(w_gate[0], 'cuts', axis=0)  26.6 us
    all_to_all x1, waiting for transfers between devices, on_device(): lax.all_to_all(projected.astype(jnp.bfloat16).reshape(lax.axis_size('cuts...  24.1 us
    all_to_all x1, waiting for transfers between devices, on_device(): lax.all_to_all(product_late.astype(jnp.bfloat16).reshape(experts_all, cap...  23.1 us
    all_gather x1, waiting for transfers between devices, on_device(): down_late = lax.all_gather(w_down[0][:, half:], 'cuts', axis=0)  16.1 us
    all_to_all x1, starting transfers between devices, on_device(): lax.all_to_all(outgoing, 'expert', split_axis=0, concat_axis=0, tiled=True)  14.7 us
    all_to_all x1, starting transfers between devices, on_device(): lax.all_to_all(product.astype(jnp.bfloat16).reshape(experts_all, capacity...  10.5 us
    dot_general x1, matrix products, on_device(): jnp.einsum('rd,cdf->rcf', rows, up_full, preferred_element_type=jnp.float32)  8.12 us
  transfers between devices with their start and end apart: 11, of which 7 were waited for; matrix products, arithmetic and copies ran while one was open for 20% of the time, Pallas kernels for 0%

profile of v8, /device:TPU:1, one launch (start us, length us, event | category | flops | bytes accessed | tf_op | source)
XLA Modules:
  0.0 267.3 jit_solution(1390686747732275645)
XLA Ops:
  7.2 0.7 all-gather.7.cloned.1.call-update
  8.0 0.7 all-gather.5.cloned.1.call-update
  9.4 0.2 convolution_minimum_fusion.6
  11.4 0.9 fusion.12
  12.3 0.3 fusion.79
  12.6 0.6 fusion.13
  13.4 0.3 fusion.51
  13.7 0.5 copy-done.15
  14.2 0.9 fusion.22
  15.1 0.2 copy.48
  15.4 0.7 copy.49
  16.2 5.0 %all-to-all-start = ((bf16[64,4,512]{2,0,1:T(8,128)(2,1)}), bf16[64,4,512]{2,0,1:T(8,128)(2,1)S(1)}, u32[]{:S(2)}, u32[]{:S(2)}) async-start(bf16[64,4,512]{2,0,1:T(8,128)(2,1)} %copy.49), calls=%async_computation | async-start | bytes 524288 | tf_op jit(solution)/shard_map/all_to_all | solution.py:119
  21.6 0.6 reduce-window.6
  22.2 0.2 slice_reduce_fusion
  22.7 4.0 %all-to-all-done = bf16[64,4,512]{2,0,1:T(8,128)(2,1)S(1)} async-done(((bf16[64,4,512]{2,0,1:T(8,128)(2,1)}), bf16[64,4,512]{2,0,1:T(8,128)(2,1)S(1)}, u32[]{:S(2)}, u32[]{:S(2)}) %all-to-all-start) | async-done | bytes 262176 | tf_op jit(solution)/shard_map/all_to_all | solution.py:119
  26.7 3.5 %convolution_convert_fusion = bf16[256,2048]{1,0:T(8,128)(2,1)} fusion(bf16[256,512]{1,0:T(8,128)(2,1)S(1)} %bitcast.163, bf16[512,2048]{1,0:T(8,128)(2,1)} %param.28), kind=kOutput, calls=%fused_computation.7 | convolution fusion | flops 537395200 | bytes 3407872 | tf_op jit(solution)/shard_map/dot_general | solution.py:130
  30.2 3.6 %all-to-all-start.1 = ((bf16[4,64,2048]{2,1,0:T(8,128)(2,1)}), bf16[4,64,2048]{2,1,0:T(8,128)(2,1)S(1)}, u32[]{:S(2)}, u32[]{:S(2)}) async-start(bf16[4,64,2048]{2,1,0:T(8,128)(2,1)} %bitcast.158), calls=%async_computation.1 | async-start | bytes 2097152 | tf_op jit(solution)/shard_map/all_to_all | solution.py:131
  34.2 1.4 scatter_custom_fusion
  35.7 24.1 %all-to-all-done.1 = bf16[4,64,2048]{2,1,0:T(8,128)(2,1)S(1)} async-done(((bf16[4,64,2048]{2,1,0:T(8,128)(2,1)}), bf16[4,64,2048]{2,1,0:T(8,128)(2,1)S(1)}, u32[]{:S(2)}, u32[]{:S(2)}) %all-to-all-start.1) | async-done | bytes 1048608 | tf_op jit(solution)/shard_map/all_to_all | solution.py:131
  60.2 0.6 copy-done.1
  60.9 3.3 %gather_fusion = bf16[512,2048]{1,0:T(8,128)(2,1)} fusion(bf16[64,2048]{1,0:T(8,128)(2,1)S(1)} %multiply_convert_fusion.1, s32[1024]{0:T(1024)S(1)} %pad_clamp_fusion.2), kind=kCustom, calls=%fused_computation | custom fusion | bytes 4196352 | tf_op jit(solution)/shard_map/gather | solution.py:155
  64.3 3.1 %bitcast_select_fusion = bf16[64,8,2048]{2,1,0:T(8,128)(2,1)} fusion(bf16[512,2048]{1,0:T(8,128)(2,1)} %gather_fusion, pred[64,8]{1,0:T(8,128)(4,1)S(1)} %broadcast_in_dim.89), kind=kLoop, calls=%fused_computation.19 | loop fusion | flops 1048576 | bytes 4194816 | tf_op jit(solution)/shard_map/jit(_where)/select_n | solution.py:154
  67.4 14.7 %all-to-all-start.2 = ((bf16[64,8,2048]{2,1,0:T(8,128)(2,1)}), bf16[64,8,2048]{2,1,0:T(8,128)(2,1)}, u32[]{:S(2)}, u32[]{:S(2)}) async-start(bf16[64,8,2048]{2,1,0:T(8,128)(2,1)} %bitcast_select_fusion), calls=%async_computation.2 | async-start | bytes 4194304 | tf_op jit(solution)/shard_map/all_to_all | solution.py:158
  82.2 1.2 fusion.78
  83.4 0.3 collective-permute-start
  83.7 1.8 collective-permute-start.1
  85.5 0.6 collective-permute-start.2
  86.2 45.5 %all-to-all-done.2 = bf16[64,8,2048]{2,1,0:T(8,128)(2,1)} async-done(((bf16[64,8,2048]{2,1,0:T(8,128)(2,1)}), bf16[64,8,2048]{2,1,0:T(8,128)(2,1)}, u32[]{:S(2)}, u32[]{:S(2)}) %all-to-all-start.2) | async-done | bytes 2097184 | tf_op jit(solution)/shard_map/all_to_all | solution.py:158
  131.8 8.1 %fusion.6 = f32[512,4,352]{0,2,1:T(8,128)} fusion(bf16[4,2048,352]{1,2,0:T(8,128)(2,1)} %all-gather.7.cloned.1.call-done, bf16[64,8,2048]{2,1,0:T(8,128)(2,1)} %all-to-all-done.2), kind=kOutput, calls=%fused_computation.15 | convolution fusion | flops 2952790016 | bytes 10747904 | tf_op jit(solution)/shard_map/rd,cdf->rcf/dot_general | solution.py:161
  139.9 26.6 %all-gather.5.cloned.1.call-done = bf16[4,2048,352]{1,2,0:T(8,128)(2,1)} async-done(((bf16[1,2048,352]{1,2,0:T(8,128)(2,1)}), bf16[4,2048,352]{1,2,0:T(8,128)(2,1)}) %all-gather.5.cloned.1.call-update) | async-done | bytes 5767184 | tf_op jit(solution)/shard_map/all_gather | solution.py:120
  166.5 7.8 %multiply_convert_fusion = bf16[512,4,352]{0,2,1:T(8,128)(2,1)S(1)} fusion(f32[512,4,352]{0,2,1:T(8,128)} %fusion.6, bf16[4,2048,352]{1,2,0:T(8,128)(2,1)} %all-gather.5.cloned.1.call-done, bf16[64,8,2048]{2,1,0:T(8,128)(2,1)} %all-to-all-done.2), kind=kOutput, calls=%fused_computation.6 | convolution fusion | flops 2957115392 | bytes 12189696 | tf_op jit(solution)/shard_map/rd,cdf->rcf/dot_general | solution.py:160
  174.3 0.7 fusion.45
  175.0 1.8 fusion.43
  176.9 1.8 fusion.41
  178.8 2.9 %fusion.27 = bf16[64,8,1024]{2,1,0:T(8,128)(2,1)} fusion(f32[512,1024]{1,0:T(8,128)S(1)} %fusion.41, f32[512,1024]{1,0:T(8,128)S(1)} %fusion.45, f32[512,1024]{1,0:T(8,128)S(1)} %fusion.43, bf16[352,1024]{1,0:T(8,128)(2,1)} %collective-permute-done.2, bf16[512,4,352]{0,2,1:T(8,128)(2,1)S(1)} %multiply_convert_fusion, s32[]{:T(128)S(6)} %select_n.102), kind=kOutput, calls=%fused_computation.42 | convolution fusion | flops 371195904 | bytes 8421380 | tf_op jit(solution)/shard_map/dot_general | solution.py:167
  181.6 10.5 %all-to-all-start.3 = ((bf16[64,8,1024]{2,1,0:T(8,128)(2,1)}), bf16[64,8,1024]{2,1,0:T(8,128)(2,1)S(1)}, u32[]{:S(2)}, u32[]{:S(2)}) async-start(bf16[64,8,1024]{2,1,0:T(8,128)(2,1)} %fusion.27), calls=%async_computation.3 | async-start | bytes 2097152 | tf_op jit(solution)/shard_map/all_to_all | solution.py:169
  192.1 16.1 %all-gather.9.cloned.1.call-done = bf16[1408,1024]{1,0:T(8,128)(2,1)} async-done(((bf16[352,1024]{1,0:T(8,128)(2,1)}), bf16[1408,1024]{1,0:T(8,128)(2,1)}) %all-gather.9.cloned.1.call-update) | async-done | bytes 2883600 | tf_op jit(solution)/shard_map/all_gather | solution.py:129
  208.2 5.0 %fusion.14 = bf16[64,8,1024]{2,1,0:T(8,128)(2,1)} fusion(bf16[512,4,352]{0,2,1:T(8,128)(2,1)} %copy-done.7, bf16[4,352,1024]{2,1,0:T(8,128)(2,1)} %bitcast.167), kind=kOutput, calls=%fused_computation.27 | convolution fusion | flops 1476919296 | bytes 5373952 | tf_op jit(solution)/shard_map/rcf,cfd->rd/dot_general | solution.py:176
  213.3 7.0 %all-to-all-done.3 = bf16[64,8,1024]{2,1,0:T(8,128)(2,1)S(1)} async-done(((bf16[64,8,1024]{2,1,0:T(8,128)(2,1)}), bf16[64,8,1024]{2,1,0:T(8,128)(2,1)S(1)}, u32[]{:S(2)}, u32[]{:S(2)}) %all-to-all-start.3) | async-done | bytes 1048608 | tf_op jit(solution)/shard_map/all_to_all | solution.py:169
  220.3 6.5 %all-to-all-start.4 = ((bf16[64,8,1024]{2,1,0:T(8,128)(2,1)}), bf16[64,8,1024]{2,1,0:T(8,128)(2,1)}, u32[]{:S(2)}, u32[]{:S(2)}) async-start(bf16[64,8,1024]{2,1,0:T(8,128)(2,1)} %fusion.14), calls=%async_computation.4 | async-start | bytes 2097152 | tf_op jit(solution)/shard_map/all_to_all | solution.py:177
  226.8 0.6 gather_fusion.3
  227.4 1.6 gather_fusion.4
  229.1 0.6 pad_maximum_fusion
  229.7 2.0 gather_fusion.1
  231.7 23.1 %all-to-all-done.4 = bf16[64,8,1024]{2,1,0:T(8,128)(2,1)} async-done(((bf16[64,8,1024]{2,1,0:T(8,128)(2,1)}), bf16[64,8,1024]{2,1,0:T(8,128)(2,1)}, u32[]{:S(2)}, u32[]{:S(2)}) %all-to-all-start.4) | async-done | bytes 1048608 | tf_op jit(solution)/shard_map/all_to_all | solution.py:177
  254.8 3.8 %gather_fusion.2 = bf16[256,1024]{1,0:T(8,128)(2,1)} fusion(bf16[512,1024]{1,0:T(8,128)(2,1)} %bitcast.28, s32[1024]{0:T(1024)S(1)} %pad_clamp_fusion.1), kind=kCustom, calls=%fused_computation.2 | custom fusion | bytes 1049600 | tf_op jit(solution)/shard_map/gather | solution.py:188
  258.6 1.4 fusion.29
  260.0 0.8 fusion.35
  (82 shorter events, 3.1 us)
Async XLA Ops:
  7.2 4.2 %copy-start = (bf16[512,2048]{1,0:T(8,128)(2,1)S(1)}, bf16[512,2048]{1,0:T(8,128)(2,1)}, u32[]{:S(2)}) copy-start(bf16[512,2048]{1,0:T(8,128)(2,1)} %param.20) | copy-start | bytes 6291460
  7.2 2.2 copy-start.16
  7.2 4.2 %copy-start.8 = (bf16[64,2048]{1,0:T(8,128)(2,1)S(1)}, bf16[64,2048]{1,0:T(8,128)(2,1)}, u32[]{:S(2)}) copy-start(bf16[64,2048]{1,0:T(8,128)(2,1)} %param.17) | copy-start | bytes 786436
  7.2 124.6 %all-gather.7.cloned.1.call-start = ((), (), s32[]{:S(2)}) async-start(), calls=%async_computation.6 | async-start | bytes 7208960 | tf_op jit(solution)/shard_map/all_gather | solution.py:121
  7.9 158.5 %all-gather.5.cloned.1.call-start = ((), (), s32[]{:S(2)}) async-start(), calls=%async_computation.5 | async-start | bytes 7208960 | tf_op jit(solution)/shard_map/all_gather | solution.py:120
  11.4 1.0 copy-start.9
  12.3 1.1 copy-start.11
  12.6 1.6 copy-start.15
  15.1 6.1 %copy-start.13 = (s32[256,4]{0,1:T(4,128)S(1)}, s32[256,4]{0,1:T(4,128)}, u32[]{:S(2)}) copy-start(s32[256,4]{0,1:T(4,128)} %param.29) | copy-start | bytes 12292
  16.2 10.5 %all-to-all-start = ((bf16[64,4,512]{2,0,1:T(8,128)(2,1)}), bf16[64,4,512]{2,0,1:T(8,128)(2,1)S(1)}, u32[]{:S(2)}, u32[]{:S(2)}) async-start(bf16[64,4,512]{2,0,1:T(8,128)(2,1)} %copy.49), calls=%async_computation | async-start | bytes 524288 | tf_op jit(solution)/shard_map/all_to_all | solution.py:119
  30.2 29.8 %copy-start.4 = (bf16[64,2048]{1,0:T(8,128)(2,1)S(1)}, bf16[64,2048]{1,0:T(8,128)(2,1)}, u32[]{:S(2)}) copy-start(bf16[64,2048]{1,0:T(8,128)(2,1)} %param.26) | copy-start | bytes 786436
  30.2 30.6 %copy-start.12 = (f32[2048]{0:T(1024)S(1)}, f32[2048]{0:T(1024)}, u32[]{:S(2)}) copy-start(f32[2048]{0:T(1024)} %param.27) | copy-start | bytes 24580
  30.2 29.6 %all-to-all-start.1 = ((bf16[4,64,2048]{2,1,0:T(8,128)(2,1)}), bf16[4,64,2048]{2,1,0:T(8,128)(2,1)S(1)}, u32[]{:S(2)}, u32[]{:S(2)}) async-start(bf16[4,64,2048]{2,1,0:T(8,128)(2,1)} %bitcast.158), calls=%async_computation.1 | async-start | bytes 2097152 | tf_op jit(solution)/shard_map/all_to_all | solution.py:131
  60.0 0.8 copy-start.1
  67.4 14.8 %copy-start.3 = (bf16[1,352,2048]{2,1,0:T(8,128)(2,1)S(1)}, bf16[1,352,2048]{2,1,0:T(8,128)(2,1)}, u32[]{:S(2)}) copy-start(bf16[1,352,2048]{2,1,0:T(8,128)(2,1)} %param.33) | copy-start | bytes 4325380
  67.4 64.4 %all-to-all-start.2 = ((bf16[64,8,2048]{2,1,0:T(8,128)(2,1)}), bf16[64,8,2048]{2,1,0:T(8,128)(2,1)}, u32[]{:S(2)}, u32[]{:S(2)}) async-start(bf16[64,8,2048]{2,1,0:T(8,128)(2,1)} %bitcast_select_fusion), calls=%async_computation.2 | async-start | bytes 4194304 | tf_op jit(solution)/shard_map/all_to_all | solution.py:158
  82.1 126.1 %all-gather.9.cloned.1.call-start = ((), (), s32[]{:S(2)}) async-start(), calls=%async_computation.7 | async-start | bytes 3604480 | tf_op jit(solution)/shard_map/all_gather | solution.py:129
  83.4 91.6 %collective-permute-start = (bf16[352,1024]{1,0:T(8,128)(2,1)}, bf16[352,1024]{1,0:T(8,128)(2,1)}, u32[]{:S(2)}, u32[]{:S(2)}) collective-permute-start(bf16[352,1024]{1,0:T(8,128)(2,1)} %get-tuple-element.25), channel_id=1, source_target_pairs={{0,1},{1,2},{2,3},{3,0},{4,5},{5,6},{6,7},{7,4},{8,9},{9,10},{10,1... | collective-permute-start | bytes 2162696 | tf_op jit(solution)/shard_map/ppermute | solution.py:126
  83.7 93.1 %collective-permute-start.1 = (bf16[352,1024]{1,0:T(8,128)(2,1)}, bf16[352,1024]{1,0:T(8,128)(2,1)}, u32[]{:S(2)}, u32[]{:S(2)}) collective-permute-start(bf16[352,1024]{1,0:T(8,128)(2,1)} %get-tuple-element.25), channel_id=1, source_target_pairs={{0,2},{1,3},{2,0},{3,1},{4,6},{5,7},{6,4},{7,5},{8,10},{9,11},{10,... | collective-permute-start | bytes 2162696 | tf_op jit(solution)/shard_map/ppermute | solution.py:126
  85.5 93.2 %collective-permute-start.2 = (bf16[352,1024]{1,0:T(8,128)(2,1)}, bf16[352,1024]{1,0:T(8,128)(2,1)}, u32[]{:S(2)}, u32[]{:S(2)}) collective-permute-start(bf16[352,1024]{1,0:T(8,128)(2,1)} %get-tuple-element.25), channel_id=1, source_target_pairs={{0,3},{1,0},{2,1},{3,2},{4,7},{5,4},{6,5},{7,6},{8,11},{9,8},{10,9... | collective-permute-start | bytes 2162696 | tf_op jit(solution)/shard_map/ppermute | solution.py:126
  174.3 4.5 %copy-start.7 = (bf16[512,4,352]{0,2,1:T(8,128)(2,1)}, bf16[512,4,352]{0,2,1:T(8,128)(2,1)S(1)}, u32[]{:S(2)}) copy-start(bf16[512,4,352]{0,2,1:T(8,128)(2,1)S(1)} %multiply_convert_fusion) | copy-start | bytes 4325380
  181.6 38.7 %all-to-all-start.3 = ((bf16[64,8,1024]{2,1,0:T(8,128)(2,1)}), bf16[64,8,1024]{2,1,0:T(8,128)(2,1)S(1)}, u32[]{:S(2)}, u32[]{:S(2)}) async-start(bf16[64,8,1024]{2,1,0:T(8,128)(2,1)} %fusion.27), calls=%async_computation.3 | async-start | bytes 2097152 | tf_op jit(solution)/shard_map/all_to_all | solution.py:169
  213.3 13.5 %copy-start.17 = (s32[1,8]{1,0:T(1,128)S(1)}, s32[1,8]{1,0:T(1,128)}, u32[]{:S(2)}) copy-start(s32[1,8]{1,0:T(1,128)} %param.25) | copy-start | bytes 100
  213.3 13.5 %copy-start.10 = (bf16[64,2048]{1,0:T(8,128)(2,1)S(1)}, bf16[64,2048]{1,0:T(8,128)(2,1)}, u32[]{:S(2)}) copy-start(bf16[64,2048]{1,0:T(8,128)(2,1)} %param.18) | copy-start | bytes 786436
  213.3 15.7 %copy-start.14 = (f32[256,4]{0,1:T(4,128)S(1)}, f32[256,4]{0,1:T(4,128)}, u32[]{:S(2)}) copy-start(f32[256,4]{0,1:T(4,128)} %param.30) | copy-start | bytes 12292
  220.3 34.6 %all-to-all-start.4 = ((bf16[64,8,1024]{2,1,0:T(8,128)(2,1)}), bf16[64,8,1024]{2,1,0:T(8,128)(2,1)}, u32[]{:S(2)}, u32[]{:S(2)}) async-start(bf16[64,8,1024]{2,1,0:T(8,128)(2,1)} %fusion.14), calls=%async_computation.4 | async-start | bytes 2097152 | tf_op jit(solution)/shard_map/all_to_all | solution.py:177
  254.8 3.8 %copy-start.6 = (bf16[256,1024]{1,0:T(8,128)(2,1)S(1)}, bf16[256,1024]{1,0:T(8,128)(2,1)}, u32[]{:S(2)}) copy-start(bf16[256,1024]{1,0:T(8,128)(2,1)} %gather_fusion.1) | copy-start | bytes 1572868
  254.8 5.2 %copy-start.2 = (f32[64,2048]{1,0:T(8,128)S(1)}, f32[64,2048]{1,0:T(8,128)}, u32[]{:S(2)}) copy-start(f32[64,2048]{1,0:T(8,128)} %copy-done.1) | copy-start | bytes 1572868
  254.8 5.2 %copy-start.5 = (bf16[64,2048]{1,0:T(8,128)(2,1)S(1)}, bf16[64,2048]{1,0:T(8,128)(2,1)}, u32[]{:S(2)}) copy-start(bf16[64,2048]{1,0:T(8,128)(2,1)} %param.26) | copy-start | bytes 786436
Sparse Core Ops, SparseCore 0:
  9.8 79.0 all-gather.6
  90.8 75.6 all-gather.4
  168.3 39.9 all-gather.8

commit v9 on v8

--- a/solution.py
+++ b/solution.py
@@ -160,12 +160,9 @@
     gate = jnp.einsum("rd,cdf->rcf", rows, gate_full, preferred_element_type=jnp.float32)
     upper = jnp.einsum("rd,cdf->rcf", rows, up_full, preferred_element_type=jnp.float32)
     hidden = (jax.nn.silu(gate) * upper).astype(jnp.bfloat16)
-    product = None
-    for shift, down_part in enumerate(down_parts):
-        owner = (place - shift) % cut_count
-        slice_hidden = lax.dynamic_index_in_dim(hidden, owner, axis=1, keepdims=False)
-        term = jnp.dot(slice_hidden, down_part, preferred_element_type=jnp.float32)
-        product = term if product is None else product + term
+    shift_of = (place - jnp.arange(cut_count, dtype=jnp.int32)) % cut_count
+    down_by_owner = jnp.take(jnp.stack(down_parts), shift_of, axis=0)
+    product = jnp.einsum("rcf,cfd->rd", hidden, down_by_owner, preferred_element_type=jnp.float32)
     returned_early = lax.all_to_all(
         product.astype(jnp.bfloat16).reshape(experts_all, capacity, half),
         "expert",

time: 268 us -> 267 us (level)
  waiting for transfers between devices: 148 us -> 139 us
  local copies, waits for them, and re-layouts: 17.4 us -> 25.2 us
  matrix products: 35.3 us -> 31 us
  other arithmetic: 7.91 us -> 10.9 us
    all_to_all x1, waiting for transfers between devices: 45.5 us -> 0.01 us  [on_device(): lax.all_to_all(outgoing, 'expert', split_axis=0, concat_axis=0, tiled=True)]
    ppermute x3, waiting for transfers between devices: 0.01 us -> 43.5 us  [on_device(): lax.ppermute(down_early, 'cuts', [(i, (i + shift) % cut_count) for i in r...]
    all_gather x1, waiting for transfers between devices: 26.6 us -> 20.8 us  [on_device(): gate_full = lax.all_gather(w_gate[0], 'cuts', axis=0)]
    dot_general x4 -> x1, matrix products: 7.29 us -> 2.85 us  [on_device(): jnp.einsum('rcf,cfd->rd', hidden, down_by_owner, preferred_element_type=j...]
    gather x0 -> x1, local copies, waits for them, and re-layouts: none -> 4.08 us  [on_device(): down_by_owner = jnp.take(jnp.stack(down_parts), shift_of, axis=0)]
    all_gather x1, waiting for transfers between devices: 16.1 us -> 19.6 us  [on_device(): down_late = lax.all_gather(w_down[0][:, half:], 'cuts', axis=0)]
    all_to_all x1, waiting for transfers between devices: 6.99 us -> 3.53 us  [on_device(): lax.all_to_all(product.astype(jnp.bfloat16).reshape(experts_all, capacity...]
    another operation x2 -> x3, other arithmetic: 0.65 us -> 3.6 us  [the longest x1 2.96 us: on_device(): down_by_owner = jnp.take(jnp.stack(down_parts), shift_of, axis=0)]
  transfers between devices with their start and end apart: 11 -> 11, of which waited for: 7 -> 9; matrix products, arithmetic and copies ran while one was open for 20% -> 22% of each run, Pallas kernels for 0% -> 0%
where the time goes in v9:
time: 267 us; the launch traced here: 266 us
  waiting for transfers between devices  139 us (52%)
  starting transfers between devices  44.2 us (17%)
  matrix products  31 us (12%)
  local copies, waits for them, and re-layouts  25.2 us (9%)
  between operations  15.5 us (6%)
  other arithmetic  10.9 us (4%)
    ppermute x3, waiting for transfers between devices, on_device(): lax.ppermute(down_early, 'cuts', [(i, (i + shift) % cut_count) for i in r...  43.5 us
    all_to_all x1, waiting for transfers between devices, on_device(): lax.all_to_all(projected.astype(jnp.bfloat16).reshape(lax.axis_size('cuts...  24.3 us
    all_to_all x1, waiting for transfers between devices, on_device(): lax.all_to_all(product_late.astype(jnp.bfloat16).reshape(experts_all, cap...  22 us
    all_gather x1, waiting for transfers between devices, on_device(): gate_full = lax.all_gather(w_gate[0], 'cuts', axis=0)  20.8 us
    all_gather x1, waiting for transfers between devices, on_device(): down_late = lax.all_gather(w_down[0][:, half:], 'cuts', axis=0)  19.6 us
    all_to_all x1, starting transfers between devices, on_device(): lax.all_to_all(outgoing, 'expert', split_axis=0, concat_axis=0, tiled=True)  14.6 us
    all_to_all x1, starting transfers between devices, on_device(): lax.all_to_all(product.astype(jnp.bfloat16).reshape(experts_all, capacity...  10.5 us
    dot_general x1, matrix products, on_device(): jnp.einsum('rd,cdf->rcf', rows, up_full, preferred_element_type=jnp.float32)  8.08 us
  transfers between devices with their start and end apart: 11, of which 9 were waited for; matrix products, arithmetic and copies ran while one was open for 22% of the time, Pallas kernels for 0%

profile of v9, /device:TPU:1, one launch (start us, length us, event | category | flops | bytes accessed | tf_op | source)
XLA Modules:
  0.0 266.0 jit_solution(7813672045107406670)
XLA Ops:
  7.3 0.7 all-gather.7.cloned.1.call-update
  8.0 0.7 all-gather.5.cloned.1.call-update
  9.4 0.2 convolution_minimum_fusion.6
  11.4 0.3 fusion.72
  11.7 0.9 fusion.15
  12.7 0.6 fusion.18
  13.5 0.3 fusion.45
  13.8 0.5 copy-done.12
  14.3 0.9 fusion.31
  15.6 0.7 copy.49
  16.3 5.0 %all-to-all-start = ((bf16[64,4,512]{2,0,1:T(8,128)(2,1)}), bf16[64,4,512]{2,0,1:T(8,128)(2,1)S(1)}, u32[]{:S(2)}, u32[]{:S(2)}) async-start(bf16[64,4,512]{2,0,1:T(8,128)(2,1)} %copy.49), calls=%async_computation | async-start | bytes 524288 | tf_op jit(solution)/shard_map/all_to_all | solution.py:119
  21.7 0.6 reduce-window.6
  22.8 4.0 %all-to-all-done = bf16[64,4,512]{2,0,1:T(8,128)(2,1)S(1)} async-done(((bf16[64,4,512]{2,0,1:T(8,128)(2,1)}), bf16[64,4,512]{2,0,1:T(8,128)(2,1)S(1)}, u32[]{:S(2)}, u32[]{:S(2)}) %all-to-all-start) | async-done | bytes 262176 | tf_op jit(solution)/shard_map/all_to_all | solution.py:119
  26.9 3.5 %convolution_convert_fusion = bf16[256,2048]{1,0:T(8,128)(2,1)} fusion(bf16[256,512]{1,0:T(8,128)(2,1)S(1)} %bitcast.157, bf16[512,2048]{1,0:T(8,128)(2,1)} %param.28), kind=kOutput, calls=%fused_computation.12 | convolution fusion | flops 537395200 | bytes 3407872 | tf_op jit(solution)/shard_map/dot_general | solution.py:130
  30.3 3.6 %all-to-all-start.1 = ((bf16[4,64,2048]{2,1,0:T(8,128)(2,1)}), bf16[4,64,2048]{2,1,0:T(8,128)(2,1)S(1)}, u32[]{:S(2)}, u32[]{:S(2)}) async-start(bf16[4,64,2048]{2,1,0:T(8,128)(2,1)} %bitcast.153), calls=%async_computation.1 | async-start | bytes 2097152 | tf_op jit(solution)/shard_map/all_to_all | solution.py:131
  34.1 1.4 scatter_custom_fusion
  35.7 24.3 %all-to-all-done.1 = bf16[4,64,2048]{2,1,0:T(8,128)(2,1)S(1)} async-done(((bf16[4,64,2048]{2,1,0:T(8,128)(2,1)}), bf16[4,64,2048]{2,1,0:T(8,128)(2,1)S(1)}, u32[]{:S(2)}, u32[]{:S(2)}) %all-to-all-start.1) | async-done | bytes 1048608 | tf_op jit(solution)/shard_map/all_to_all | solution.py:131
  60.3 0.7 copy-done.1
  61.1 3.3 %gather_fusion = bf16[512,2048]{1,0:T(8,128)(2,1)} fusion(bf16[64,2048]{1,0:T(8,128)(2,1)S(1)} %multiply_convert_fusion.1, s32[1024]{0:T(1024)S(1)} %pad_clamp_fusion.3), kind=kCustom, calls=%fused_computation | custom fusion | bytes 4196352 | tf_op jit(solution)/shard_map/gather | solution.py:155
  64.4 3.1 %bitcast_select_fusion = bf16[64,8,2048]{2,1,0:T(8,128)(2,1)} fusion(bf16[512,2048]{1,0:T(8,128)(2,1)} %gather_fusion, pred[64,8]{1,0:T(8,128)(4,1)S(1)} %broadcast_in_dim.99), kind=kLoop, calls=%fused_computation.25 | loop fusion | flops 1048576 | bytes 4194816 | tf_op jit(solution)/shard_map/jit(_where)/select_n | solution.py:154
  67.6 14.6 %all-to-all-start.2 = ((bf16[64,8,2048]{2,1,0:T(8,128)(2,1)}), bf16[64,8,2048]{2,1,0:T(8,128)(2,1)}, u32[]{:S(2)}, u32[]{:S(2)}) async-start(bf16[64,8,2048]{2,1,0:T(8,128)(2,1)} %bitcast_select_fusion), calls=%async_computation.2 | async-start | bytes 4194304 | tf_op jit(solution)/shard_map/all_to_all | solution.py:158
  82.3 2.7 %fusion.71 = (bf16[352,1024]{1,0:T(8,128)(2,1)}, bf16[1,352,1024]{2,1,0:T(8,128)(2,1)S(1)}, bf16[352,1024]{1,0:T(8,128)(2,1)}) fusion(bf16[352,2048]{1,0:T(8,128)(2,1)} %bitcast.156), kind=kLoop, calls=%fused_computation.129 | loop fusion | bytes 3604480 | tf_op jit(solution)/shard_map/slice | solution.py:129
  85.0 0.3 collective-permute-start
  85.3 1.8 collective-permute-start.1
  87.1 0.6 collective-permute-start.2
  87.8 15.9 %collective-permute-done = bf16[352,1024]{1,0:T(8,128)(2,1)} collective-permute-done((bf16[352,1024]{1,0:T(8,128)(2,1)}, bf16[352,1024]{1,0:T(8,128)(2,1)}, u32[]{:S(2)}, u32[]{:S(2)}) %collective-permute-start) | collective-permute-done | bytes 720928 | tf_op jit(solution)/shard_map/ppermute | solution.py:126
  103.7 25.9 %collective-permute-done.1 = bf16[352,1024]{1,0:T(8,128)(2,1)} collective-permute-done((bf16[352,1024]{1,0:T(8,128)(2,1)}, bf16[352,1024]{1,0:T(8,128)(2,1)}, u32[]{:S(2)}, u32[]{:S(2)}) %collective-permute-start.1) | collective-permute-done | bytes 720928 | tf_op jit(solution)/shard_map/ppermute | solution.py:126
  129.6 1.7 collective-permute-done.2
  131.3 3.0 %pad_maximum_fusion = bf16[4,352,1024]{2,1,0:T(8,128)(2,1)} fusion(bf16[1,352,1024]{2,1,0:T(8,128)(2,1)} %bitcast.19, bf16[1,352,1024]{2,1,0:T(8,128)(2,1)} %bitcast.18, bf16[1,352,1024]{2,1,0:T(8,128)(2,1)} %bitcast.17, bf16[1,352,1024]{2,1,0:T(8,128)(2,1)S(1)} %get-tuple-element.25), kind=kLoop, calls=%fused_computation.7 | loop fusion | flops 4325376 | bytes 5767168 | tf_op jit(solution)/shard_map/stack | solution.py:164
  134.3 4.1 %gather_fusion.1 = bf16[4,352,1024]{2,1,0:T(8,128)(2,1)} fusion(bf16[4,352,1024]{2,1,0:T(8,128)(2,1)} %pad_maximum_fusion, s32[1024]{0:T(1024)S(1)} %pad_clamp_fusion.2), kind=kCustom, calls=%fused_computation.1 | custom fusion | bytes 5767184 | tf_op jit(solution)/shard_map/jit(_take)/gather | solution.py:164
  138.3 8.1 %fusion.9 = f32[512,4,352]{0,2,1:T(8,128)} fusion(bf16[4,2048,352]{1,2,0:T(8,128)(2,1)} %all-gather.7.cloned.1.call-done, bf16[64,8,2048]{2,1,0:T(8,128)(2,1)} %all-to-all-done.2), kind=kOutput, calls=%fused_computation.21 | convolution fusion | flops 2952790016 | bytes 10747904 | tf_op jit(solution)/shard_map/rd,cdf->rcf/dot_general | solution.py:161
  146.4 20.8 %all-gather.5.cloned.1.call-done = bf16[4,2048,352]{1,2,0:T(8,128)(2,1)} async-done(((bf16[1,2048,352]{1,2,0:T(8,128)(2,1)}), bf16[4,2048,352]{1,2,0:T(8,128)(2,1)}) %all-gather.5.cloned.1.call-update) | async-done | bytes 5767184 | tf_op jit(solution)/shard_map/all_gather | solution.py:120
  167.2 7.9 %multiply_convert_fusion = bf16[512,4,352]{0,2,1:T(8,128)(2,1)S(1)} fusion(f32[512,4,352]{0,2,1:T(8,128)} %fusion.9, bf16[4,2048,352]{1,2,0:T(8,128)(2,1)} %all-gather.5.cloned.1.call-done, bf16[64,8,2048]{2,1,0:T(8,128)(2,1)} %all-to-all-done.2), kind=kOutput, calls=%fused_computation.10 | convolution fusion | flops 2957115392 | bytes 12189696 | tf_op jit(solution)/shard_map/rd,cdf->rcf/dot_general | solution.py:160
  175.2 1.1 copy-done.15
  176.3 2.8 %fusion.20 = bf16[64,8,1024]{2,1,0:T(8,128)(2,1)} fusion(bf16[512,4,352]{0,2,1:T(8,128)(2,1)S(1)} %multiply_convert_fusion, bf16[4,352,1024]{2,1,0:T(8,128)(2,1)S(1)} %copy-done.3, pred[4]{0:T(512)(128)(4,1)S(1)} %compare_and_fusion), kind=kOutput, calls=%fused_computation.33 | convolution fusion | flops 1478361088 | bytes 5373956 | tf_op jit(solution)/shard_map/rcf,cfd->rd/dot_general | solution.py:165
  179.1 10.5 %all-to-all-start.3 = ((bf16[64,8,1024]{2,1,0:T(8,128)(2,1)}), bf16[64,8,1024]{2,1,0:T(8,128)(2,1)S(1)}, u32[]{:S(2)}, u32[]{:S(2)}) async-start(bf16[64,8,1024]{2,1,0:T(8,128)(2,1)} %fusion.20), calls=%async_computation.3 | async-start | bytes 2097152 | tf_op jit(solution)/shard_map/all_to_all | solution.py:166
  189.6 19.6 %all-gather.9.cloned.1.call-done = bf16[1408,1024]{1,0:T(8,128)(2,1)} async-done(((bf16[352,1024]{1,0:T(8,128)(2,1)}), bf16[1408,1024]{1,0:T(8,128)(2,1)}) %all-gather.9.cloned.1.call-update) | async-done | bytes 2883600 | tf_op jit(solution)/shard_map/all_gather | solution.py:129
  209.2 5.0 %fusion.23 = bf16[64,8,1024]{2,1,0:T(8,128)(2,1)} fusion(bf16[512,4,352]{0,2,1:T(8,128)(2,1)} %copy-done.15, bf16[4,352,1024]{2,1,0:T(8,128)(2,1)} %bitcast.161), kind=kOutput, calls=%fused_computation.34 | convolution fusion | flops 1476919296 | bytes 5373952 | tf_op jit(solution)/shard_map/rcf,cfd->rd/dot_general | solution.py:173
  214.2 3.5 %all-to-all-done.3 = bf16[64,8,1024]{2,1,0:T(8,128)(2,1)S(1)} async-done(((bf16[64,8,1024]{2,1,0:T(8,128)(2,1)}), bf16[64,8,1024]{2,1,0:T(8,128)(2,1)S(1)}, u32[]{:S(2)}, u32[]{:S(2)}) %all-to-all-start.3) | async-done | bytes 1048608 | tf_op jit(solution)/shard_map/all_to_all | solution.py:166
  217.8 7.6 %all-to-all-start.4 = ((bf16[64,8,1024]{2,1,0:T(8,128)(2,1)}), bf16[64,8,1024]{2,1,0:T(8,128)(2,1)}, u32[]{:S(2)}, u32[]{:S(2)}) async-start(bf16[64,8,1024]{2,1,0:T(8,128)(2,1)} %fusion.23), calls=%async_computation.4 | async-start | bytes 2097152 | tf_op jit(solution)/shard_map/all_to_all | solution.py:174
  225.4 1.6 gather_fusion.4
  227.0 1.6 gather_fusion.5
  228.9 0.6 pad_maximum_fusion.1
  229.5 2.0 gather_fusion.2
  231.5 22.0 %all-to-all-done.4 = bf16[64,8,1024]{2,1,0:T(8,128)(2,1)} async-done(((bf16[64,8,1024]{2,1,0:T(8,128)(2,1)}), bf16[64,8,1024]{2,1,0:T(8,128)(2,1)}, u32[]{:S(2)}, u32[]{:S(2)}) %all-to-all-start.4) | async-done | bytes 1048608 | tf_op jit(solution)/shard_map/all_to_all | solution.py:174
  253.5 3.8 %gather_fusion.3 = bf16[256,1024]{1,0:T(8,128)(2,1)} fusion(bf16[512,1024]{1,0:T(8,128)(2,1)} %bitcast.30, s32[1024]{0:T(1024)S(1)} %pad_clamp_fusion.1), kind=kCustom, calls=%fused_computation.3 | custom fusion | bytes 1049600 | tf_op jit(solution)/shard_map/gather | solution.py:185
  257.3 1.4 fusion.37
  258.7 0.8 fusion.43
  (81 shorter events, 3.7 us)
Async XLA Ops:
  7.2 4.5 %copy-start = (bf16[512,2048]{1,0:T(8,128)(2,1)S(1)}, bf16[512,2048]{1,0:T(8,128)(2,1)}, u32[]{:S(2)}) copy-start(bf16[512,2048]{1,0:T(8,128)(2,1)} %param.20) | copy-start | bytes 6291460
  7.2 2.2 copy-start.13
  7.2 4.2 %copy-start.6 = (bf16[64,2048]{1,0:T(8,128)(2,1)S(1)}, bf16[64,2048]{1,0:T(8,128)(2,1)}, u32[]{:S(2)}) copy-start(bf16[64,2048]{1,0:T(8,128)(2,1)} %param.17) | copy-start | bytes 786436
  7.2 4.2 %copy-start.7 = (bf16[64,2048]{1,0:T(8,128)(2,1)S(1)}, bf16[64,2048]{1,0:T(8,128)(2,1)}, u32[]{:S(2)}) copy-start(bf16[64,2048]{1,0:T(8,128)(2,1)} %param.18) | copy-start | bytes 786436
  7.2 131.1 %all-gather.7.cloned.1.call-start = ((), (), s32[]{:S(2)}) async-start(), calls=%async_computation.6 | async-start | bytes 7208960 | tf_op jit(solution)/shard_map/all_gather | solution.py:121
  7.9 159.2 %all-gather.5.cloned.1.call-start = ((), (), s32[]{:S(2)}) async-start(), calls=%async_computation.5 | async-start | bytes 7208960 | tf_op jit(solution)/shard_map/all_gather | solution.py:120
  12.6 1.0 copy-start.8
  12.7 1.6 copy-start.12
  15.3 6.1 %copy-start.10 = (s32[256,4]{0,1:T(4,128)S(1)}, s32[256,4]{0,1:T(4,128)}, u32[]{:S(2)}) copy-start(s32[256,4]{0,1:T(4,128)} %param.29) | copy-start | bytes 12292
  16.3 10.5 %all-to-all-start = ((bf16[64,4,512]{2,0,1:T(8,128)(2,1)}), bf16[64,4,512]{2,0,1:T(8,128)(2,1)S(1)}, u32[]{:S(2)}, u32[]{:S(2)}) async-start(bf16[64,4,512]{2,0,1:T(8,128)(2,1)} %copy.49), calls=%async_computation | async-start | bytes 524288 | tf_op jit(solution)/shard_map/all_to_all | solution.py:119
  30.3 29.8 %copy-start.4 = (bf16[64,2048]{1,0:T(8,128)(2,1)S(1)}, bf16[64,2048]{1,0:T(8,128)(2,1)}, u32[]{:S(2)}) copy-start(bf16[64,2048]{1,0:T(8,128)(2,1)} %param.26) | copy-start | bytes 786436
  30.3 30.6 %copy-start.9 = (f32[2048]{0:T(1024)S(1)}, f32[2048]{0:T(1024)}, u32[]{:S(2)}) copy-start(f32[2048]{0:T(1024)} %param.27) | copy-start | bytes 24580
  30.3 29.6 %all-to-all-start.1 = ((bf16[4,64,2048]{2,1,0:T(8,128)(2,1)}), bf16[4,64,2048]{2,1,0:T(8,128)(2,1)S(1)}, u32[]{:S(2)}, u32[]{:S(2)}) async-start(bf16[4,64,2048]{2,1,0:T(8,128)(2,1)} %bitcast.153), calls=%async_computation.1 | async-start | bytes 2097152 | tf_op jit(solution)/shard_map/all_to_all | solution.py:131
  60.1 0.9 copy-start.1
  67.6 70.7 %all-to-all-start.2 = ((bf16[64,8,2048]{2,1,0:T(8,128)(2,1)}), bf16[64,8,2048]{2,1,0:T(8,128)(2,1)}, u32[]{:S(2)}, u32[]{:S(2)}) async-start(bf16[64,8,2048]{2,1,0:T(8,128)(2,1)} %bitcast_select_fusion), calls=%async_computation.2 | async-start | bytes 4194304 | tf_op jit(solution)/shard_map/all_to_all | solution.py:158
  82.2 127.0 %all-gather.9.cloned.1.call-start = ((), (), s32[]{:S(2)}) async-start(), calls=%async_computation.7 | async-start | bytes 3604480 | tf_op jit(solution)/shard_map/all_gather | solution.py:129
  85.0 18.7 %collective-permute-start = (bf16[352,1024]{1,0:T(8,128)(2,1)}, bf16[352,1024]{1,0:T(8,128)(2,1)}, u32[]{:S(2)}, u32[]{:S(2)}) collective-permute-start(bf16[352,1024]{1,0:T(8,128)(2,1)} %get-tuple-element.26), channel_id=1, source_target_pairs={{0,1},{1,2},{2,3},{3,0},{4,5},{5,6},{6,7},{7,4},{8,9},{9,10},{10,1... | collective-permute-start | bytes 2162696 | tf_op jit(solution)/shard_map/ppermute | solution.py:126
  85.3 44.3 %collective-permute-start.1 = (bf16[352,1024]{1,0:T(8,128)(2,1)}, bf16[352,1024]{1,0:T(8,128)(2,1)}, u32[]{:S(2)}, u32[]{:S(2)}) collective-permute-start(bf16[352,1024]{1,0:T(8,128)(2,1)} %get-tuple-element.26), channel_id=1, source_target_pairs={{0,2},{1,3},{2,0},{3,1},{4,6},{5,7},{6,4},{7,5},{8,10},{9,11},{10,... | collective-permute-start | bytes 2162696 | tf_op jit(solution)/shard_map/ppermute | solution.py:126
  87.1 44.2 %collective-permute-start.2 = (bf16[352,1024]{1,0:T(8,128)(2,1)}, bf16[352,1024]{1,0:T(8,128)(2,1)}, u32[]{:S(2)}, u32[]{:S(2)}) collective-permute-start(bf16[352,1024]{1,0:T(8,128)(2,1)} %get-tuple-element.26), channel_id=1, source_target_pairs={{0,3},{1,0},{2,1},{3,2},{4,7},{5,4},{6,5},{7,6},{8,11},{9,8},{10,9... | collective-permute-start | bytes 2162696 | tf_op jit(solution)/shard_map/ppermute | solution.py:126
  167.2 9.1 %copy-start.3 = (bf16[4,352,1024]{2,1,0:T(8,128)(2,1)S(1)}, bf16[4,352,1024]{2,1,0:T(8,128)(2,1)}, u32[]{:S(2)}) copy-start(bf16[4,352,1024]{2,1,0:T(8,128)(2,1)} %gather_fusion.1) | copy-start | bytes 8650756
  175.1 1.1 copy-start.15
  179.1 38.6 %all-to-all-start.3 = ((bf16[64,8,1024]{2,1,0:T(8,128)(2,1)}), bf16[64,8,1024]{2,1,0:T(8,128)(2,1)S(1)}, u32[]{:S(2)}, u32[]{:S(2)}) async-start(bf16[64,8,1024]{2,1,0:T(8,128)(2,1)} %fusion.20), calls=%async_computation.3 | async-start | bytes 2097152 | tf_op jit(solution)/shard_map/all_to_all | solution.py:166
  214.2 11.2 %copy-start.14 = (s32[1,8]{1,0:T(1,128)S(1)}, s32[1,8]{1,0:T(1,128)}, u32[]{:S(2)}) copy-start(s32[1,8]{1,0:T(1,128)} %param.25) | copy-start | bytes 100
  214.2 14.6 %copy-start.11 = (f32[256,4]{0,1:T(4,128)S(1)}, f32[256,4]{0,1:T(4,128)}, u32[]{:S(2)}) copy-start(f32[256,4]{0,1:T(4,128)} %param.30) | copy-start | bytes 12292
  217.8 35.7 %all-to-all-start.4 = ((bf16[64,8,1024]{2,1,0:T(8,128)(2,1)}), bf16[64,8,1024]{2,1,0:T(8,128)(2,1)}, u32[]{:S(2)}, u32[]{:S(2)}) async-start(bf16[64,8,1024]{2,1,0:T(8,128)(2,1)} %fusion.23), calls=%async_computation.4 | async-start | bytes 2097152 | tf_op jit(solution)/shard_map/all_to_all | solution.py:174
  253.5 3.8 %copy-start.5 = (bf16[256,1024]{1,0:T(8,128)(2,1)S(1)}, bf16[256,1024]{1,0:T(8,128)(2,1)}, u32[]{:S(2)}) copy-start(bf16[256,1024]{1,0:T(8,128)(2,1)} %gather_fusion.2) | copy-start | bytes 1572868
  253.5 5.2 %copy-start.2 = (f32[64,2048]{1,0:T(8,128)S(1)}, f32[64,2048]{1,0:T(8,128)}, u32[]{:S(2)}) copy-start(f32[64,2048]{1,0:T(8,128)} %copy-done.1) | copy-start | bytes 1572868
Sparse Core Ops, SparseCore 0:
  9.8 78.7 all-gather.6
  90.5 76.6 all-gather.4
  169.0 40.1 all-gather.8

commit v10 on v9

--- a/solution.py
+++ b/solution.py
@@ -178,12 +178,25 @@
         concat_axis=0,
         tiled=True,
     )
-    route_major = dest.reshape(tok_rows, TOPK).T.reshape(-1)
-    gains_route_major = own_gains.T[:, :, None]
+    slot_ids = jnp.arange(experts_all * capacity, dtype=jnp.int32)
+    mixing = jnp.sum(
+        jnp.where(
+            dest.reshape(tok_rows, TOPK)[:, :, None] == slot_ids[None, None, :],
+            own_gains[:, :, None],
+            0.0,
+        ),
+        axis=1,
+    )
     moe_parts = []
     for returned in (returned_early, returned_late):
-        picked = returned.reshape(-1, half)[route_major].reshape(TOPK, tok_rows, half)
-        moe_parts.append(jnp.sum(gains_route_major * picked.astype(jnp.float32), axis=0))
+        moe_parts.append(
+            jnp.dot(
+                mixing,
+                returned.reshape(-1, half).astype(jnp.float32),
+                precision=lax.Precision.HIGHEST,
+                preferred_element_type=jnp.float32,
+            )
+        )
     moe = jnp.concatenate(moe_parts, axis=1)
     layer_out = (stream + moe).astype(jnp.bfloat16)
     picks = (jnp.arange(requests, dtype=jnp.int32)[:, None] * TREE + accepted_path).reshape(-1)

time: 267 us -> 265 us (level)
  local copies, waits for them, and re-layouts: 25.2 us -> 16.7 us
  matrix products: 31 us -> 34.8 us
    gather x2 -> x0, local copies, waits for them, and re-layouts: 5.78 us -> none  [on_device(): returned.reshape(-1, half)[route_major].reshape(TOPK, tok_rows, half)]
    dot_general x0 -> x2, matrix products: none -> 3.77 us  [on_device(): jnp.dot(mixing, returned.reshape(-1, half).astype(jnp.float32), precision...]
    another operation x1 -> x2, local copies, waits for them, and re-layouts: 0.01 us -> 2.75 us  [the longest x1 2.75 us: on_device(): down_by_owner = jnp.take(jnp.stack(down_parts), shift_of, axis=0)]
    slice x2 -> x1, local copies, waits for them, and re-layouts: 2.91 us -> 0.18 us  [the longest x1 2.73 us: on_device(): down_late = lax.all_gather(w_down[0][:, half:], 'cuts', axis=0)]
where the time goes in v10:
time: 265 us; the launch traced here: 264 us
  waiting for transfers between devices  141 us (53%)
  starting transfers between devices  45 us (17%)
  matrix products  34.8 us (13%)
  local copies, waits for them, and re-layouts  16.7 us (6%)
  between operations  15.5 us (6%)
  other arithmetic  11 us (4%)
    ppermute x3, waiting for transfers between devices, on_device(): lax.ppermute(down_early, 'cuts', [(i, (i + shift) % cut_count) for i in r...  45 us
    all_to_all x1, waiting for transfers between devices, on_device(): lax.all_to_all(projected.astype(jnp.bfloat16).reshape(lax.axis_size('cuts...  24.4 us
    all_to_all x1, waiting for transfers between devices, on_device(): lax.all_to_all(product_late.astype(jnp.bfloat16).reshape(experts_all, cap...  24 us
    all_gather x1, waiting for transfers between devices, on_device(): down_late = lax.all_gather(w_down[0][:, half:], 'cuts', axis=0)  19.4 us
    all_gather x1, waiting for transfers between devices, on_device(): gate_full = lax.all_gather(w_gate[0], 'cuts', axis=0)  19.2 us
    all_to_all x1, starting transfers between devices, on_device(): lax.all_to_all(outgoing, 'expert', split_axis=0, concat_axis=0, tiled=True)  14.6 us
    all_to_all x1, starting transfers between devices, on_device(): lax.all_to_all(product.astype(jnp.bfloat16).reshape(experts_all, capacity...  10.7 us
    dot_general x1, matrix products, on_device(): jnp.einsum('rd,cdf->rcf', rows, up_full, preferred_element_type=jnp.float32)  8.14 us
  transfers between devices with their start and end apart: 11, of which 9 were waited for; matrix products, arithmetic and copies ran while one was open for 22% of the time, Pallas kernels for 0%

profile of v10, /device:TPU:1, one launch (start us, length us, event | category | flops | bytes accessed | tf_op | source)
XLA Modules:
  0.0 264.2 jit_solution(10133971809270691257)
XLA Ops:
  7.3 0.7 all-gather.7.cloned.1.call-update
  8.0 0.7 all-gather.5.cloned.1.call-update
  9.4 0.2 convolution_minimum_fusion.6
  11.4 0.3 fusion.74
  11.7 0.9 fusion.15
  12.7 0.6 fusion.18
  13.5 0.3 fusion.47
  13.8 0.5 copy-done.12
  14.3 0.9 fusion.31
  15.6 0.7 copy.64
  16.3 5.0 %all-to-all-start = ((bf16[64,4,512]{2,0,1:T(8,128)(2,1)}), bf16[64,4,512]{2,0,1:T(8,128)(2,1)S(1)}, u32[]{:S(2)}, u32[]{:S(2)}) async-start(bf16[64,4,512]{2,0,1:T(8,128)(2,1)} %copy.64), calls=%async_computation | async-start | bytes 524288 | tf_op jit(solution)/shard_map/all_to_all | solution.py:119
  21.7 0.6 reduce-window.6
  22.3 0.2 slice_reduce_fusion
  22.8 4.0 %all-to-all-done = bf16[64,4,512]{2,0,1:T(8,128)(2,1)S(1)} async-done(((bf16[64,4,512]{2,0,1:T(8,128)(2,1)}), bf16[64,4,512]{2,0,1:T(8,128)(2,1)S(1)}, u32[]{:S(2)}, u32[]{:S(2)}) %all-to-all-start) | async-done | bytes 262176 | tf_op jit(solution)/shard_map/all_to_all | solution.py:119
  26.9 3.5 %convolution_convert_fusion = bf16[256,2048]{1,0:T(8,128)(2,1)} fusion(bf16[256,512]{1,0:T(8,128)(2,1)S(1)} %bitcast.150, bf16[512,2048]{1,0:T(8,128)(2,1)} %param.28), kind=kOutput, calls=%fused_computation.10 | convolution fusion | flops 537395200 | bytes 3407872 | tf_op jit(solution)/shard_map/dot_general | solution.py:130
  30.4 4.4 %all-to-all-start.1 = ((bf16[4,64,2048]{2,1,0:T(8,128)(2,1)}), bf16[4,64,2048]{2,1,0:T(8,128)(2,1)}, u32[]{:S(2)}, u32[]{:S(2)}) async-start(bf16[4,64,2048]{2,1,0:T(8,128)(2,1)} %bitcast.6), calls=%async_computation.1 | async-start | bytes 2097152 | tf_op jit(solution)/shard_map/all_to_all | solution.py:131
  34.9 1.4 scatter_custom_fusion
  36.4 24.4 %all-to-all-done.1 = bf16[4,64,2048]{2,1,0:T(8,128)(2,1)} async-done(((bf16[4,64,2048]{2,1,0:T(8,128)(2,1)}), bf16[4,64,2048]{2,1,0:T(8,128)(2,1)}, u32[]{:S(2)}, u32[]{:S(2)}) %all-to-all-start.1) | async-done | bytes 1048608 | tf_op jit(solution)/shard_map/all_to_all | solution.py:131
  60.8 1.5 convert_reduce_fusion
  62.6 3.3 %gather_fusion = bf16[512,2048]{1,0:T(8,128)(2,1)} fusion(bf16[64,2048]{1,0:T(8,128)(2,1)S(1)} %multiply_convert_fusion.1, s32[1024]{0:T(1024)S(1)} %pad_clamp_fusion.2), kind=kCustom, calls=%fused_computation | custom fusion | bytes 4196352 | tf_op jit(solution)/shard_map/gather | solution.py:155
  65.9 3.2 %bitcast_select_fusion = bf16[64,8,2048]{2,1,0:T(8,128)(2,1)} fusion(bf16[512,2048]{1,0:T(8,128)(2,1)} %gather_fusion, pred[64,8]{1,0:T(8,128)(4,1)S(1)} %broadcast_in_dim.112), kind=kLoop, calls=%fused_computation.23 | loop fusion | flops 1048576 | bytes 4194816 | tf_op jit(solution)/shard_map/jit(_where)/select_n | solution.py:154
  69.1 14.6 %all-to-all-start.2 = ((bf16[64,8,2048]{2,1,0:T(8,128)(2,1)}), bf16[64,8,2048]{2,1,0:T(8,128)(2,1)}, u32[]{:S(2)}, u32[]{:S(2)}) async-start(bf16[64,8,2048]{2,1,0:T(8,128)(2,1)} %bitcast_select_fusion), calls=%async_computation.2 | async-start | bytes 4194304 | tf_op jit(solution)/shard_map/all_to_all | solution.py:158
  83.8 2.7 %slice_bitcast_fusion = (bf16[1,352,1024]{2,1,0:T(8,128)(2,1)S(1)}, bf16[352,1024]{1,0:T(8,128)(2,1)}, bf16[352,1024]{1,0:T(8,128)(2,1)}) fusion(bf16[352,2048]{1,0:T(8,128)(2,1)} %bitcast.149), kind=kLoop, calls=%fused_computation.126 | loop fusion | bytes 3604480 | tf_op jit(solution)/shard_map/stack | solution.py:164
  86.5 0.3 collective-permute-start
  86.8 1.8 collective-permute-start.1
  88.6 0.6 collective-permute-start.2
  89.3 16.5 %collective-permute-done = bf16[352,1024]{1,0:T(8,128)(2,1)} collective-permute-done((bf16[352,1024]{1,0:T(8,128)(2,1)}, bf16[352,1024]{1,0:T(8,128)(2,1)}, u32[]{:S(2)}, u32[]{:S(2)}) %collective-permute-start) | collective-permute-done | bytes 720928 | tf_op jit(solution)/shard_map/ppermute | solution.py:126
  105.8 25.3 %collective-permute-done.1 = bf16[352,1024]{1,0:T(8,128)(2,1)} collective-permute-done((bf16[352,1024]{1,0:T(8,128)(2,1)}, bf16[352,1024]{1,0:T(8,128)(2,1)}, u32[]{:S(2)}, u32[]{:S(2)}) %collective-permute-start.1) | collective-permute-done | bytes 720928 | tf_op jit(solution)/shard_map/ppermute | solution.py:126
  131.1 3.2 %collective-permute-done.2 = bf16[352,1024]{1,0:T(8,128)(2,1)} collective-permute-done((bf16[352,1024]{1,0:T(8,128)(2,1)}, bf16[352,1024]{1,0:T(8,128)(2,1)}, u32[]{:S(2)}, u32[]{:S(2)}) %collective-permute-start.2) | collective-permute-done | bytes 720928 | tf_op jit(solution)/shard_map/ppermute | solution.py:126
  134.3 3.0 %pad_maximum_fusion = bf16[4,352,1024]{2,1,0:T(8,128)(2,1)} fusion(bf16[1,352,1024]{2,1,0:T(8,128)(2,1)} %bitcast.18, bf16[1,352,1024]{2,1,0:T(8,128)(2,1)} %bitcast.17, bf16[1,352,1024]{2,1,0:T(8,128)(2,1)} %bitcast.16, bf16[1,352,1024]{2,1,0:T(8,128)(2,1)S(1)} %get-tuple-element.22), kind=kLoop, calls=%fused_computation.5 | loop fusion | flops 4325376 | bytes 5767168 | tf_op jit(solution)/shard_map/stack | solution.py:164
  137.3 4.1 %gather_fusion.1 = bf16[4,352,1024]{2,1,0:T(8,128)(2,1)} fusion(bf16[4,352,1024]{2,1,0:T(8,128)(2,1)} %pad_maximum_fusion, s32[1024]{0:T(1024)S(1)} %pad_clamp_fusion.1), kind=kCustom, calls=%fused_computation.1 | custom fusion | bytes 5767184 | tf_op jit(solution)/shard_map/jit(_take)/gather | solution.py:164
  141.4 8.1 %fusion.9 = f32[512,4,352]{0,2,1:T(8,128)} fusion(bf16[4,2048,352]{1,2,0:T(8,128)(2,1)} %all-gather.7.cloned.1.call-done, bf16[64,8,2048]{2,1,0:T(8,128)(2,1)} %all-to-all-done.2), kind=kOutput, calls=%fused_computation.19 | convolution fusion | flops 2952790016 | bytes 10747904 | tf_op jit(solution)/shard_map/rd,cdf->rcf/dot_general | solution.py:161
  149.6 19.2 %all-gather.5.cloned.1.call-done = bf16[4,2048,352]{1,2,0:T(8,128)(2,1)} async-done(((bf16[1,2048,352]{1,2,0:T(8,128)(2,1)}), bf16[4,2048,352]{1,2,0:T(8,128)(2,1)}) %all-gather.5.cloned.1.call-update) | async-done | bytes 5767184 | tf_op jit(solution)/shard_map/all_gather | solution.py:120
  168.7 7.9 %multiply_convert_fusion = bf16[512,4,352]{0,2,1:T(8,128)(2,1)S(1)} fusion(f32[512,4,352]{0,2,1:T(8,128)} %fusion.9, bf16[4,2048,352]{1,2,0:T(8,128)(2,1)} %all-gather.5.cloned.1.call-done, bf16[64,8,2048]{2,1,0:T(8,128)(2,1)} %all-to-all-done.2), kind=kOutput, calls=%fused_computation.8 | convolution fusion | flops 2957115392 | bytes 12189696 | tf_op jit(solution)/shard_map/rd,cdf->rcf/dot_general | solution.py:160
  176.7 1.1 copy-done.15
  177.8 2.8 %fusion.20 = bf16[64,8,1024]{2,1,0:T(8,128)(2,1)} fusion(bf16[512,4,352]{0,2,1:T(8,128)(2,1)S(1)} %multiply_convert_fusion, bf16[4,352,1024]{2,1,0:T(8,128)(2,1)S(1)} %copy-done.1, pred[4]{0:T(512)(128)(4,1)S(1)} %compare_and_fusion), kind=kOutput, calls=%fused_computation.31 | convolution fusion | flops 1478361088 | bytes 5373956 | tf_op jit(solution)/shard_map/rcf,cfd->rd/dot_general | solution.py:165
  180.6 10.7 %all-to-all-start.3 = ((bf16[64,8,1024]{2,1,0:T(8,128)(2,1)}), bf16[64,8,1024]{2,1,0:T(8,128)(2,1)}, u32[]{:S(2)}, u32[]{:S(2)}) async-start(bf16[64,8,1024]{2,1,0:T(8,128)(2,1)} %fusion.20), calls=%async_computation.3 | async-start | bytes 2097152 | tf_op jit(solution)/shard_map/all_to_all | solution.py:166
  191.3 19.4 %all-gather.9.cloned.1.call-done = bf16[1408,1024]{1,0:T(8,128)(2,1)} async-done(((bf16[352,1024]{1,0:T(8,128)(2,1)}), bf16[1408,1024]{1,0:T(8,128)(2,1)}) %all-gather.9.cloned.1.call-update) | async-done | bytes 2883600 | tf_op jit(solution)/shard_map/all_gather | solution.py:129
  210.7 5.1 %fusion.23 = bf16[64,8,1024]{2,1,0:T(8,128)(2,1)} fusion(bf16[512,4,352]{0,2,1:T(8,128)(2,1)} %copy-done.15, bf16[4,352,1024]{2,1,0:T(8,128)(2,1)} %bitcast.153), kind=kOutput, calls=%fused_computation.32 | convolution fusion | flops 1476919296 | bytes 5373952 | tf_op jit(solution)/shard_map/rcf,cfd->rd/dot_general | solution.py:173
  215.8 3.6 %all-to-all-done.3 = bf16[64,8,1024]{2,1,0:T(8,128)(2,1)} async-done(((bf16[64,8,1024]{2,1,0:T(8,128)(2,1)}), bf16[64,8,1024]{2,1,0:T(8,128)(2,1)}, u32[]{:S(2)}, u32[]{:S(2)}) %all-to-all-start.3) | async-done | bytes 1048608 | tf_op jit(solution)/shard_map/all_to_all | solution.py:166
  219.3 7.6 %all-to-all-start.4 = ((bf16[64,8,1024]{2,1,0:T(8,128)(2,1)}), bf16[64,8,1024]{2,1,0:T(8,128)(2,1)}, u32[]{:S(2)}, u32[]{:S(2)}) async-start(bf16[64,8,1024]{2,1,0:T(8,128)(2,1)} %fusion.23), calls=%async_computation.4 | async-start | bytes 2097152 | tf_op jit(solution)/shard_map/all_to_all | solution.py:174
  227.0 0.6 gather_fusion.2
  227.6 0.6 gather_fusion.3
  228.5 0.6 pad_maximum_fusion.1
  229.1 1.9 fusion.38
  231.0 24.0 %all-to-all-done.4 = bf16[64,8,1024]{2,1,0:T(8,128)(2,1)} async-done(((bf16[64,8,1024]{2,1,0:T(8,128)(2,1)}), bf16[64,8,1024]{2,1,0:T(8,128)(2,1)}, u32[]{:S(2)}, u32[]{:S(2)}) %all-to-all-start.4) | async-done | bytes 1048608 | tf_op jit(solution)/shard_map/all_to_all | solution.py:174
  255.0 1.9 fusion.36
  256.9 0.8 fusion.45
  (78 shorter events, 3.4 us)
Async XLA Ops:
  7.2 4.5 %copy-start = (bf16[512,2048]{1,0:T(8,128)(2,1)S(1)}, bf16[512,2048]{1,0:T(8,128)(2,1)}, u32[]{:S(2)}) copy-start(bf16[512,2048]{1,0:T(8,128)(2,1)} %param.20) | copy-start | bytes 6291460
  7.2 2.2 copy-start.13
  7.2 4.2 %copy-start.4 = (bf16[64,2048]{1,0:T(8,128)(2,1)S(1)}, bf16[64,2048]{1,0:T(8,128)(2,1)}, u32[]{:S(2)}) copy-start(bf16[64,2048]{1,0:T(8,128)(2,1)} %param.17) | copy-start | bytes 786436
  7.2 4.2 %copy-start.5 = (bf16[64,2048]{1,0:T(8,128)(2,1)S(1)}, bf16[64,2048]{1,0:T(8,128)(2,1)}, u32[]{:S(2)}) copy-start(bf16[64,2048]{1,0:T(8,128)(2,1)} %param.18) | copy-start | bytes 786436
  7.2 134.2 %all-gather.7.cloned.1.call-start = ((), (), s32[]{:S(2)}) async-start(), calls=%async_computation.6 | async-start | bytes 7208960 | tf_op jit(solution)/shard_map/all_gather | solution.py:121
  7.9 160.8 %all-gather.5.cloned.1.call-start = ((), (), s32[]{:S(2)}) async-start(), calls=%async_computation.5 | async-start | bytes 7208960 | tf_op jit(solution)/shard_map/all_gather | solution.py:120
  12.6 1.0 copy-start.7
  12.7 1.6 copy-start.12
  15.3 6.1 %copy-start.10 = (s32[256,4]{0,1:T(4,128)S(1)}, s32[256,4]{0,1:T(4,128)}, u32[]{:S(2)}) copy-start(s32[256,4]{0,1:T(4,128)} %param.29) | copy-start | bytes 12292
  16.3 10.5 %all-to-all-start = ((bf16[64,4,512]{2,0,1:T(8,128)(2,1)}), bf16[64,4,512]{2,0,1:T(8,128)(2,1)S(1)}, u32[]{:S(2)}, u32[]{:S(2)}) async-start(bf16[64,4,512]{2,0,1:T(8,128)(2,1)} %copy.64), calls=%async_computation | async-start | bytes 524288 | tf_op jit(solution)/shard_map/all_to_all | solution.py:119
  30.4 31.9 %copy-start.2 = (bf16[64,2048]{1,0:T(8,128)(2,1)S(1)}, bf16[64,2048]{1,0:T(8,128)(2,1)}, u32[]{:S(2)}) copy-start(bf16[64,2048]{1,0:T(8,128)(2,1)} %param.26) | copy-start | bytes 786436
  30.4 32.1 %copy-start.9 = (f32[2048]{0:T(1024)S(1)}, f32[2048]{0:T(1024)}, u32[]{:S(2)}) copy-start(f32[2048]{0:T(1024)} %param.27) | copy-start | bytes 24580
  30.4 30.4 %all-to-all-start.1 = ((bf16[4,64,2048]{2,1,0:T(8,128)(2,1)}), bf16[4,64,2048]{2,1,0:T(8,128)(2,1)}, u32[]{:S(2)}, u32[]{:S(2)}) async-start(bf16[4,64,2048]{2,1,0:T(8,128)(2,1)} %bitcast.6), calls=%async_computation.1 | async-start | bytes 2097152 | tf_op jit(solution)/shard_map/all_to_all | solution.py:131
  69.1 72.3 %all-to-all-start.2 = ((bf16[64,8,2048]{2,1,0:T(8,128)(2,1)}), bf16[64,8,2048]{2,1,0:T(8,128)(2,1)}, u32[]{:S(2)}, u32[]{:S(2)}) async-start(bf16[64,8,2048]{2,1,0:T(8,128)(2,1)} %bitcast_select_fusion), calls=%async_computation.2 | async-start | bytes 4194304 | tf_op jit(solution)/shard_map/all_to_all | solution.py:158
  83.7 127.0 %all-gather.9.cloned.1.call-start = ((), (), s32[]{:S(2)}) async-start(), calls=%async_computation.7 | async-start | bytes 3604480 | tf_op jit(solution)/shard_map/all_gather | solution.py:129
  86.5 19.3 %collective-permute-start = (bf16[352,1024]{1,0:T(8,128)(2,1)}, bf16[352,1024]{1,0:T(8,128)(2,1)}, u32[]{:S(2)}, u32[]{:S(2)}) collective-permute-start(bf16[352,1024]{1,0:T(8,128)(2,1)} %get-tuple-element.24), channel_id=1, source_target_pairs={{0,1},{1,2},{2,3},{3,0},{4,5},{5,6},{6,7},{7,4},{8,9},{9,10},{10,1... | collective-permute-start | bytes 2162696 | tf_op jit(solution)/shard_map/ppermute | solution.py:126
  86.8 44.3 %collective-permute-start.1 = (bf16[352,1024]{1,0:T(8,128)(2,1)}, bf16[352,1024]{1,0:T(8,128)(2,1)}, u32[]{:S(2)}, u32[]{:S(2)}) collective-permute-start(bf16[352,1024]{1,0:T(8,128)(2,1)} %get-tuple-element.24), channel_id=1, source_target_pairs={{0,2},{1,3},{2,0},{3,1},{4,6},{5,7},{6,4},{7,5},{8,10},{9,11},{10,... | collective-permute-start | bytes 2162696 | tf_op jit(solution)/shard_map/ppermute | solution.py:126
  88.6 45.7 %collective-permute-start.2 = (bf16[352,1024]{1,0:T(8,128)(2,1)}, bf16[352,1024]{1,0:T(8,128)(2,1)}, u32[]{:S(2)}, u32[]{:S(2)}) collective-permute-start(bf16[352,1024]{1,0:T(8,128)(2,1)} %get-tuple-element.24), channel_id=1, source_target_pairs={{0,3},{1,0},{2,1},{3,2},{4,7},{5,4},{6,5},{7,6},{8,11},{9,8},{10,9... | collective-permute-start | bytes 2162696 | tf_op jit(solution)/shard_map/ppermute | solution.py:126
  168.7 9.1 %copy-start.1 = (bf16[4,352,1024]{2,1,0:T(8,128)(2,1)S(1)}, bf16[4,352,1024]{2,1,0:T(8,128)(2,1)}, u32[]{:S(2)}) copy-start(bf16[4,352,1024]{2,1,0:T(8,128)(2,1)} %gather_fusion.1) | copy-start | bytes 8650756
  176.7 1.1 copy-start.15
  180.6 38.7 %all-to-all-start.3 = ((bf16[64,8,1024]{2,1,0:T(8,128)(2,1)}), bf16[64,8,1024]{2,1,0:T(8,128)(2,1)}, u32[]{:S(2)}, u32[]{:S(2)}) async-start(bf16[64,8,1024]{2,1,0:T(8,128)(2,1)} %fusion.20), calls=%async_computation.3 | async-start | bytes 2097152 | tf_op jit(solution)/shard_map/all_to_all | solution.py:166
  215.8 11.2 %copy-start.14 = (s32[1,8]{1,0:T(1,128)S(1)}, s32[1,8]{1,0:T(1,128)}, u32[]{:S(2)}) copy-start(s32[1,8]{1,0:T(1,128)} %param.25) | copy-start | bytes 100
  215.8 11.2 %copy-start.6 = (bf16[64,2048]{1,0:T(8,128)(2,1)S(1)}, bf16[64,2048]{1,0:T(8,128)(2,1)}, u32[]{:S(2)}) copy-start(bf16[64,2048]{1,0:T(8,128)(2,1)} %param.18) | copy-start | bytes 786436
  215.8 11.8 %copy-start.8 = (bf16[64,2048]{1,0:T(8,128)(2,1)S(1)}, bf16[64,2048]{1,0:T(8,128)(2,1)}, u32[]{:S(2)}) copy-start(bf16[64,2048]{1,0:T(8,128)(2,1)} %param.19) | copy-start | bytes 786436
  215.8 12.5 %copy-start.11 = (f32[256,4]{0,1:T(4,128)S(1)}, f32[256,4]{0,1:T(4,128)}, u32[]{:S(2)}) copy-start(f32[256,4]{0,1:T(4,128)} %param.30) | copy-start | bytes 12292
  219.3 35.7 %all-to-all-start.4 = ((bf16[64,8,1024]{2,1,0:T(8,128)(2,1)}), bf16[64,8,1024]{2,1,0:T(8,128)(2,1)}, u32[]{:S(2)}, u32[]{:S(2)}) async-start(bf16[64,8,1024]{2,1,0:T(8,128)(2,1)} %fusion.23), calls=%async_computation.4 | async-start | bytes 2097152 | tf_op jit(solution)/shard_map/all_to_all | solution.py:174
  227.0 30.0 %copy-start.3 = (bf16[64,2048]{1,0:T(8,128)(2,1)S(1)}, bf16[64,2048]{1,0:T(8,128)(2,1)}, u32[]{:S(2)}) copy-start(bf16[64,2048]{1,0:T(8,128)(2,1)} %param.26) | copy-start | bytes 786436
Sparse Core Ops, SparseCore 0:
  9.8 78.7 all-gather.6
  90.5 78.2 all-gather.4
  170.5 40.1 all-gather.8

commit v11 on v10

--- a/solution.py
+++ b/solution.py
@@ -117,8 +117,8 @@
     )
     attended = attended.reshape(tok_rows, width)
     head_group = lax.all_to_all(attended, "cuts", split_axis=1, concat_axis=0, tiled=True)
-    gate_full = lax.all_gather(w_gate[0], "cuts", axis=0)
-    up_full = lax.all_gather(w_up[0], "cuts", axis=0)
+    gate_full = lax.all_gather(w_gate[0], "cuts", axis=1, tiled=True)
+    up_full = lax.all_gather(w_up[0], "cuts", axis=1, tiled=True)
     cut_count = lax.axis_size("cuts")
     half = width // 2
     down_early = w_down[0][:, :half]
@@ -157,9 +157,9 @@
     outgoing = outgoing.reshape(experts_all, capacity, width)
     arrived = lax.all_to_all(outgoing, "expert", split_axis=0, concat_axis=0, tiled=True)
     rows = arrived.reshape(-1, width)
-    gate = jnp.einsum("rd,cdf->rcf", rows, gate_full, preferred_element_type=jnp.float32)
-    upper = jnp.einsum("rd,cdf->rcf", rows, up_full, preferred_element_type=jnp.float32)
-    hidden = (jax.nn.silu(gate) * upper).astype(jnp.bfloat16)
+    gate = jnp.dot(rows, gate_full, preferred_element_type=jnp.float32)
+    upper = jnp.dot(rows, up_full, preferred_element_type=jnp.float32)
+    hidden = (jax.nn.silu(gate) * upper).astype(jnp.bfloat16).reshape(rows.shape[0], cut_count, -1)
     shift_of = (place - jnp.arange(cut_count, dtype=jnp.int32)) % cut_count
     down_by_owner = jnp.take(jnp.stack(down_parts), shift_of, axis=0)
     product = jnp.einsum("rcf,cfd->rd", hidden, down_by_owner, preferred_element_type=jnp.float32)

time: 265 us -> 269 us (1.015)
  matrix products: 34.8 us -> 38.2 us
    all_to_all x1, waiting for transfers between devices: 3.57 us -> 8.16 us  [on_device(): lax.all_to_all(product.astype(jnp.bfloat16).reshape(experts_all, capacity...]
    all_gather x1, waiting for transfers between devices: 19.4 us -> 14.9 us  [on_device(): down_late = lax.all_gather(w_down[0][:, half:], 'cuts', axis=0)]
  transfers between devices with their start and end apart: 11 -> 11, of which waited for: 9 -> 9; matrix products, arithmetic and copies ran while one was open for 22% -> 24% of each run, Pallas kernels for 0% -> 0%
where the time goes in v11:
time: 269 us; the launch traced here: 268 us
  waiting for transfers between devices  141 us (52%)
  starting transfers between devices  43.9 us (16%)
  matrix products  38.2 us (14%)
  local copies, waits for them, and re-layouts  18.2 us (7%)
  between operations  15.5 us (6%)
  other arithmetic  11.1 us (4%)
    ppermute x3, waiting for transfers between devices, on_device(): lax.ppermute(down_early, 'cuts', [(i, (i + shift) % cut_count) for i in r...  45 us
    all_to_all x1, waiting for transfers between devices, on_device(): lax.all_to_all(projected.astype(jnp.bfloat16).reshape(lax.axis_size('cuts...  24.4 us
    all_to_all x1, waiting for transfers between devices, on_device(): lax.all_to_all(product_late.astype(jnp.bfloat16).reshape(experts_all, cap...  24 us
    all_gather x1, waiting for transfers between devices, on_device(): up_full = lax.all_gather(w_up[0], 'cuts', axis=1, tiled=True)  18.9 us
    all_gather x1, waiting for transfers between devices, on_device(): down_late = lax.all_gather(w_down[0][:, half:], 'cuts', axis=0)  14.9 us
    all_to_all x1, starting transfers between devices, on_device(): lax.all_to_all(outgoing, 'expert', split_axis=0, concat_axis=0, tiled=True)  14.6 us
    all_to_all x1, starting transfers between devices, on_device(): lax.all_to_all(product.astype(jnp.bfloat16).reshape(experts_all, capacity...  10.6 us
    dot_general x1, matrix products, on_device(): upper = jnp.dot(rows, up_full, preferred_element_type=jnp.float32)  8.79 us
  transfers between devices with their start and end apart: 11, of which 9 were waited for; matrix products, arithmetic and copies ran while one was open for 24% of the time, Pallas kernels for 0%

profile of v11, /device:TPU:1, one launch (start us, length us, event | category | flops | bytes accessed | tf_op | source)
XLA Modules:
  0.0 267.6 jit_solution(1790138317899952531)
XLA Ops:
  7.3 0.7 all-gather.7.cloned.1.call-update
  8.0 0.7 all-gather.9.cloned.1.call-update
  9.4 0.2 convolution_minimum_fusion.6
  11.4 0.3 fusion.80
  11.7 0.9 fusion.21
  12.7 0.6 fusion.24
  13.5 0.3 fusion.53
  13.8 0.5 copy-done.11
  14.3 0.9 fusion.37
  15.6 0.7 copy.68
  16.3 5.0 %all-to-all-start = ((bf16[64,4,512]{2,0,1:T(8,128)(2,1)}), bf16[64,4,512]{2,0,1:T(8,128)(2,1)S(1)}, u32[]{:S(2)}, u32[]{:S(2)}) async-start(bf16[64,4,512]{2,0,1:T(8,128)(2,1)} %copy.68), calls=%async_computation | async-start | bytes 524288 | tf_op jit(solution)/shard_map/all_to_all | solution.py:119
  21.7 0.6 reduce-window.6
  22.3 0.2 slice_reduce_fusion
  22.8 4.0 %all-to-all-done = bf16[64,4,512]{2,0,1:T(8,128)(2,1)S(1)} async-done(((bf16[64,4,512]{2,0,1:T(8,128)(2,1)}), bf16[64,4,512]{2,0,1:T(8,128)(2,1)S(1)}, u32[]{:S(2)}, u32[]{:S(2)}) %all-to-all-start) | async-done | bytes 262176 | tf_op jit(solution)/shard_map/all_to_all | solution.py:119
  26.9 3.5 %convolution_convert_fusion = bf16[256,2048]{1,0:T(8,128)(2,1)} fusion(bf16[256,512]{1,0:T(8,128)(2,1)S(1)} %bitcast.157, bf16[512,2048]{1,0:T(8,128)(2,1)} %param.28), kind=kOutput, calls=%fused_computation.15 | convolution fusion | flops 537395200 | bytes 3407872 | tf_op jit(solution)/shard_map/dot_general | solution.py:130
  30.4 4.4 %all-to-all-start.1 = ((bf16[4,64,2048]{2,1,0:T(8,128)(2,1)}), bf16[4,64,2048]{2,1,0:T(8,128)(2,1)}, u32[]{:S(2)}, u32[]{:S(2)}) async-start(bf16[4,64,2048]{2,1,0:T(8,128)(2,1)} %bitcast.6), calls=%async_computation.1 | async-start | bytes 2097152 | tf_op jit(solution)/shard_map/all_to_all | solution.py:131
  34.9 1.4 scatter_custom_fusion
  36.4 24.4 %all-to-all-done.1 = bf16[4,64,2048]{2,1,0:T(8,128)(2,1)} async-done(((bf16[4,64,2048]{2,1,0:T(8,128)(2,1)}), bf16[4,64,2048]{2,1,0:T(8,128)(2,1)}, u32[]{:S(2)}, u32[]{:S(2)}) %all-to-all-start.1) | async-done | bytes 1048608 | tf_op jit(solution)/shard_map/all_to_all | solution.py:131
  60.8 1.5 convert_reduce_fusion
  62.6 3.3 %gather_fusion = bf16[512,2048]{1,0:T(8,128)(2,1)} fusion(bf16[64,2048]{1,0:T(8,128)(2,1)S(1)} %multiply_convert_fusion, s32[1024]{0:T(1024)S(1)} %pad_clamp_fusion.2), kind=kCustom, calls=%fused_computation | custom fusion | bytes 4196352 | tf_op jit(solution)/shard_map/gather | solution.py:155
  65.9 3.2 %bitcast_select_fusion = bf16[64,8,2048]{2,1,0:T(8,128)(2,1)} fusion(bf16[512,2048]{1,0:T(8,128)(2,1)} %gather_fusion, pred[64,8]{1,0:T(8,128)(4,1)S(1)} %broadcast_in_dim.112), kind=kLoop, calls=%fused_computation.26 | loop fusion | flops 1048576 | bytes 4194816 | tf_op jit(solution)/shard_map/jit(_where)/select_n | solution.py:154
  69.1 14.6 %all-to-all-start.2 = ((bf16[64,8,2048]{2,1,0:T(8,128)(2,1)}), bf16[64,8,2048]{2,1,0:T(8,128)(2,1)}, u32[]{:S(2)}, u32[]{:S(2)}) async-start(bf16[64,8,2048]{2,1,0:T(8,128)(2,1)} %bitcast_select_fusion), calls=%async_computation.2 | async-start | bytes 4194304 | tf_op jit(solution)/shard_map/all_to_all | solution.py:158
  83.8 2.8 %slice_bitcast_fusion = (bf16[1,352,1024]{2,1,0:T(8,128)(2,1)S(1)}, bf16[352,1024]{1,0:T(8,128)(2,1)}, bf16[352,1024]{1,0:T(8,128)(2,1)}) fusion(bf16[352,2048]{1,0:T(8,128)(2,1)} %bitcast.154), kind=kLoop, calls=%fused_computation.129 | loop fusion | bytes 3604480 | tf_op jit(solution)/shard_map/stack | solution.py:164
  86.5 0.3 collective-permute-start
  86.8 1.8 collective-permute-start.1
  88.6 0.6 collective-permute-start.2
  89.3 16.5 %collective-permute-done = bf16[352,1024]{1,0:T(8,128)(2,1)} collective-permute-done((bf16[352,1024]{1,0:T(8,128)(2,1)}, bf16[352,1024]{1,0:T(8,128)(2,1)}, u32[]{:S(2)}, u32[]{:S(2)}) %collective-permute-start) | collective-permute-done | bytes 720928 | tf_op jit(solution)/shard_map/ppermute | solution.py:126
  105.8 25.3 %collective-permute-done.1 = bf16[352,1024]{1,0:T(8,128)(2,1)} collective-permute-done((bf16[352,1024]{1,0:T(8,128)(2,1)}, bf16[352,1024]{1,0:T(8,128)(2,1)}, u32[]{:S(2)}, u32[]{:S(2)}) %collective-permute-start.1) | collective-permute-done | bytes 720928 | tf_op jit(solution)/shard_map/ppermute | solution.py:126
  131.1 3.2 %collective-permute-done.2 = bf16[352,1024]{1,0:T(8,128)(2,1)} collective-permute-done((bf16[352,1024]{1,0:T(8,128)(2,1)}, bf16[352,1024]{1,0:T(8,128)(2,1)}, u32[]{:S(2)}, u32[]{:S(2)}) %collective-permute-start.2) | collective-permute-done | bytes 720928 | tf_op jit(solution)/shard_map/ppermute | solution.py:126
  134.3 3.0 %pad_maximum_fusion = bf16[4,352,1024]{2,1,0:T(8,128)(2,1)} fusion(bf16[1,352,1024]{2,1,0:T(8,128)(2,1)} %bitcast.19, bf16[1,352,1024]{2,1,0:T(8,128)(2,1)} %bitcast.18, bf16[1,352,1024]{2,1,0:T(8,128)(2,1)} %bitcast.17, bf16[1,352,1024]{2,1,0:T(8,128)(2,1)S(1)} %get-tuple-element.22), kind=kLoop, calls=%fused_computation.11 | loop fusion | flops 4325376 | bytes 5767168 | tf_op jit(solution)/shard_map/stack | solution.py:164
  137.3 4.1 %gather_fusion.1 = bf16[4,352,1024]{2,1,0:T(8,128)(2,1)} fusion(bf16[4,352,1024]{2,1,0:T(8,128)(2,1)} %pad_maximum_fusion, s32[1024]{0:T(1024)S(1)} %pad_clamp_fusion.1), kind=kCustom, calls=%fused_computation.1 | custom fusion | bytes 5767184 | tf_op jit(solution)/shard_map/jit(_take)/gather | solution.py:164
  141.4 8.4 %fusion.2 = f32[512,1408]{1,0:T(8,128)} fusion(bf16[1,2048,1408]{1,2,0:T(8,128)(2,1)} %all-gather.7.cloned.1.call-done, bf16[64,8,2048]{2,1,0:T(8,128)(2,1)} %all-to-all-done.2), kind=kOutput, calls=%fused_computation.7 | convolution fusion | flops 2952790016 | bytes 10747904 | tf_op jit(solution)/shard_map/dot_general | solution.py:160
  149.8 18.9 %all-gather.9.cloned.1.call-done = bf16[1,2048,1408]{1,2,0:T(8,128)(2,1)} async-done(((bf16[1,2048,352]{1,2,0:T(8,128)(2,1)}), bf16[1,2048,1408]{1,2,0:T(8,128)(2,1)}) %all-gather.9.cloned.1.call-update) | async-done | bytes 5767184 | tf_op jit(solution)/shard_map/all_gather | solution.py:121
  168.7 8.8 %fusion.7 = bf16[512,1408]{1,0:T(8,128)(2,1)} fusion(bf16[1,2048,1408]{1,2,0:T(8,128)(2,1)} %all-gather.9.cloned.1.call-done, f32[512,1408]{1,0:T(8,128)} %fusion.2, bf16[64,8,2048]{2,1,0:T(8,128)(2,1)} %all-to-all-done.2), kind=kOutput, calls=%fused_computation.10 | convolution fusion | flops 2957115392 | bytes 12189696 | tf_op jit(solution)/shard_map/dot_general | solution.py:161
  177.5 2.6 copy.72
  180.1 5.1 %fusion.26 = bf16[64,8,1024]{2,1,0:T(8,128)(2,1)} fusion(bf16[512,4,352]{0,2,1:T(8,128)(2,1)} %bitcast.155, bf16[4,352,1024]{2,1,0:T(8,128)(2,1)} %gather_fusion.1, pred[4]{0:T(512)(128)(4,1)S(1)} %compare_and_fusion), kind=kOutput, calls=%fused_computation.34 | convolution fusion | flops 1478361088 | bytes 5373956 | tf_op jit(solution)/shard_map/rcf,cfd->rd/dot_general | solution.py:165
  185.2 10.6 %all-to-all-start.3 = ((bf16[64,8,1024]{2,1,0:T(8,128)(2,1)}), bf16[64,8,1024]{2,1,0:T(8,128)(2,1)}, u32[]{:S(2)}, u32[]{:S(2)}) async-start(bf16[64,8,1024]{2,1,0:T(8,128)(2,1)} %fusion.26), calls=%async_computation.3 | async-start | bytes 2097152 | tf_op jit(solution)/shard_map/all_to_all | solution.py:166
  195.8 14.9 %all-gather.11.cloned.1.call-done = bf16[1408,1024]{1,0:T(8,128)(2,1)} async-done(((bf16[352,1024]{1,0:T(8,128)(2,1)}), bf16[1408,1024]{1,0:T(8,128)(2,1)}) %all-gather.11.cloned.1.call-update) | async-done | bytes 2883600 | tf_op jit(solution)/shard_map/all_gather | solution.py:129
  210.7 5.0 %fusion.29 = bf16[64,8,1024]{2,1,0:T(8,128)(2,1)} fusion(bf16[512,4,352]{0,2,1:T(8,128)(2,1)} %bitcast.156, bf16[4,352,1024]{2,1,0:T(8,128)(2,1)} %bitcast.160), kind=kOutput, calls=%fused_computation.35 | convolution fusion | flops 1476919296 | bytes 5373952 | tf_op jit(solution)/shard_map/rcf,cfd->rd/dot_general | solution.py:173
  215.7 8.2 %all-to-all-done.3 = bf16[64,8,1024]{2,1,0:T(8,128)(2,1)} async-done(((bf16[64,8,1024]{2,1,0:T(8,128)(2,1)}), bf16[64,8,1024]{2,1,0:T(8,128)(2,1)}, u32[]{:S(2)}, u32[]{:S(2)}) %all-to-all-start.3) | async-done | bytes 1048608 | tf_op jit(solution)/shard_map/all_to_all | solution.py:166
  223.9 6.5 %all-to-all-start.4 = ((bf16[64,8,1024]{2,1,0:T(8,128)(2,1)}), bf16[64,8,1024]{2,1,0:T(8,128)(2,1)}, u32[]{:S(2)}, u32[]{:S(2)}) async-start(bf16[64,8,1024]{2,1,0:T(8,128)(2,1)} %fusion.29), calls=%async_computation.4 | async-start | bytes 2097152 | tf_op jit(solution)/shard_map/all_to_all | solution.py:174
  230.4 0.6 gather_fusion.2
  231.0 0.6 gather_fusion.3
  231.9 0.6 pad_maximum_fusion.1
  232.5 1.9 fusion.44
  234.4 24.0 %all-to-all-done.4 = bf16[64,8,1024]{2,1,0:T(8,128)(2,1)} async-done(((bf16[64,8,1024]{2,1,0:T(8,128)(2,1)}), bf16[64,8,1024]{2,1,0:T(8,128)(2,1)}, u32[]{:S(2)}, u32[]{:S(2)}) %all-to-all-start.4) | async-done | bytes 1048608 | tf_op jit(solution)/shard_map/all_to_all | solution.py:174
  258.4 1.9 fusion.42
  260.3 0.8 fusion.51
  (75 shorter events, 3.4 us)
Async XLA Ops:
  7.2 4.5 %copy-start = (bf16[512,2048]{1,0:T(8,128)(2,1)S(1)}, bf16[512,2048]{1,0:T(8,128)(2,1)}, u32[]{:S(2)}) copy-start(bf16[512,2048]{1,0:T(8,128)(2,1)} %param.20) | copy-start | bytes 6291460
  7.2 2.2 copy-start.12
  7.2 4.2 %copy-start.3 = (bf16[64,2048]{1,0:T(8,128)(2,1)S(1)}, bf16[64,2048]{1,0:T(8,128)(2,1)}, u32[]{:S(2)}) copy-start(bf16[64,2048]{1,0:T(8,128)(2,1)} %param.17) | copy-start | bytes 786436
  7.2 4.2 %copy-start.4 = (bf16[64,2048]{1,0:T(8,128)(2,1)S(1)}, bf16[64,2048]{1,0:T(8,128)(2,1)}, u32[]{:S(2)}) copy-start(bf16[64,2048]{1,0:T(8,128)(2,1)} %param.18) | copy-start | bytes 786436
  7.2 134.2 %all-gather.7.cloned.1.call-start = ((), (), s32[]{:S(2)}) async-start(), calls=%async_computation.5 | async-start | bytes 7208960 | tf_op jit(solution)/shard_map/all_gather | solution.py:120
  7.9 160.8 %all-gather.9.cloned.1.call-start = ((), (), s32[]{:S(2)}) async-start(), calls=%async_computation.6 | async-start | bytes 7208960 | tf_op jit(solution)/shard_map/all_gather | solution.py:121
  12.6 1.0 copy-start.6
  12.7 1.6 copy-start.11
  15.3 6.1 %copy-start.9 = (s32[256,4]{0,1:T(4,128)S(1)}, s32[256,4]{0,1:T(4,128)}, u32[]{:S(2)}) copy-start(s32[256,4]{0,1:T(4,128)} %param.29) | copy-start | bytes 12292
  16.3 10.5 %all-to-all-start = ((bf16[64,4,512]{2,0,1:T(8,128)(2,1)}), bf16[64,4,512]{2,0,1:T(8,128)(2,1)S(1)}, u32[]{:S(2)}, u32[]{:S(2)}) async-start(bf16[64,4,512]{2,0,1:T(8,128)(2,1)} %copy.68), calls=%async_computation | async-start | bytes 524288 | tf_op jit(solution)/shard_map/all_to_all | solution.py:119
  30.4 31.9 %copy-start.1 = (bf16[64,2048]{1,0:T(8,128)(2,1)S(1)}, bf16[64,2048]{1,0:T(8,128)(2,1)}, u32[]{:S(2)}) copy-start(bf16[64,2048]{1,0:T(8,128)(2,1)} %param.26) | copy-start | bytes 786436
  30.4 32.1 %copy-start.8 = (f32[2048]{0:T(1024)S(1)}, f32[2048]{0:T(1024)}, u32[]{:S(2)}) copy-start(f32[2048]{0:T(1024)} %param.27) | copy-start | bytes 24580
  30.4 30.4 %all-to-all-start.1 = ((bf16[4,64,2048]{2,1,0:T(8,128)(2,1)}), bf16[4,64,2048]{2,1,0:T(8,128)(2,1)}, u32[]{:S(2)}, u32[]{:S(2)}) async-start(bf16[4,64,2048]{2,1,0:T(8,128)(2,1)} %bitcast.6), calls=%async_computation.1 | async-start | bytes 2097152 | tf_op jit(solution)/shard_map/all_to_all | solution.py:131
  69.1 72.3 %all-to-all-start.2 = ((bf16[64,8,2048]{2,1,0:T(8,128)(2,1)}), bf16[64,8,2048]{2,1,0:T(8,128)(2,1)}, u32[]{:S(2)}, u32[]{:S(2)}) async-start(bf16[64,8,2048]{2,1,0:T(8,128)(2,1)} %bitcast_select_fusion), calls=%async_computation.2 | async-start | bytes 4194304 | tf_op jit(solution)/shard_map/all_to_all | solution.py:158
  83.7 127.0 %all-gather.11.cloned.1.call-start = ((), (), s32[]{:S(2)}) async-start(), calls=%async_computation.7 | async-start | bytes 3604480 | tf_op jit(solution)/shard_map/all_gather | solution.py:129
  86.5 19.3 %collective-permute-start = (bf16[352,1024]{1,0:T(8,128)(2,1)}, bf16[352,1024]{1,0:T(8,128)(2,1)}, u32[]{:S(2)}, u32[]{:S(2)}) collective-permute-start(bf16[352,1024]{1,0:T(8,128)(2,1)} %get-tuple-element.24), channel_id=1, source_target_pairs={{0,1},{1,2},{2,3},{3,0},{4,5},{5,6},{6,7},{7,4},{8,9},{9,10},{10,1... | collective-permute-start | bytes 2162696 | tf_op jit(solution)/shard_map/ppermute | solution.py:126
  86.8 44.3 %collective-permute-start.1 = (bf16[352,1024]{1,0:T(8,128)(2,1)}, bf16[352,1024]{1,0:T(8,128)(2,1)}, u32[]{:S(2)}, u32[]{:S(2)}) collective-permute-start(bf16[352,1024]{1,0:T(8,128)(2,1)} %get-tuple-element.24), channel_id=1, source_target_pairs={{0,2},{1,3},{2,0},{3,1},{4,6},{5,7},{6,4},{7,5},{8,10},{9,11},{10,... | collective-permute-start | bytes 2162696 | tf_op jit(solution)/shard_map/ppermute | solution.py:126
  88.6 45.7 %collective-permute-start.2 = (bf16[352,1024]{1,0:T(8,128)(2,1)}, bf16[352,1024]{1,0:T(8,128)(2,1)}, u32[]{:S(2)}, u32[]{:S(2)}) collective-permute-start(bf16[352,1024]{1,0:T(8,128)(2,1)} %get-tuple-element.24), channel_id=1, source_target_pairs={{0,3},{1,0},{2,1},{3,2},{4,7},{5,4},{6,5},{7,6},{8,11},{9,8},{10,9... | collective-permute-start | bytes 2162696 | tf_op jit(solution)/shard_map/ppermute | solution.py:126
  185.2 38.7 %all-to-all-start.3 = ((bf16[64,8,1024]{2,1,0:T(8,128)(2,1)}), bf16[64,8,1024]{2,1,0:T(8,128)(2,1)}, u32[]{:S(2)}, u32[]{:S(2)}) async-start(bf16[64,8,1024]{2,1,0:T(8,128)(2,1)} %fusion.26), calls=%async_computation.3 | async-start | bytes 2097152 | tf_op jit(solution)/shard_map/all_to_all | solution.py:166
  215.7 14.6 %copy-start.13 = (s32[1,8]{1,0:T(1,128)S(1)}, s32[1,8]{1,0:T(1,128)}, u32[]{:S(2)}) copy-start(s32[1,8]{1,0:T(1,128)} %param.25) | copy-start | bytes 100
  215.7 14.7 %copy-start.5 = (bf16[64,2048]{1,0:T(8,128)(2,1)S(1)}, bf16[64,2048]{1,0:T(8,128)(2,1)}, u32[]{:S(2)}) copy-start(bf16[64,2048]{1,0:T(8,128)(2,1)} %param.18) | copy-start | bytes 786436
  215.7 15.3 %copy-start.7 = (bf16[64,2048]{1,0:T(8,128)(2,1)S(1)}, bf16[64,2048]{1,0:T(8,128)(2,1)}, u32[]{:S(2)}) copy-start(bf16[64,2048]{1,0:T(8,128)(2,1)} %param.19) | copy-start | bytes 786436
  215.7 15.9 %copy-start.10 = (f32[256,4]{0,1:T(4,128)S(1)}, f32[256,4]{0,1:T(4,128)}, u32[]{:S(2)}) copy-start(f32[256,4]{0,1:T(4,128)} %param.30) | copy-start | bytes 12292
  223.9 34.6 %all-to-all-start.4 = ((bf16[64,8,1024]{2,1,0:T(8,128)(2,1)}), bf16[64,8,1024]{2,1,0:T(8,128)(2,1)}, u32[]{:S(2)}, u32[]{:S(2)}) async-start(bf16[64,8,1024]{2,1,0:T(8,128)(2,1)} %fusion.29), calls=%async_computation.4 | async-start | bytes 2097152 | tf_op jit(solution)/shard_map/all_to_all | solution.py:174
  230.4 30.0 %copy-start.2 = (bf16[64,2048]{1,0:T(8,128)(2,1)S(1)}, bf16[64,2048]{1,0:T(8,128)(2,1)}, u32[]{:S(2)}) copy-start(bf16[64,2048]{1,0:T(8,128)(2,1)} %param.26) | copy-start | bytes 786436
Sparse Core Ops, SparseCore 0:
  9.8 78.7 all-gather.6
  90.5 78.1 all-gather.8
  170.5 40.1 all-gather.10
